TPU v7x, 128 devices: a whole 4x4x4 slice. The times are simulated.
128 devices in a mesh: tile: 32 (over x_lo, y, z), src: 4 (over x_hi, core).
Axes of the slice: x: 4 (x_hi: 2, x_lo: 2; x = x_hi * 2 + x_lo), y: 4, z: 4, core: 2. Of those that a mesh axis runs over, the one named last changes fastest.
Arguments:
- tile_tokens: bfloat16 [32768, 2048], P(('tile', 'src')), may hold values from -6 to 6
- norm_gain: float32 [2048], replicated, may hold values from 0.25 to 2.5
- up_weight: bfloat16 [2048, 2816], P('tile'), may hold values from -0.125 to 0.125
- down_weight: bfloat16 [2816, 2048], P('tile'), may hold values from -0.109375 to 0.109375
- head_weight: bfloat16 [2048, 768], P(None, 'src'), may hold values from -0.125 to 0.125
- source_index: int32 [128, 2], replicated, may hold values from 0 to 96, as said below
- source_cutoff: int32 [128], replicated, may hold values from 8 to 16
- source_weight: float32 [128], replicated, may hold values from 0.3 to 3
Outputs:
- intensity: float32 [128, 4096], P(('tile', 'src'))
Inputs may be any that keep to these rules, and one draw needn't show every extreme that they name: `source_index`: in each aligned group of 4 source points the first has the least value of the group in both coordinates, the second lies exactly 32 beyond it in both, and every other lies within 32 of the first in both.
All inputs are finite; a program needn't handle non-finite values.
Results may differ from a plain program's by a relative error of at most 0.0007.
Values may be sent and summed in bfloat16 or wider, within the bound.
No kernel may reach another device: no remote copies, remote signals or barrier semaphores. Data moves between devices by JAX's collectives and lax.ppermute only.
A program may use at most 128 MiB of HBM per device.

v0:
```python
import math

import jax
import jax.numpy as jnp
from jax import lax
from jax.sharding import PartitionSpec as P

GRID = 16
SUB = 8
W = 32
REG = 64
PIX = 64
SRC_DEV = 4
PATCH = 256
ORD = 128
f32 = jnp.float32
bf16 = jnp.bfloat16


def split_bf16(x):
    hi = lax.reduce_precision(x, exponent_bits=8, mantissa_bits=7)
    lo = x - hi
    return hi.astype(bf16), lo.astype(bf16)


def phase_tables():
    turn = 2.0 * math.pi / PIX
    v = jnp.arange(ORD, dtype=jnp.int32)
    y = jnp.arange(PIX, dtype=jnp.int32)
    ang = jnp.mod(v[:, None] * y[None, :], PIX).astype(f32) * turn
    cv, sv = jnp.cos(ang), jnp.sin(ang)
    t1 = jnp.stack([jnp.concatenate([cv, sv], 1), jnp.concatenate([-sv, cv], 1)], 0)
    i = jnp.arange(W, dtype=jnp.int32)
    x = jnp.arange(PIX, dtype=jnp.int32)
    ang2 = jnp.mod(x[:, None] * i[None, :], PIX).astype(f32) * turn
    ca, sa = jnp.cos(ang2), jnp.sin(ang2)
    t2 = jnp.stack([jnp.stack([ca, -sa], 1), jnp.stack([sa, ca], 1)], 0)
    return t1, t2


def imaging(spec, source_index, source_cutoff, source_weight):
    T = spec.shape[0]
    S = source_index.shape[0]
    x0 = jnp.clip(source_index[:, 0], 0, ORD - W)
    y0 = jnp.clip(source_index[:, 1], 0, ORD - W)
    rows = x0[:, None] + jnp.arange(W, dtype=jnp.int32)[None, :]
    pick = (rows[:, :, None] == jnp.arange(ORD, dtype=jnp.int32)[None, None, :]).astype(bf16)
    spec_rows = spec.reshape(T, 6, 2, ORD, ORD)
    strips = jnp.einsum("siu,tkpuv->sitkpv", pick, spec_rows, preferred_element_type=f32).astype(bf16)
    i = jnp.arange(W, dtype=jnp.int32)
    j = jnp.arange(ORD, dtype=jnp.int32)[None, :] - y0[:, None]
    dist = (i[None, :, None] - W // 2) ** 2 + (j[:, None, :] - W // 2) ** 2
    keep = (dist <= (source_cutoff * source_cutoff)[:, None, None]) & (j[:, None, :] >= 0) & (j[:, None, :] < W)
    masked = jnp.where(keep[:, :, None, None, None, :], strips, jnp.zeros((), bf16))
    t1, t2 = phase_tables()
    t1h, t1l = split_bf16(t1)
    t1s = jnp.concatenate([t1h, t1l], -1)
    out1 = jnp.einsum("sitkpv,pvn->sitkn", masked, t1s, preferred_element_type=f32)
    half = out1[..., : 2 * PIX] + out1[..., 2 * PIX:]
    half = half.reshape(S, W, T, 6, 2, PIX)
    hh, hl = split_bf16(half)
    hcat = jnp.concatenate([hh, hl, hh], 4)
    t2h, t2l = split_bf16(t2)
    t2cat = jnp.concatenate([t2h, t2h, t2l], 2)
    field = jnp.einsum("cxqi,sitkqy->tskcxy", t2cat, hcat, preferred_element_type=f32)
    power = jnp.sum(field * field * source_weight[None, :, None, None, None, None], axis=(1, 2, 3))
    return power.reshape(T, PIX * PIX) * (1.0 / (6.0 * W * W * S))


def local(
    tile_tokens,
    norm_gain,
    up_weight,
    down_weight,
    head_weight,
    source_index,
    source_cutoff,
    source_weight,
):
    token_count, d_model = tile_tokens.shape
    n_tile = lax.axis_size("tile")
    n_src = lax.axis_size("src")
    me = lax.axis_index("src")
    half = me % 2
    up_rows, ff = up_weight.shape
    down_rows = down_weight.shape[0]
    up_half, down_half = up_rows // 2, down_rows // 2
    depth = max(up_half, down_half)
    width = max(ff, d_model)
    up_part = lax.dynamic_slice_in_dim(up_weight, half * up_half, up_half, 0)
    down_part = lax.dynamic_slice_in_dim(down_weight, half * down_half, down_half, 0)
    packed = jnp.stack(
        [
            jnp.pad(up_part, ((0, depth - up_half), (0, width - ff))),
            jnp.pad(down_part, ((0, depth - down_half), (0, width - d_model))),
        ],
        0,
    )
    gathered = lax.all_gather(packed, "tile", axis=1, tiled=False)
    sibling = lax.ppermute(gathered, "src", [(s, s ^ 1) for s in range(n_src)])
    head_parts = [head_weight] + [
        lax.ppermute(head_weight, "src", [(s, s ^ k) for s in range(n_src)]) for k in range(1, n_src)
    ]

    residual = tile_tokens.astype(jnp.float32)
    mean_square = jnp.mean(residual * residual, axis=1, keepdims=True)
    normed = (residual * lax.rsqrt(mean_square + 1e-05) * norm_gain).astype(jnp.bfloat16)

    def halves(x, rows):
        view = x.reshape(x.shape[0], n_tile, 2, rows // 2)
        pad = ((0, 0), (0, 0), (0, depth - rows // 2))
        mine = jnp.pad(lax.dynamic_index_in_dim(view, half, 2, keepdims=False), pad)
        other = jnp.pad(lax.dynamic_index_in_dim(view, 1 - half, 2, keepdims=False), pad)
        return mine.reshape(x.shape[0], -1), other.reshape(x.shape[0], -1)

    def weights(g):
        return g[0].reshape(n_tile * depth, width), g[1].reshape(n_tile * depth, width)

    up_mine, down_mine = weights(gathered)
    up_other, down_other = weights(sibling)
    normed_mine, normed_other = halves(normed, up_rows)
    pre_act = jnp.dot(normed_mine, up_mine, preferred_element_type=jnp.float32) + jnp.dot(
        normed_other, up_other, preferred_element_type=jnp.float32
    )
    hidden = jax.nn.gelu(pre_act[:, :ff]).astype(jnp.bfloat16)
    hidden_mine, hidden_other = halves(hidden, down_rows)
    branch_out = jnp.dot(hidden_mine, down_mine, preferred_element_type=jnp.float32) + jnp.dot(
        hidden_other, down_other, preferred_element_type=jnp.float32
    )
    branch_out = branch_out[:, :d_model]
    mixed = (residual + branch_out).astype(jnp.bfloat16)
    parts = jnp.stack(head_parts, 0)
    coeff_parts = jnp.einsum("tk,pkc->ptc", mixed, parts, preferred_element_type=jnp.float32).astype(
        jnp.bfloat16
    )
    order = me ^ jnp.arange(n_src, dtype=jnp.int32)
    coeffs = jnp.take(coeff_parts, order, axis=0).transpose(1, 0, 2).reshape(token_count, -1)
    tile_count = token_count // PATCH
    spectra = (
        coeffs.reshape(tile_count, GRID, GRID, 12, SUB, SUB)
        .transpose(0, 3, 1, 4, 2, 5)
        .reshape(tile_count, 12, ORD, ORD)
    )
    return imaging(spectra, source_index, source_cutoff, source_weight)


def solution(mesh):
    return jax.shard_map(
        local,
        mesh=mesh,
        in_specs=(
            P(("tile", "src"), None),
            P(),
            P("tile", None),
            P("tile", None),
            P(None, "src"),
            P(),
            P(),
            P(),
        ),
        out_specs=P(("tile", "src"), None),
        check_vma=False,
    )
```

profile of v0, /device:TPU:0, one launch (start us, length us, event | category | flops | bytes accessed | tf_op | source)
XLA Modules:
  0.0 460.4 jit_solution(6744710418892648294)
XLA Ops:
  6.5 1.0 copy-done
  7.6 0.9 constant_dynamic-slice_fusion.3
  8.6 1.2 copy.26
  9.8 190.6 %all-gather.3.cloned.1.call-done = bf16[2,1408,2816]{2,0,1:T(2,128)(2,1)} async-done(((bf16[2,44,2816]{2,0,1:T(2,128)(2,1)}), bf16[2,1408,2816]{2,0,1:T(2,128)(2,1)}) %all-gather.3.cloned.1.call-update) | async-done | bytes 15859728 | tf_op jit(solution)/shard_map/all_gather | solution.py:99
  200.4 2.4 collective-permute-start.2
  202.9 1.2 collective-permute-start.1
  204.1 0.7 mul.201
  204.8 1.5 fusion.35
  206.4 1.5 fusion.37
  207.9 0.7 copy.25
  208.6 0.1 dynamic-slice_bitcast_fusion
  208.8 0.1 reshape.294
  209.0 0.1 reshape.295
  209.2 0.1 fusion.81
  209.3 0.1 fusion.79
  209.3 0.3 fusion.72
  209.6 0.6 reduce-precision_convert_fusion.2
  210.3 0.3 fusion.70
  210.5 0.1 maximum_bitcast_fusion.8
  210.7 0.1 fusion.68
  210.8 0.1 add_multiply_fusion
  210.9 1.6 fusion.40
  212.5 30.5 %fusion.87 = (bf16[1,1408,2816]{2,0,1:T(2,128)(2,1)}, bf16[1,1408,2816]{2,0,1:T(2,128)(2,1)S(1)}) fusion(bf16[2,1408,2816]{2,0,1:T(2,128)(2,1)} %all-gather.3.cloned.1.call-done), kind=kLoop, calls=%fused_computation.135 | loop fusion | bytes 31719424 | tf_op jit(solution)/shard_map/slice | solution.py:117
  243.0 4.0 fusion.17
  247.0 76.3 %slice_reduce_fusion = (bf16[32,44,2816]{2,1,0:T(8,128)(2,1)}, bf16[32,44,2816]{2,1,0:T(8,128)(2,1)}) fusion(bf16[2,32,44,2816]{3,0,2,1:T(2,128)(2,1)} %collective-permute-done.3), kind=kLoop, calls=%fused_computation.12 | loop fusion | bytes 31719424 | tf_op jit(solution)/shard_map/slice | solution.py:117
  323.3 9.7 %reshape_squeeze.13 = bf16[1408,2816]{1,0:T(8,128)(2,1)} reshape(bf16[32,44,2816]{2,1,0:T(8,128)(2,1)} %get-tuple-element.6) | data formatting | bytes 15859712 | tf_op jit(solution)/shard_map/reshape;squeeze | solution.py:117
  333.0 7.3 %fusion.34 = bf16[256,2816]{1,0:T(8,128)(2,1)S(1)} fusion(f32[256,2816]{1,0:T(8,128)} %fusion.17, bf16[256,1408]{0,1:T(8,128)(2,1)S(1)} %reshape.295, bf16[1408,2816]{1,0:T(8,128)(2,1)} %reshape_squeeze.13), kind=kOutput, calls=%fused_computation.47 | convolution fusion | flops 2037252096 | bytes 12976128 | tf_op jit(solution)/shard_map/dot_general | solution.py:122
  340.3 0.7 copy.28
  341.0 0.3 reshape.296
  341.3 0.1 constant_dynamic-slice_fusion.1
  341.4 0.1 reshape.298
  341.6 9.3 %reshape_squeeze.15 = bf16[1408,2816]{1,0:T(8,128)(2,1)} reshape(bf16[32,44,2816]{2,1,0:T(8,128)(2,1)} %get-tuple-element.5) | data formatting | bytes 15859712 | tf_op jit(solution)/shard_map/reshape;squeeze | solution.py:117
  350.9 7.3 %fusion.88 = f32[256,2816]{1,0:T(8,128)} fusion(bf16[256,1408]{0,1:T(8,128)(2,1)S(1)} %reshape.298, bf16[1408,2816]{1,0:T(8,128)(2,1)} %reshape_squeeze.15), kind=kOutput, calls=%fused_computation.136 | convolution fusion | flops 2030043136 | bytes 11534336 | tf_op jit(solution)/shard_map/dot_general | solution.py:127
  358.2 0.1 reshape.297
  358.3 8.1 %fusion.16 = f32[256,2816]{1,0:T(8,128)S(1)} fusion(bf16[256,1408]{0,1:T(8,128)(2,1)S(1)} %reshape.297, bf16[1,1408,2816]{2,0,1:T(2,128)(2,1)} %get-tuple-element.7), kind=kOutput, calls=%fused_computation.23 | convolution fusion | flops 2030043136 | bytes 11534336 | tf_op jit(solution)/shard_map/dot_general | solution.py:127
  366.6 2.7 fusion.47
  369.2 0.6 gather_fusion
  369.8 0.9 select_bitcast_fusion
  370.7 3.5 reshape_reshape.4
  374.2 5.4 %copy.30 = bf16[1,16,16,12,8,8]{5,2,4,1,3,0:T(8,128)(2,1)} copy(bf16[1,16,16,12,8,8]{2,1,5,4,3,0:T(8,128)(2,1)S(1)} %reshape_reshape.4) | data formatting | bytes 786432 | tf_op jit(solution)/shard_map/reshape;reshape | solution.py:140
  379.5 8.4 %reshape.317 = bf16[6,2,128,128,1]{3,2,1,0,4:T(8,128)(2,1)S(1)} reshape(bf16[1,12,16,8,16,8]{5,4,3,2,1,0:T(8,128)(2,1)} %bitcast.105) | data formatting | bytes 786432 | tf_op jit(solution)/shard_map/reshape.4
  387.9 10.9 %fusion.13 = f32[128,32,1,6,256]{4,0,3,1,2:T(8,128)} fusion(pred[128,32,128]{2,0,1:T(8,128)(4,1)S(1)} %copy-done.3, bf16[6,2,128,128,1]{3,2,1,0,4:T(8,128)(2,1)S(1)} %reshape.317, s32[128,32]{0,1:T(8,128)S(1)} %iota_add_fusion, bf16[2,128,128]{2,1,0:T(8,128)(2,1)S(1)} %get-tuple-element.16, bf16[2,128,128]{2,1,0:T(8,128)(2,1)S(1)} %get-tuple-element.15), kind=kOutput, calls=%fused_computation.21 | convolution fusion | flops 4845207552 | bytes 26230784 | tf_op jit(solution)/shard_map/sitkpv,pvn->sitkn/dot_general | solution.py:58
  398.8 14.5 %slice_add_fusion = f32[128,32,1,6,128]{4,0,3,1,2:T(8,128)} fusion(f32[128,32,1,6,256]{4,0,3,1,2:T(8,128)} %fusion.13), kind=kLoop, calls=%fused_computation.15 | loop fusion | flops 3145728 | bytes 37748736 | tf_op jit(solution)/shard_map/add | solution.py:59
  413.3 12.6 %copy.31 = f32[128,32,1,6,128]{0,4,3,1,2:T(8,128)} copy(f32[128,32,1,6,128]{4,0,3,1,2:T(8,128)} %slice_add_fusion) | data formatting | bytes 25165824 | tf_op jit(solution)/shard_map/add | solution.py:59
  425.9 17.3 %fusion.6 = (bf16[128,32,1,6,2,64]{0,1,4,5,3,2:T(8,128)(2,1)}, bf16[128,32,1,6,2,64]{0,1,4,5,3,2:T(8,128)(2,1)}) fusion(f32[128,32,1,6,2,64]{0,5,4,3,1,2:T(8,128)} %bitcast.104), kind=kLoop, calls=%fused_computation.14 | loop fusion | flops 12582912 | bytes 25165824 | tf_op jit(solution)/shard_map/convert_element_type | solution.py:23
  443.2 9.3 %fusion = f32[64,64]{1,0:T(8,128)S(1)} fusion(f32[128]{0:T(128)S(1)} %copy-done.8, bf16[128,32,1,6,2,64]{0,1,4,5,3,2:T(8,128)(2,1)} %get-tuple-element.10, bf16[128,32,1,6,2,64]{0,1,4,5,3,2:T(8,128)(2,1)} %get-tuple-element.9, bf16[2,64,2,32]{1,3,2,0:T(8,128)(2,1)S(1)} %copy-done.5, bf16[2,64,2,32]{1,3,2,0:T(8,128)(2,1)S(1)} %get-tuple-element.17), kind=kOutput, calls=%fused_computation.2 | convolution fusion | flops 2491559936 | bytes 12632576 | tf_op jit(solution)/shard_map/cxqi,sitkqy->tskcxy/dot_general | solution.py:65
  452.6 0.1 copy.34
  452.7 0.7 mul.233
  (40 shorter events, 0.4 us)
Async XLA Ops:
  6.5 1.0 copy-start
  6.5 193.9 %all-gather.3.cloned.1.call-start = ((), (), s32[]{:S(2)}) async-start(), calls=%async_computation | async-start | bytes 16355328 | tf_op jit(solution)/shard_map/all_gather | solution.py:99
  200.4 46.6 %collective-permute-start.3 = (bf16[2,32,44,2816]{3,0,2,1:T(2,128)(2,1)}, bf16[2,32,44,2816]{3,0,2,1:T(2,128)(2,1)}, u32[]{:S(2)}, u32[]{:S(2)}) collective-permute-start(bf16[2,32,44,2816]{3,0,2,1:T(2,128)(2,1)} %bitcast.103), channel_id=1, source_target_pairs={{0,1},{1,0},{2,3},{3,2},{4,5},{5,4},{6,7},{7,6},{8,9},{9,8},{10,11... | collective-permute-start | bytes 47579144 | tf_op jit(solution)/shard_map/ppermute | solution.py:100
  200.4 166.0 %collective-permute-start.2 = (bf16[2048,192]{0,1:T(8,128)(2,1)}, bf16[2048,192]{0,1:T(8,128)(2,1)}, u32[]{:S(2)}, u32[]{:S(2)}) collective-permute-start(bf16[2048,192]{0,1:T(8,128)(2,1)} %param.12), channel_id=1, source_target_pairs={{0,3},{1,2},{2,1},{3,0},{4,7},{5,6},{6,5},{7,4},{8,11},{9,10},{10,... | collective-permute-start | bytes 2359304 | tf_op jit(solution)/shard_map/ppermute | solution.py:102
  202.9 163.6 %collective-permute-start.1 = (bf16[2048,192]{0,1:T(8,128)(2,1)}, bf16[2048,192]{0,1:T(8,128)(2,1)}, u32[]{:S(2)}, u32[]{:S(2)}) collective-permute-start(bf16[2048,192]{0,1:T(8,128)(2,1)} %param.12), channel_id=1, source_target_pairs={{0,2},{1,3},{2,0},{3,1},{4,6},{5,7},{6,4},{7,5},{8,10},{9,11},{10,... | collective-permute-start | bytes 2359304 | tf_op jit(solution)/shard_map/ppermute | solution.py:102
  204.1 162.4 %collective-permute-start = (bf16[2048,192]{0,1:T(8,128)(2,1)}, bf16[2048,192]{0,1:T(8,128)(2,1)}, u32[]{:S(2)}, u32[]{:S(2)}) collective-permute-start(bf16[2048,192]{0,1:T(8,128)(2,1)} %param.12), channel_id=1, source_target_pairs={{0,1},{1,0},{2,3},{3,2},{4,5},{5,4},{6,7},{7,6},{8,9},{9,8},{10,11... | collective-permute-start | bytes 2359304 | tf_op jit(solution)/shard_map/ppermute | solution.py:102
  206.3 4.3 copy-start.6
  358.3 8.2 %copy-start.2 = (bf16[256,2048]{1,0:T(8,128)(2,1)S(1)}, bf16[256,2048]{1,0:T(8,128)(2,1)}, u32[]{:S(2)}) copy-start(bf16[256,2048]{1,0:T(8,128)(2,1)} %param.8) | copy-start | bytes 3145732
  358.3 8.2 %copy-start.4 = (f32[256,2816]{1,0:T(8,128)S(1)}, f32[256,2816]{1,0:T(8,128)}, u32[]{:S(2)}) copy-start(f32[256,2816]{1,0:T(8,128)} %fusion.88) | copy-start | bytes 8650756
  358.3 8.2 %copy-start.7 = (bf16[2048,192]{0,1:T(8,128)(2,1)S(1)}, bf16[2048,192]{0,1:T(8,128)(2,1)}, u32[]{:S(2)}) copy-start(bf16[2048,192]{0,1:T(8,128)(2,1)} %param.12) | copy-start | bytes 2359300
  379.5 8.4 %copy-start.3 = (pred[128,32,128]{2,0,1:T(8,128)(4,1)S(1)}, pred[128,32,128]{2,0,1:T(8,128)(4,1)}, u32[]{:S(2)}) copy-start(pred[128,32,128]{2,0,1:T(8,128)(4,1)} %fusion.40) | copy-start | bytes 1572868
  425.9 17.3 %copy-start.5 = (bf16[2,64,2,32]{1,3,2,0:T(8,128)(2,1)S(1)}, bf16[2,64,2,32]{1,3,2,0:T(8,128)(2,1)}, u32[]{:S(2)}) copy-start(bf16[2,64,2,32]{1,3,2,0:T(8,128)(2,1)} %get-tuple-element.18) | copy-start | bytes 49156
  425.9 17.3 %copy-start.8 = (f32[128]{0:T(128)S(1)}, f32[128]{0:T(128)}, u32[]{:S(2)}) copy-start(f32[128]{0:T(128)} %param.15) | copy-start | bytes 1540
  443.2 10.2 %copy-start.1 = (bf16[88,2048]{1,0:T(8,128)(2,1)S(1)}, bf16[88,2048]{1,0:T(8,128)(2,1)}, u32[]{:S(2)}) copy-start(bf16[88,2048]{1,0:T(8,128)(2,1)} %param.11) | copy-start | bytes 1081348
Sparse Core Ops, SparseCore 0:
  9.9 190.4 all-gather.2
where the time goes:
time: 465 us; the launch traced here: 460 us
  waiting for transfers between devices  191 us (41%)
  local copies, waits for them, and re-layouts  163 us (35%)
  matrix products  49.7 us (11%)
  other arithmetic  39.8 us (9%)
  between operations  14 us (3%)
    all_gather x1, waiting for transfers between devices, local(): gathered = lax.all_gather(packed, 'tile', axis=1, tiled=False)  191 us
    slice x2, local copies, waits for them, and re-layouts, weights(): g[1].reshape(n_tile * depth, width)  107 us
    convert_element_type x3, other arithmetic, split_bf16(): return (hi.astype(bf16), lo.astype(bf16))  18 us
    add x1, other arithmetic, imaging(): half = out1[..., :2 * PIX] + out1[..., 2 * PIX:]  14.5 us
    add x1, local copies, waits for them, and re-layouts, imaging(): half = out1[..., :2 * PIX] + out1[..., 2 * PIX:]  12.6 us
    dot_general x1, matrix products, imaging(): jnp.einsum('sitkpv,pvn->sitkn', masked, t1s, preferred_element_type=f32)  10.9 us
    another operation x1, local copies, waits for them, and re-layouts, weights(): g[0].reshape(n_tile * depth, width)  9.69 us
    dot_general x1, matrix products, imaging(): jnp.einsum('cxqi,sitkqy->tskcxy', t2cat, hcat, preferred_element_type=f32)  9.35 us
  transfers between devices with their start and end apart: 5, of which 1 were waited for; matrix products, arithmetic and copies ran while one was open for 35% of the time, Pallas kernels for 0%

commit v1 on v0

--- a/solution.py
+++ b/solution.py
@@ -85,18 +85,18 @@
     up_rows, ff = up_weight.shape
     down_rows = down_weight.shape[0]
     up_half, down_half = up_rows // 2, down_rows // 2
-    depth = max(up_half, down_half)
+    depth = -(-(up_half + down_half) // 16) * 16
     width = max(ff, d_model)
     up_part = lax.dynamic_slice_in_dim(up_weight, half * up_half, up_half, 0)
     down_part = lax.dynamic_slice_in_dim(down_weight, half * down_half, down_half, 0)
-    packed = jnp.stack(
+    packed = jnp.concatenate(
         [
-            jnp.pad(up_part, ((0, depth - up_half), (0, width - ff))),
-            jnp.pad(down_part, ((0, depth - down_half), (0, width - d_model))),
+            jnp.pad(up_part, ((0, 0), (0, width - ff))),
+            jnp.pad(down_part, ((0, depth - up_half - down_half), (0, width - d_model))),
         ],
         0,
     )
-    gathered = lax.all_gather(packed, "tile", axis=1, tiled=False)
+    gathered = lax.all_gather(packed, "tile", axis=0, tiled=True)
     sibling = lax.ppermute(gathered, "src", [(s, s ^ 1) for s in range(n_src)])
     head_parts = [head_weight] + [
         lax.ppermute(head_weight, "src", [(s, s ^ k) for s in range(n_src)]) for k in range(1, n_src)
@@ -106,26 +106,21 @@
     mean_square = jnp.mean(residual * residual, axis=1, keepdims=True)
     normed = (residual * lax.rsqrt(mean_square + 1e-05) * norm_gain).astype(jnp.bfloat16)
 
-    def halves(x, rows):
+    def spread(x, rows, start):
         view = x.reshape(x.shape[0], n_tile, 2, rows // 2)
-        pad = ((0, 0), (0, 0), (0, depth - rows // 2))
+        pad = ((0, 0), (0, 0), (start, depth - start - rows // 2))
         mine = jnp.pad(lax.dynamic_index_in_dim(view, half, 2, keepdims=False), pad)
         other = jnp.pad(lax.dynamic_index_in_dim(view, 1 - half, 2, keepdims=False), pad)
         return mine.reshape(x.shape[0], -1), other.reshape(x.shape[0], -1)
 
-    def weights(g):
-        return g[0].reshape(n_tile * depth, width), g[1].reshape(n_tile * depth, width)
-
-    up_mine, down_mine = weights(gathered)
-    up_other, down_other = weights(sibling)
-    normed_mine, normed_other = halves(normed, up_rows)
-    pre_act = jnp.dot(normed_mine, up_mine, preferred_element_type=jnp.float32) + jnp.dot(
-        normed_other, up_other, preferred_element_type=jnp.float32
+    normed_mine, normed_other = spread(normed, up_rows, 0)
+    pre_act = jnp.dot(normed_mine, gathered, preferred_element_type=jnp.float32) + jnp.dot(
+        normed_other, sibling, preferred_element_type=jnp.float32
     )
     hidden = jax.nn.gelu(pre_act[:, :ff]).astype(jnp.bfloat16)
-    hidden_mine, hidden_other = halves(hidden, down_rows)
-    branch_out = jnp.dot(hidden_mine, down_mine, preferred_element_type=jnp.float32) + jnp.dot(
-        hidden_other, down_other, preferred_element_type=jnp.float32
+    hidden_mine, hidden_other = spread(hidden, down_rows, up_half)
+    branch_out = jnp.dot(hidden_mine, gathered, preferred_element_type=jnp.float32) + jnp.dot(
+        hidden_other, sibling, preferred_element_type=jnp.float32
     )
     branch_out = branch_out[:, :d_model]
     mixed = (residual + branch_out).astype(jnp.bfloat16)

time: 465 us -> 337 us (0.72)
  local copies, waits for them, and re-layouts: 163 us -> 35.4 us
  matrix products: 49.7 us -> 55.8 us
    slice x2 -> x0, local copies, waits for them, and re-layouts: 107 us -> none  [weights(): g[1].reshape(n_tile * depth, width)]
    another operation x5 -> x1, local copies, waits for them, and re-layouts: 28.6 us -> 8.26 us  [the longest x1 9.69 us: weights(): g[0].reshape(n_tile * depth, width)]
    all_gather x1, waiting for transfers between devices: 191 us -> 184 us  [local(): gathered = lax.all_gather(packed, 'tile', axis=0, tiled=True)]
    dot_general x4, matrix products: 26.7 us -> 33.1 us  [the longest x1 9.91 us: local(): jnp.dot(normed_other, sibling, preferred_element_type=jnp.float32)]
  transfers between devices with their start and end apart: 5 -> 5, of which waited for: 1 -> 2; matrix products, arithmetic and copies ran while one was open for 35% -> 12% of each run, Pallas kernels for 0% -> 0%
where the time goes in v1:
time: 337 us; the launch traced here: 336 us
  waiting for transfers between devices  188 us (56%)
  matrix products  55.8 us (17%)
  other arithmetic  38.5 us (11%)
  local copies, waits for them, and re-layouts  35.4 us (11%)
  between operations  13.8 us (4%)
  starting transfers between devices  3.89 us (1%)
    all_gather x1, waiting for transfers between devices, local(): gathered = lax.all_gather(packed, 'tile', axis=0, tiled=True)  184 us
    convert_element_type x3, other arithmetic, split_bf16(): return (hi.astype(bf16), lo.astype(bf16))  18 us
    add x1, other arithmetic, imaging(): half = out1[..., :2 * PIX] + out1[..., 2 * PIX:]  14.5 us
    add x1, local copies, waits for them, and re-layouts, imaging(): half = out1[..., :2 * PIX] + out1[..., 2 * PIX:]  12.6 us
    dot_general x1, matrix products, imaging(): jnp.einsum('sitkpv,pvn->sitkn', masked, t1s, preferred_element_type=f32)  10.7 us
    dot_general x1, matrix products, local(): jnp.dot(normed_other, sibling, preferred_element_type=jnp.float32)  9.91 us
    dot_general x1, matrix products, imaging(): jnp.einsum('cxqi,sitkqy->tskcxy', t2cat, hcat, preferred_element_type=f32)  9.27 us
    another operation x2, local copies, waits for them, and re-layouts, local(): coeffs.reshape(tile_count, GRID, GRID, 12, SUB, SUB)  8.8 us
  transfers between devices with their start and end apart: 5, of which 2 were waited for; matrix products, arithmetic and copies ran while one was open for 12% of the time, Pallas kernels for 0%

profile of v1, /device:TPU:0, one launch (start us, length us, event | category | flops | bytes accessed | tf_op | source)
XLA Modules:
  0.0 335.9 jit_solution(12676455966001698916)
XLA Ops:
  6.6 1.0 copy-done
  7.5 0.1 constant_dynamic-slice_fusion
  7.6 0.9 constant_dynamic-slice_fusion.1
  8.5 0.8 fusion.53
  9.3 0.0 all-gather.2.cloned.1.call-update
  9.4 184.2 %all-gather.2.cloned.1.call-done = bf16[2560,2816]{1,0:T(8,128)(2,1)} async-done(((bf16[80,2816]{1,0:T(8,128)(2,1)}), bf16[2560,2816]{1,0:T(8,128)(2,1)}) %all-gather.2.cloned.1.call-update) | async-done | bytes 14417936 | tf_op jit(solution)/shard_map/all_gather | solution.py:99
  193.6 0.5 collective-permute-start
  194.1 3.4 %collective-permute-start.1 = (bf16[2048,192]{0,1:T(8,128)(2,1)}, bf16[2048,192]{0,1:T(8,128)(2,1)}, u32[]{:S(2)}, u32[]{:S(2)}) collective-permute-start(bf16[2048,192]{0,1:T(8,128)(2,1)} %param.12), channel_id=1, source_target_pairs={{0,2},{1,3},{2,0},{3,1},{4,6},{5,7},{6,4},{7,5},{8,10},{9,11},{10,... | collective-permute-start | bytes 2359304 | tf_op jit(solution)/shard_map/ppermute | solution.py:102
  197.5 1.5 fusion.33
  199.0 0.3 fusion.35
  199.3 0.5 copy.32
  199.9 0.1 dynamic-slice_bitcast_fusion.2
  200.0 0.1 pad.18
  200.1 0.1 pad.20
  200.2 0.4 copy-done.9
  200.6 0.1 fusion.81
  200.7 0.1 fusion.79
  200.8 0.3 fusion.72
  201.0 0.6 reduce-precision_convert_fusion.2
  201.7 0.3 fusion.70
  201.9 0.1 maximum_bitcast_fusion.8
  202.1 0.1 fusion.68
  202.2 0.1 add_multiply_fusion
  202.3 1.6 fusion.38
  203.9 7.6 %fusion.87 = f32[256,2816]{1,0:T(8,128)S(1)} fusion(bf16[256,2560]{0,1:T(8,128)(2,1)S(1)} %bitcast.98, bf16[2560,2816]{1,0:T(8,128)(2,1)} %all-gather.2.cloned.1.call-done), kind=kOutput, calls=%fused_computation.129 | convolution fusion | flops 3690987520 | bytes 18612224 | tf_op jit(solution)/shard_map/dot_general | solution.py:117
  211.5 4.2 %collective-permute-done.3 = bf16[2560,2816]{1,0:T(8,128)(2,1)} collective-permute-done((bf16[2560,2816]{1,0:T(8,128)(2,1)}, bf16[2560,2816]{1,0:T(8,128)(2,1)}, u32[]{:S(2)}, u32[]{:S(2)}) %collective-permute-start.3) | collective-permute-done | bytes 14417952 | tf_op jit(solution)/shard_map/ppermute | solution.py:100
  215.7 9.9 %fusion.32 = bf16[256,2816]{1,0:T(8,128)(2,1)S(1)} fusion(f32[256,2816]{1,0:T(8,128)S(1)} %fusion.87, bf16[256,2560]{0,1:T(8,128)(2,1)S(1)} %bitcast.102, bf16[2560,2816]{1,0:T(8,128)(2,1)} %collective-permute-done.3), kind=kOutput, calls=%fused_computation.41 | convolution fusion | flops 3698196480 | bytes 20054016 | tf_op jit(solution)/shard_map/dot_general | solution.py:117
  225.6 0.7 copy.33
  226.3 0.3 reshape.294
  226.7 0.1 dynamic-slice_bitcast_fusion.1
  226.8 0.1 pad.21.clone
  226.9 0.1 pad.22.clone
  227.0 7.6 %fusion.88 = f32[256,2816]{1,0:T(8,128)S(1)} fusion(bf16[256,2560]{0,1:T(8,128)(2,1)S(1)} %bitcast.99, bf16[2560,2816]{1,0:T(8,128)(2,1)} %all-gather.2.cloned.1.call-done), kind=kOutput, calls=%fused_computation.130 | convolution fusion | flops 3690987520 | bytes 18612224 | tf_op jit(solution)/shard_map/dot_general | solution.py:122
  234.6 0.0 copy-start.3
  234.6 7.9 %fusion.89 = f32[256,2816]{1,0:T(8,128)S(1)} fusion(bf16[256,2560]{0,1:T(8,128)(2,1)S(1)} %bitcast.100, bf16[2560,2816]{1,0:T(8,128)(2,1)} %collective-permute-done.3), kind=kOutput, calls=%fused_computation.131 | convolution fusion | flops 3690987520 | bytes 18612224 | tf_op jit(solution)/shard_map/dot_general | solution.py:122
  242.6 2.7 fusion.45
  245.3 0.6 gather_fusion
  245.9 0.9 select_bitcast_fusion
  246.7 3.5 %reshape_reshape.4 = bf16[1,16,16,12,8,8]{2,1,5,4,3,0:T(8,128)(2,1)S(1)} reshape(bf16[256,4,192]{0,2,1:T(8,128)(2,1)} %select_bitcast_fusion) | data formatting | bytes 786432 | tf_op jit(solution)/shard_map/reshape;reshape | solution.py:135
  250.2 5.3 %copy.38 = bf16[1,16,16,12,8,8]{5,2,4,1,3,0:T(8,128)(2,1)} copy(bf16[1,16,16,12,8,8]{2,1,5,4,3,0:T(8,128)(2,1)S(1)} %reshape_reshape.4) | data formatting | bytes 786432 | tf_op jit(solution)/shard_map/reshape;reshape | solution.py:135
  255.6 8.3 %reshape.310 = bf16[6,2,128,128,1]{3,2,1,0,4:T(8,128)(2,1)S(1)} reshape(bf16[1,12,16,8,16,8]{5,4,3,2,1,0:T(8,128)(2,1)} %bitcast.97) | data formatting | bytes 786432 | tf_op jit(solution)/shard_map/reshape.2
  263.8 10.7 %fusion.13 = f32[128,32,1,6,256]{4,0,3,1,2:T(8,128)} fusion(pred[128,32,128]{2,0,1:T(8,128)(4,1)S(1)} %copy-done.4, bf16[6,2,128,128,1]{3,2,1,0,4:T(8,128)(2,1)S(1)} %reshape.310, s32[128,32]{0,1:T(8,128)S(1)} %iota_add_fusion, bf16[2,128,128]{2,1,0:T(8,128)(2,1)S(1)} %get-tuple-element.12, bf16[2,128,128]{2,1,0:T(8,128)(2,1)S(1)} %get-tuple-element.11), kind=kOutput, calls=%fused_computation.19 | convolution fusion | flops 4845207552 | bytes 26230784 | tf_op jit(solution)/shard_map/sitkpv,pvn->sitkn/dot_general | solution.py:58
  274.5 14.5 %slice_add_fusion = f32[128,32,1,6,128]{4,0,3,1,2:T(8,128)} fusion(f32[128,32,1,6,256]{4,0,3,1,2:T(8,128)} %fusion.13), kind=kLoop, calls=%fused_computation.13 | loop fusion | flops 3145728 | bytes 37748736 | tf_op jit(solution)/shard_map/add | solution.py:59
  289.0 12.6 %copy.39 = f32[128,32,1,6,128]{0,4,3,1,2:T(8,128)} copy(f32[128,32,1,6,128]{4,0,3,1,2:T(8,128)} %slice_add_fusion) | data formatting | bytes 25165824 | tf_op jit(solution)/shard_map/add | solution.py:59
  301.6 17.3 %fusion.6 = (bf16[128,32,1,6,2,64]{0,1,4,5,3,2:T(8,128)(2,1)}, bf16[128,32,1,6,2,64]{0,1,4,5,3,2:T(8,128)(2,1)}) fusion(f32[128,32,1,6,2,64]{0,5,4,3,1,2:T(8,128)} %bitcast.96), kind=kLoop, calls=%fused_computation.12 | loop fusion | flops 12582912 | bytes 25165824 | tf_op jit(solution)/shard_map/convert_element_type | solution.py:23
  319.0 9.3 %fusion = f32[64,64]{1,0:T(8,128)S(1)} fusion(f32[128]{0:T(128)S(1)} %copy-done.10, bf16[128,32,1,6,2,64]{0,1,4,5,3,2:T(8,128)(2,1)} %get-tuple-element.6, bf16[128,32,1,6,2,64]{0,1,4,5,3,2:T(8,128)(2,1)} %get-tuple-element.5, bf16[2,64,2,32]{1,3,2,0:T(8,128)(2,1)S(1)} %copy-done.5, bf16[2,64,2,32]{1,3,2,0:T(8,128)(2,1)S(1)} %get-tuple-element.13), kind=kOutput, calls=%fused_computation.2 | convolution fusion | flops 2491559936 | bytes 12632576 | tf_op jit(solution)/shard_map/cxqi,sitkqy->tskcxy/dot_general | solution.py:65
  328.3 0.1 copy.42
  328.3 0.7 mul.233
  (36 shorter events, 0.1 us)
Async XLA Ops:
  6.5 1.0 copy-start
  6.5 192.5 %copy-start.2 = (bf16[256,2048]{1,0:T(8,128)(2,1)S(1)}, bf16[256,2048]{1,0:T(8,128)(2,1)}, u32[]{:S(2)}) copy-start(bf16[256,2048]{1,0:T(8,128)(2,1)} %param.8) | copy-start | bytes 3145732
  6.5 192.5 %copy-start.6 = (f32[2048]{0:T(1024)S(1)}, f32[2048]{0:T(1024)}, u32[]{:S(2)}) copy-start(f32[2048]{0:T(1024)} %param.9) | copy-start | bytes 24580
  6.5 187.0 %all-gather.2.cloned.1.call-start = ((), (), s32[]{:S(2)}) async-start(), calls=%async_computation | async-start | bytes 14868480 | tf_op jit(solution)/shard_map/all_gather | solution.py:99
  193.6 22.1 %collective-permute-start.3 = (bf16[2560,2816]{1,0:T(8,128)(2,1)}, bf16[2560,2816]{1,0:T(8,128)(2,1)}, u32[]{:S(2)}, u32[]{:S(2)}) collective-permute-start(bf16[2560,2816]{1,0:T(8,128)(2,1)} %all-gather.2.cloned.1.call-done), channel_id=1, source_target_pairs={{0,1},{1,0},{2,3},{3,2},{4,5},{5,4},{6,7},{7,6},{8,9},{9,8},{10,11... | collective-permute-start | bytes 43253768 | tf_op jit(solution)/shard_map/ppermute | solution.py:100
  193.6 49.0 %collective-permute-start = (bf16[2048,192]{0,1:T(8,128)(2,1)}, bf16[2048,192]{0,1:T(8,128)(2,1)}, u32[]{:S(2)}, u32[]{:S(2)}) collective-permute-start(bf16[2048,192]{0,1:T(8,128)(2,1)} %param.12), channel_id=1, source_target_pairs={{0,1},{1,0},{2,3},{3,2},{4,5},{5,4},{6,7},{7,6},{8,9},{9,8},{10,11... | collective-permute-start | bytes 2359304 | tf_op jit(solution)/shard_map/ppermute | solution.py:102
  194.1 48.5 %collective-permute-start.1 = (bf16[2048,192]{0,1:T(8,128)(2,1)}, bf16[2048,192]{0,1:T(8,128)(2,1)}, u32[]{:S(2)}, u32[]{:S(2)}) collective-permute-start(bf16[2048,192]{0,1:T(8,128)(2,1)} %param.12), channel_id=1, source_target_pairs={{0,2},{1,3},{2,0},{3,1},{4,6},{5,7},{6,4},{7,5},{8,10},{9,11},{10,... | collective-permute-start | bytes 2359304 | tf_op jit(solution)/shard_map/ppermute | solution.py:102
  197.5 45.1 %collective-permute-start.2 = (bf16[2048,192]{0,1:T(8,128)(2,1)}, bf16[2048,192]{0,1:T(8,128)(2,1)}, u32[]{:S(2)}, u32[]{:S(2)}) collective-permute-start(bf16[2048,192]{0,1:T(8,128)(2,1)} %param.12), channel_id=1, source_target_pairs={{0,3},{1,2},{2,1},{3,0},{4,7},{5,6},{6,5},{7,4},{8,11},{9,10},{10,... | collective-permute-start | bytes 2359304 | tf_op jit(solution)/shard_map/ppermute | solution.py:102
  199.9 0.7 copy-start.9
  200.0 2.1 copy-start.7
  234.6 8.0 %copy-start.3 = (bf16[256,2048]{1,0:T(8,128)(2,1)S(1)}, bf16[256,2048]{1,0:T(8,128)(2,1)}, u32[]{:S(2)}) copy-start(bf16[256,2048]{1,0:T(8,128)(2,1)} %param.8) | copy-start | bytes 3145732
  234.6 8.0 %copy-start.8 = (bf16[2048,192]{0,1:T(8,128)(2,1)S(1)}, bf16[2048,192]{0,1:T(8,128)(2,1)}, u32[]{:S(2)}) copy-start(bf16[2048,192]{0,1:T(8,128)(2,1)} %param.12) | copy-start | bytes 2359300
  255.5 8.3 %copy-start.4 = (pred[128,32,128]{2,0,1:T(8,128)(4,1)S(1)}, pred[128,32,128]{2,0,1:T(8,128)(4,1)}, u32[]{:S(2)}) copy-start(pred[128,32,128]{2,0,1:T(8,128)(4,1)} %fusion.38) | copy-start | bytes 1572868
  301.6 17.3 %copy-start.5 = (bf16[2,64,2,32]{1,3,2,0:T(8,128)(2,1)S(1)}, bf16[2,64,2,32]{1,3,2,0:T(8,128)(2,1)}, u32[]{:S(2)}) copy-start(bf16[2,64,2,32]{1,3,2,0:T(8,128)(2,1)} %get-tuple-element.14) | copy-start | bytes 49156
  301.6 17.3 %copy-start.10 = (f32[128]{0:T(128)S(1)}, f32[128]{0:T(128)}, u32[]{:S(2)}) copy-start(f32[128]{0:T(128)} %param.15) | copy-start | bytes 1540
  319.0 10.1 %copy-start.1 = (bf16[88,2048]{1,0:T(8,128)(2,1)S(1)}, bf16[88,2048]{1,0:T(8,128)(2,1)}, u32[]{:S(2)}) copy-start(bf16[88,2048]{1,0:T(8,128)(2,1)} %param.11) | copy-start | bytes 1081348
Sparse Core Ops, SparseCore 0:
  9.5 184.0 all-gather.1

commit v2 on v1

--- a/solution.py
+++ b/solution.py
@@ -53,16 +53,9 @@
     keep = (dist <= (source_cutoff * source_cutoff)[:, None, None]) & (j[:, None, :] >= 0) & (j[:, None, :] < W)
     masked = jnp.where(keep[:, :, None, None, None, :], strips, jnp.zeros((), bf16))
     t1, t2 = phase_tables()
-    t1h, t1l = split_bf16(t1)
-    t1s = jnp.concatenate([t1h, t1l], -1)
-    out1 = jnp.einsum("sitkpv,pvn->sitkn", masked, t1s, preferred_element_type=f32)
-    half = out1[..., : 2 * PIX] + out1[..., 2 * PIX:]
+    half = jnp.einsum("sitkpv,pvn->sitkn", masked.astype(f32), t1, precision=lax.Precision.HIGH)
     half = half.reshape(S, W, T, 6, 2, PIX)
-    hh, hl = split_bf16(half)
-    hcat = jnp.concatenate([hh, hl, hh], 4)
-    t2h, t2l = split_bf16(t2)
-    t2cat = jnp.concatenate([t2h, t2h, t2l], 2)
-    field = jnp.einsum("cxqi,sitkqy->tskcxy", t2cat, hcat, preferred_element_type=f32)
+    field = jnp.einsum("cxqi,sitkqy->tskcxy", t2, half, precision=lax.Precision.HIGH)
     power = jnp.sum(field * field * source_weight[None, :, None, None, None, None], axis=(1, 2, 3))
     return power.reshape(T, PIX * PIX) * (1.0 / (6.0 * W * W * S))
 

time: 337 us -> 336 us (level)
  other arithmetic: 38.5 us -> 7.29 us
  matrix products: 55.8 us -> 75.9 us
  local copies, waits for them, and re-layouts: 35.4 us -> 45.7 us
    dot_general x0 -> x1, local copies, waits for them, and re-layouts: none -> 22.9 us  [imaging(): jnp.einsum('sitkpv,pvn->sitkn', masked.astype(f32), t1, precision=lax.Pre...]
    dot_general x2 -> x3, matrix products: 20 us -> 40.2 us  [the longest x1 19 us: imaging(): jnp.einsum('cxqi,sitkqy->tskcxy', t2, half, precision=lax.Precision.HIGH)]
    convert_element_type x3 -> x0, other arithmetic: 18 us -> none  [split_bf16(): return (hi.astype(bf16), lo.astype(bf16))]
    add x1 -> x0, other arithmetic: 14.5 us -> none  [imaging(): half = out1[..., :2 * PIX] + out1[..., 2 * PIX:]]
    add x1 -> x0, local copies, waits for them, and re-layouts: 12.6 us -> none  [imaging(): half = out1[..., :2 * PIX] + out1[..., 2 * PIX:]]
where the time goes in v2:
time: 336 us; the launch traced here: 334 us
  waiting for transfers between devices  188 us (56%)
  matrix products  75.9 us (23%)
  local copies, waits for them, and re-layouts  45.7 us (14%)
  between operations  13.8 us (4%)
  other arithmetic  7.29 us (2%)
  starting transfers between devices  3.89 us (1%)
    all_gather x1, waiting for transfers between devices, local(): gathered = lax.all_gather(packed, 'tile', axis=0, tiled=True)  184 us
    dot_general x1, local copies, waits for them, and re-layouts, imaging(): jnp.einsum('sitkpv,pvn->sitkn', masked.astype(f32), t1, precision=lax.Pre...  22.9 us
    dot_general x1, matrix products, imaging(): jnp.einsum('cxqi,sitkqy->tskcxy', t2, half, precision=lax.Precision.HIGH)  19 us
    dot_general x1, matrix products, imaging(): jnp.einsum('sitkpv,pvn->sitkn', masked.astype(f32), t1, precision=lax.Pre...  14.6 us
    dot_general x1, matrix products, local(): jnp.dot(normed_other, sibling, preferred_element_type=jnp.float32)  9.91 us
    another operation x2, local copies, waits for them, and re-layouts, local(): coeffs.reshape(tile_count, GRID, GRID, 12, SUB, SUB)  8.8 us
    another operation x1, local copies, waits for them, and re-layouts  8.2 us
    dot_general x1, matrix products, local(): jnp.dot(hidden_other, sibling, preferred_element_type=jnp.float32)  7.93 us
  transfers between devices with their start and end apart: 5, of which 2 were waited for; matrix products, arithmetic and copies ran while one was open for 12% of the time, Pallas kernels for 0%

profile of v2, /device:TPU:0, one launch (start us, length us, event | category | flops | bytes accessed | tf_op | source)
XLA Modules:
  0.0 334.5 jit_solution(13254922369213393428)
XLA Ops:
  6.6 1.0 copy-done
  7.5 0.1 constant_dynamic-slice_fusion
  7.6 0.9 constant_dynamic-slice_fusion.1
  8.5 0.8 fusion.45
  9.3 0.0 all-gather.2.cloned.1.call-update
  9.3 184.2 %all-gather.2.cloned.1.call-done = bf16[2560,2816]{1,0:T(8,128)(2,1)} async-done(((bf16[80,2816]{1,0:T(8,128)(2,1)}), bf16[2560,2816]{1,0:T(8,128)(2,1)}) %all-gather.2.cloned.1.call-update) | async-done | bytes 14417936 | tf_op jit(solution)/shard_map/all_gather | solution.py:92
  193.6 0.5 collective-permute-start
  194.1 3.4 %collective-permute-start.1 = (bf16[2048,192]{0,1:T(8,128)(2,1)}, bf16[2048,192]{0,1:T(8,128)(2,1)}, u32[]{:S(2)}, u32[]{:S(2)}) collective-permute-start(bf16[2048,192]{0,1:T(8,128)(2,1)} %param.12), channel_id=1, source_target_pairs={{0,2},{1,3},{2,0},{3,1},{4,6},{5,7},{6,4},{7,5},{8,10},{9,11},{10,... | collective-permute-start | bytes 2359304 | tf_op jit(solution)/shard_map/ppermute | solution.py:95
  197.5 1.5 fusion.26
  199.0 0.3 fusion.28
  199.3 0.5 copy.27
  199.9 0.0 copy-start.9
  199.9 0.0 copy-start.7
  199.9 0.1 dynamic-slice_bitcast_fusion.2
  200.0 0.1 pad.18
  200.1 0.1 pad.20
  200.2 0.4 copy-done.9
  200.6 0.1 fusion.67
  200.6 0.1 fusion.64
  200.8 0.1 fusion.65
  200.9 0.1 fusion.61
  201.0 0.6 maximum_bitcast_fusion.4
  201.7 0.1 fusion.49
  201.8 0.1 add_multiply_fusion
  201.9 0.1 iota_add_fusion
  202.0 2.4 fusion.31
  204.4 7.6 %fusion.72 = f32[256,2816]{1,0:T(8,128)S(1)} fusion(bf16[256,2560]{0,1:T(8,128)(2,1)S(1)} %bitcast.100, bf16[2560,2816]{1,0:T(8,128)(2,1)} %all-gather.2.cloned.1.call-done), kind=kOutput, calls=%fused_computation.107 | convolution fusion | flops 3690987520 | bytes 18612224 | tf_op jit(solution)/shard_map/dot_general | solution.py:110
  212.0 3.6 %collective-permute-done.3 = bf16[2560,2816]{1,0:T(8,128)(2,1)} collective-permute-done((bf16[2560,2816]{1,0:T(8,128)(2,1)}, bf16[2560,2816]{1,0:T(8,128)(2,1)}, u32[]{:S(2)}, u32[]{:S(2)}) %collective-permute-start.3) | collective-permute-done | bytes 14417952 | tf_op jit(solution)/shard_map/ppermute | solution.py:93
  215.7 9.9 %fusion.25 = bf16[256,2816]{1,0:T(8,128)(2,1)S(1)} fusion(f32[256,2816]{1,0:T(8,128)S(1)} %fusion.72, bf16[256,2560]{0,1:T(8,128)(2,1)S(1)} %bitcast.104, bf16[2560,2816]{1,0:T(8,128)(2,1)} %collective-permute-done.3), kind=kOutput, calls=%fused_computation.31 | convolution fusion | flops 3698196480 | bytes 20054016 | tf_op jit(solution)/shard_map/dot_general | solution.py:110
  225.6 0.7 copy.28
  226.3 0.3 reshape.262
  226.6 0.1 dynamic-slice_bitcast_fusion.1
  226.8 0.1 pad.21.clone
  226.8 0.1 pad.22.clone
  226.9 7.6 %fusion.73 = f32[256,2816]{1,0:T(8,128)S(1)} fusion(bf16[256,2560]{0,1:T(8,128)(2,1)S(1)} %bitcast.101, bf16[2560,2816]{1,0:T(8,128)(2,1)} %all-gather.2.cloned.1.call-done), kind=kOutput, calls=%fused_computation.108 | convolution fusion | flops 3690987520 | bytes 18612224 | tf_op jit(solution)/shard_map/dot_general | solution.py:115
  234.6 7.9 %fusion.74 = f32[256,2816]{1,0:T(8,128)S(1)} fusion(bf16[256,2560]{0,1:T(8,128)(2,1)S(1)} %bitcast.102, bf16[2560,2816]{1,0:T(8,128)(2,1)} %collective-permute-done.3), kind=kOutput, calls=%fused_computation.109 | convolution fusion | flops 3690987520 | bytes 18612224 | tf_op jit(solution)/shard_map/dot_general | solution.py:115
  242.6 2.7 fusion.38
  245.3 0.6 gather_fusion
  245.9 0.9 select_bitcast_fusion
  246.7 3.5 %reshape_reshape.4 = bf16[1,16,16,12,8,8]{2,1,5,4,3,0:T(8,128)(2,1)S(1)} reshape(bf16[256,4,192]{0,2,1:T(8,128)(2,1)} %select_bitcast_fusion) | data formatting | bytes 786432 | tf_op jit(solution)/shard_map/reshape;reshape | solution.py:128
  250.2 5.3 %copy.33 = bf16[1,16,16,12,8,8]{5,2,4,1,3,0:T(8,128)(2,1)} copy(bf16[1,16,16,12,8,8]{2,1,5,4,3,0:T(8,128)(2,1)S(1)} %reshape_reshape.4) | data formatting | bytes 786432 | tf_op jit(solution)/shard_map/reshape;reshape | solution.py:128
  255.5 8.2 %reshape.276 = bf16[6,2,128,128,1]{3,2,1,0,4:T(8,128)(2,1)S(1)} reshape(bf16[1,12,16,8,16,8]{5,4,3,2,1,0:T(8,128)(2,1)} %bitcast.99) | data formatting | bytes 786432 | tf_op jit(solution)/shard_map/reshape.2
  263.8 6.5 %fusion.33 = bf16[128,32,6,2,128]{4,1,3,2,0:T(8,128)(2,1)} fusion(bf16[6,2,128,128,1]{3,2,1,0,4:T(8,128)(2,1)S(1)} %reshape.276, s32[128,32]{1,0:T(8,128)S(1)} %iota_add_fusion), kind=kOutput, calls=%fused_computation.42 | convolution fusion | flops 1611137024 | bytes 12992512 | tf_op jit(solution)/shard_map/siu,tkpuv->sitkpv/dot_general | solution.py:49
  270.2 14.6 %fusion.6 = f32[128,32,6,2,64,1]{4,1,3,2,0,5:T(8,128)} fusion(f32[2,64,2,128,1,1]{3,1,0,2,5,4:T(8,128)S(1)} %bitcast.105, bf16[128,32,6,2,128]{4,1,3,2,0:T(8,128)(2,1)} %fusion.33, pred[128,32,128]{2,1,0:T(8,128)(4,1)S(1)} %copy-done.2), kind=kOutput, calls=%fused_computation.9 | convolution fusion | flops 4838129664 | bytes 25821184 | tf_op jit(solution)/shard_map/sitkpv,pvn->sitkn/dot_general | solution.py:56
  284.9 22.9 %copy.42 = f32[128,32,6,2,64,1]{0,1,3,5,4,2:T(8,128)} copy(f32[128,32,6,2,64,1]{4,1,3,2,0,5:T(8,128)} %fusion.6) | data formatting | bytes 25165824 | tf_op jit(solution)/shard_map/sitkpv,pvn->sitkn/dot_general | solution.py:56
  307.8 19.0 %fusion = f32[64,64]{1,0:T(8,128)S(1)} fusion(f32[128]{0:T(128)S(1)} %copy-done.10, f32[128,32,6,2,64,1]{0,1,3,5,4,2:T(8,128)} %copy.42, f32[1,64,2,32]{1,3,2,0:T(8,128)S(1)} %copy-done.5, f32[1,64,2,32]{1,3,2,0:T(8,128)S(1)} %get-tuple-element.11), kind=kOutput, calls=%fused_computation.2 | convolution fusion | flops 2434797568 | bytes 12632576 | tf_op jit(solution)/shard_map/cxqi,sitkqy->tskcxy/dot_general | solution.py:58
  326.8 0.1 copy.37
  326.9 0.7 mul.233
  (34 shorter events, 0.1 us)
Async XLA Ops:
  6.5 1.0 copy-start
  6.5 192.4 %copy-start.3 = (bf16[256,2048]{1,0:T(8,128)(2,1)S(1)}, bf16[256,2048]{1,0:T(8,128)(2,1)}, u32[]{:S(2)}) copy-start(bf16[256,2048]{1,0:T(8,128)(2,1)} %param.8) | copy-start | bytes 3145732
  6.5 192.4 %copy-start.6 = (f32[2048]{0:T(1024)S(1)}, f32[2048]{0:T(1024)}, u32[]{:S(2)}) copy-start(f32[2048]{0:T(1024)} %param.9) | copy-start | bytes 24580
  6.5 187.0 %all-gather.2.cloned.1.call-start = ((), (), s32[]{:S(2)}) async-start(), calls=%async_computation | async-start | bytes 14868480 | tf_op jit(solution)/shard_map/all_gather | solution.py:92
  193.6 22.1 %collective-permute-start.3 = (bf16[2560,2816]{1,0:T(8,128)(2,1)}, bf16[2560,2816]{1,0:T(8,128)(2,1)}, u32[]{:S(2)}, u32[]{:S(2)}) collective-permute-start(bf16[2560,2816]{1,0:T(8,128)(2,1)} %all-gather.2.cloned.1.call-done), channel_id=1, source_target_pairs={{0,1},{1,0},{2,3},{3,2},{4,5},{5,4},{6,7},{7,6},{8,9},{9,8},{10,11... | collective-permute-start | bytes 43253768 | tf_op jit(solution)/shard_map/ppermute | solution.py:93
  193.6 49.0 %collective-permute-start = (bf16[2048,192]{0,1:T(8,128)(2,1)}, bf16[2048,192]{0,1:T(8,128)(2,1)}, u32[]{:S(2)}, u32[]{:S(2)}) collective-permute-start(bf16[2048,192]{0,1:T(8,128)(2,1)} %param.12), channel_id=1, source_target_pairs={{0,1},{1,0},{2,3},{3,2},{4,5},{5,4},{6,7},{7,6},{8,9},{9,8},{10,11... | collective-permute-start | bytes 2359304 | tf_op jit(solution)/shard_map/ppermute | solution.py:95
  194.1 48.5 %collective-permute-start.1 = (bf16[2048,192]{0,1:T(8,128)(2,1)}, bf16[2048,192]{0,1:T(8,128)(2,1)}, u32[]{:S(2)}, u32[]{:S(2)}) collective-permute-start(bf16[2048,192]{0,1:T(8,128)(2,1)} %param.12), channel_id=1, source_target_pairs={{0,2},{1,3},{2,0},{3,1},{4,6},{5,7},{6,4},{7,5},{8,10},{9,11},{10,... | collective-permute-start | bytes 2359304 | tf_op jit(solution)/shard_map/ppermute | solution.py:95
  197.5 45.1 %collective-permute-start.2 = (bf16[2048,192]{0,1:T(8,128)(2,1)}, bf16[2048,192]{0,1:T(8,128)(2,1)}, u32[]{:S(2)}, u32[]{:S(2)}) collective-permute-start(bf16[2048,192]{0,1:T(8,128)(2,1)} %param.12), channel_id=1, source_target_pairs={{0,3},{1,2},{2,1},{3,0},{4,7},{5,6},{6,5},{7,4},{8,11},{9,10},{10,... | collective-permute-start | bytes 2359304 | tf_op jit(solution)/shard_map/ppermute | solution.py:95
  199.9 0.7 copy-start.9
  199.9 1.8 copy-start.7
  234.6 8.0 %copy-start.4 = (bf16[256,2048]{1,0:T(8,128)(2,1)S(1)}, bf16[256,2048]{1,0:T(8,128)(2,1)}, u32[]{:S(2)}) copy-start(bf16[256,2048]{1,0:T(8,128)(2,1)} %param.8) | copy-start | bytes 3145732
  234.6 8.0 %copy-start.8 = (bf16[2048,192]{0,1:T(8,128)(2,1)S(1)}, bf16[2048,192]{0,1:T(8,128)(2,1)}, u32[]{:S(2)}) copy-start(bf16[2048,192]{0,1:T(8,128)(2,1)} %param.12) | copy-start | bytes 2359300
  263.8 6.5 %copy-start.2 = (pred[128,32,128]{2,1,0:T(8,128)(4,1)S(1)}, pred[128,32,128]{2,1,0:T(8,128)(4,1)}, u32[]{:S(2)}) copy-start(pred[128,32,128]{2,1,0:T(8,128)(4,1)} %fusion.31) | copy-start | bytes 1572868
  284.9 22.9 %copy-start.5 = (f32[1,64,2,32]{1,3,2,0:T(8,128)S(1)}, f32[1,64,2,32]{1,3,2,0:T(8,128)}, u32[]{:S(2)}) copy-start(f32[1,64,2,32]{1,3,2,0:T(8,128)} %get-tuple-element.12) | copy-start | bytes 49156
  284.9 22.9 %copy-start.10 = (f32[128]{0:T(128)S(1)}, f32[128]{0:T(128)}, u32[]{:S(2)}) copy-start(f32[128]{0:T(128)} %param.15) | copy-start | bytes 1540
  307.8 19.8 %copy-start.1 = (bf16[88,2048]{1,0:T(8,128)(2,1)S(1)}, bf16[88,2048]{1,0:T(8,128)(2,1)}, u32[]{:S(2)}) copy-start(bf16[88,2048]{1,0:T(8,128)(2,1)} %param.11) | copy-start | bytes 1081348
Sparse Core Ops, SparseCore 0:
  9.5 184.0 all-gather.1

commit v3 on v2

--- a/solution.py
+++ b/solution.py
@@ -1,8 +1,11 @@
+import functools
 import math
 
 import jax
 import jax.numpy as jnp
 from jax import lax
+from jax.experimental import pallas as pl
+from jax.experimental.pallas import tpu as pltpu
 from jax.sharding import PartitionSpec as P
 
 GRID = 16
@@ -29,16 +32,50 @@
     y = jnp.arange(PIX, dtype=jnp.int32)
     ang = jnp.mod(v[:, None] * y[None, :], PIX).astype(f32) * turn
     cv, sv = jnp.cos(ang), jnp.sin(ang)
-    t1 = jnp.stack([jnp.concatenate([cv, sv], 1), jnp.concatenate([-sv, cv], 1)], 0)
+    t1 = jnp.concatenate([jnp.concatenate([cv, sv], 1), jnp.concatenate([-sv, cv], 1)], 0)
     i = jnp.arange(W, dtype=jnp.int32)
     x = jnp.arange(PIX, dtype=jnp.int32)
     ang2 = jnp.mod(x[:, None] * i[None, :], PIX).astype(f32) * turn
-    ca, sa = jnp.cos(ang2), jnp.sin(ang2)
-    t2 = jnp.stack([jnp.stack([ca, -sa], 1), jnp.stack([sa, ca], 1)], 0)
+    t2 = jnp.concatenate([jnp.cos(ang2), jnp.sin(ang2)], 0)
     return t1, t2
 
 
-def imaging(spec, source_index, source_cutoff, source_weight):
+def power_kernel(w_ref, wm_ref, t1_ref, t2_ref, out_ref, rcat, *, sb):
+    step = pl.program_id(0)
+    blocks = sb * 6
+    x = wm_ref[...].reshape(blocks * W, 2 * ORD)
+    y = jnp.dot(x, t1_ref[...], preferred_element_type=f32)
+    h = y[:, : 2 * PIX] + y[:, 2 * PIX:]
+    hh = h.astype(bf16)
+    hl = (h - hh.astype(f32)).astype(bf16)
+    rcat[3 * W:, :] = jnp.zeros((W, blocks * 2 * PIX), bf16)
+    for n in range(blocks):
+        cols = slice(n * 2 * PIX, (n + 1) * 2 * PIX)
+        rows = slice(n * W, (n + 1) * W)
+        rcat[0:W, cols] = hh[rows, :]
+        rcat[W:2 * W, cols] = hl[rows, :]
+        rcat[2 * W:3 * W, cols] = hh[rows, :]
+    q = jnp.dot(t2_ref[...], rcat[...], preferred_element_type=f32)
+    acc = jnp.zeros((PIX, 2 * PIX), f32)
+    for j in range(sb):
+        part = jnp.zeros((PIX, 2 * PIX), f32)
+        for k in range(6):
+            n = j * 6 + k
+            blk = q[:, n * 2 * PIX:(n + 1) * 2 * PIX]
+            rolled = pltpu.roll(blk, PIX, 1)
+            er = blk[:PIX] - rolled[PIX:]
+            ei = blk[PIX:] + rolled[:PIX]
+            part = part + er * er + ei * ei
+        acc = acc + w_ref[step * sb + j] * part
+
+    @pl.when(step == 0)
+    def _():
+        out_ref[...] = jnp.zeros_like(out_ref)
+
+    out_ref[...] += acc
+
+
+def imaging(spec, source_index, source_cutoff, source_weight, sb=8):
     T = spec.shape[0]
     S = source_index.shape[0]
     x0 = jnp.clip(source_index[:, 0], 0, ORD - W)
@@ -46,17 +83,34 @@
     rows = x0[:, None] + jnp.arange(W, dtype=jnp.int32)[None, :]
     pick = (rows[:, :, None] == jnp.arange(ORD, dtype=jnp.int32)[None, None, :]).astype(bf16)
     spec_rows = spec.reshape(T, 6, 2, ORD, ORD)
-    strips = jnp.einsum("siu,tkpuv->sitkpv", pick, spec_rows, preferred_element_type=f32).astype(bf16)
+    strips = jnp.einsum("siu,tkpuv->tskipv", pick, spec_rows, preferred_element_type=f32)
     i = jnp.arange(W, dtype=jnp.int32)
     j = jnp.arange(ORD, dtype=jnp.int32)[None, :] - y0[:, None]
     dist = (i[None, :, None] - W // 2) ** 2 + (j[:, None, :] - W // 2) ** 2
     keep = (dist <= (source_cutoff * source_cutoff)[:, None, None]) & (j[:, None, :] >= 0) & (j[:, None, :] < W)
-    masked = jnp.where(keep[:, :, None, None, None, :], strips, jnp.zeros((), bf16))
+    masked = jnp.where(keep[None, :, None, :, None, :], strips, 0.0).astype(bf16)
+    masked = masked.reshape(T, S, 6, W, 2 * ORD)
     t1, t2 = phase_tables()
-    half = jnp.einsum("sitkpv,pvn->sitkn", masked.astype(f32), t1, precision=lax.Precision.HIGH)
-    half = half.reshape(S, W, T, 6, 2, PIX)
-    field = jnp.einsum("cxqi,sitkqy->tskcxy", t2, half, precision=lax.Precision.HIGH)
-    power = jnp.sum(field * field * source_weight[None, :, None, None, None, None], axis=(1, 2, 3))
+    t1h, t1l = split_bf16(t1)
+    t1s = jnp.concatenate([t1h, t1l], 1)
+    t2h, t2l = split_bf16(t2)
+    t2c = jnp.concatenate([t2h, t2h, t2l, jnp.zeros((2 * PIX, W), bf16)], 1)
+    call = pl.pallas_call(
+        functools.partial(power_kernel, sb=sb),
+        out_shape=jax.ShapeDtypeStruct((PIX, 2 * PIX), f32),
+        grid=(S // sb,),
+        in_specs=[
+            pl.BlockSpec(memory_space=pltpu.SMEM),
+            pl.BlockSpec((sb, 6, W, 2 * ORD), lambda s: (s, 0, 0, 0)),
+            pl.BlockSpec((2 * ORD, 4 * PIX), lambda s: (0, 0)),
+            pl.BlockSpec((2 * PIX, 4 * W), lambda s: (0, 0)),
+        ],
+        out_specs=pl.BlockSpec((PIX, 2 * PIX), lambda s: (0, 0)),
+        scratch_shapes=[pltpu.VMEM((4 * W, sb * 6 * 2 * PIX), bf16)],
+        compiler_params=pltpu.CompilerParams(dimension_semantics=("arbitrary",)),
+    )
+    outs = [call(source_weight.astype(f32), masked[t], t1s, t2c)[:, :PIX] for t in range(T)]
+    power = jnp.stack(outs, 0)
     return power.reshape(T, PIX * PIX) * (1.0 / (6.0 * W * W * S))
 
 

time: 336 us -> 356 us (1.060)
  matrix products: 75.9 us -> 42.3 us
  local copies, waits for them, and re-layouts: 45.7 us -> 75.1 us
  Pallas kernels: 0 us -> 22.2 us
    dot_general x3 -> x1, matrix products: 40.2 us -> 6.59 us  [imaging(): jnp.einsum('siu,tkpuv->tskipv', pick, spec_rows, preferred_element_type=f32)]
    convert_element_type x0 -> x1, local copies, waits for them, and re-layouts: none -> 31.6 us  [imaging(): jnp.where(keep[None, :, None, :, None, :], strips, 0.0).astype(bf16)]
    dot_general x1 -> x0, local copies, waits for them, and re-layouts: 22.9 us -> none  [imaging(): jnp.einsum('sitkpv,pvn->sitkn', masked.astype(f32), t1, precision=lax.Pre...]
    pallas_call x0 -> x1, Pallas kernels: none -> 22.2 us  [imaging(): call(source_weight.astype(f32), masked[t], t1s, t2c)[:, :PIX]]
    another operation x1 -> x2, local copies, waits for them, and re-layouts: 8.2 us -> 28.8 us  [the longest x1 20.5 us: imaging(): masked[t]]
where the time goes in v3:
time: 356 us; the launch traced here: 353 us
  waiting for transfers between devices  188 us (53%)
  local copies, waits for them, and re-layouts  75.1 us (21%)
  matrix products  42.3 us (12%)
  Pallas kernels  22.2 us (6%)
  between operations  13.8 us (4%)
  other arithmetic  7.91 us (2%)
  starting transfers between devices  3.89 us (1%)
    all_gather x1, waiting for transfers between devices, local(): gathered = lax.all_gather(packed, 'tile', axis=0, tiled=True)  184 us
    convert_element_type x1, local copies, waits for them, and re-layouts, imaging(): jnp.where(keep[None, :, None, :, None, :], strips, 0.0).astype(bf16)  31.6 us
    pallas_call x1, Pallas kernels, imaging(): call(source_weight.astype(f32), masked[t], t1s, t2c)[:, :PIX]  22.2 us
    another operation x1, local copies, waits for them, and re-layouts, imaging(): masked[t]  20.5 us
    dot_general x1, matrix products, local(): jnp.dot(normed_other, sibling, preferred_element_type=jnp.float32)  9.91 us
    another operation x2, local copies, waits for them, and re-layouts, local(): coeffs.reshape(tile_count, GRID, GRID, 12, SUB, SUB)  8.82 us
    another operation x1, local copies, waits for them, and re-layouts  8.26 us
    dot_general x1, matrix products, local(): jnp.dot(hidden_other, sibling, preferred_element_type=jnp.float32)  7.92 us
  transfers between devices with their start and end apart: 5, of which 2 were waited for; matrix products, arithmetic and copies ran while one was open for 12% of the time, Pallas kernels for 0%

profile of v3, /device:TPU:0, one launch (start us, length us, event | category | flops | bytes accessed | tf_op | source)
XLA Modules:
  0.0 353.1 jit_solution(7154965734868750414)
XLA Ops:
  6.6 1.0 copy-done
  7.5 0.1 constant_dynamic-slice_fusion
  7.6 0.9 constant_dynamic-slice_fusion.1
  8.5 0.8 fusion.35
  9.3 0.0 all-gather.2.cloned.1.call-update
  9.4 184.2 %all-gather.2.cloned.1.call-done = bf16[2560,2816]{1,0:T(8,128)(2,1)} async-done(((bf16[80,2816]{1,0:T(8,128)(2,1)}), bf16[2560,2816]{1,0:T(8,128)(2,1)}) %all-gather.2.cloned.1.call-update) | async-done | bytes 14417936 | tf_op jit(solution)/shard_map/all_gather | solution.py:146
  193.6 0.5 collective-permute-start
  194.1 3.4 collective-permute-start.1
  197.5 1.5 fusion.17
  199.0 0.3 fusion.19
  199.3 0.5 copy.32
  199.9 0.1 dynamic-slice_bitcast_fusion.2
  200.0 0.1 pad.18
  200.1 0.1 pad.20
  200.2 0.4 copy-done.8
  200.6 0.1 fusion.55
  200.6 0.1 fusion.59
  200.7 0.1 copy.41
  200.8 0.1 copy.42
  200.9 0.1 pad.26.clone
  201.0 0.3 fusion.48
  201.3 0.3 fusion.46
  201.6 0.1 reduce-precision_convert_fusion
  201.7 0.7 pad_maximum_fusion.t1_ref
  202.5 0.7 maximum_maximum_fusion.1.t2_ref
  203.2 1.4 fusion.22
  204.6 7.5 %fusion.61 = f32[256,2816]{1,0:T(8,128)S(1)} fusion(bf16[256,2560]{0,1:T(8,128)(2,1)S(1)} %bitcast.64, bf16[2560,2816]{1,0:T(8,128)(2,1)} %all-gather.2.cloned.1.call-done), kind=kOutput, calls=%fused_computation.98 | convolution fusion | flops 3690987520 | bytes 18612224 | tf_op jit(solution)/shard_map/dot_general | solution.py:164
  212.1 3.6 %collective-permute-done.3 = bf16[2560,2816]{1,0:T(8,128)(2,1)} collective-permute-done((bf16[2560,2816]{1,0:T(8,128)(2,1)}, bf16[2560,2816]{1,0:T(8,128)(2,1)}, u32[]{:S(2)}, u32[]{:S(2)}) %collective-permute-start.3) | collective-permute-done | bytes 14417952 | tf_op jit(solution)/shard_map/ppermute | solution.py:147
  215.7 9.9 %fusion.16 = bf16[256,2816]{1,0:T(8,128)(2,1)S(1)} fusion(f32[256,2816]{1,0:T(8,128)S(1)} %fusion.61, bf16[256,2560]{0,1:T(8,128)(2,1)S(1)} %bitcast.68, bf16[2560,2816]{1,0:T(8,128)(2,1)} %collective-permute-done.3), kind=kOutput, calls=%fused_computation.23 | convolution fusion | flops 3698196480 | bytes 20054016 | tf_op jit(solution)/shard_map/dot_general | solution.py:164
  225.6 0.7 copy.33
  226.3 0.3 reshape.164
  226.7 0.1 dynamic-slice_bitcast_fusion.1
  226.8 0.1 pad.21.clone
  226.9 0.1 pad.22.clone
  227.0 7.6 %fusion.62 = f32[256,2816]{1,0:T(8,128)S(1)} fusion(bf16[256,2560]{0,1:T(8,128)(2,1)S(1)} %bitcast.65, bf16[2560,2816]{1,0:T(8,128)(2,1)} %all-gather.2.cloned.1.call-done), kind=kOutput, calls=%fused_computation.99 | convolution fusion | flops 3690987520 | bytes 18612224 | tf_op jit(solution)/shard_map/dot_general | solution.py:169
  234.6 7.9 %fusion.63 = f32[256,2816]{1,0:T(8,128)S(1)} fusion(bf16[256,2560]{0,1:T(8,128)(2,1)S(1)} %bitcast.66, bf16[2560,2816]{1,0:T(8,128)(2,1)} %collective-permute-done.3), kind=kOutput, calls=%fused_computation.100 | convolution fusion | flops 3690987520 | bytes 18612224 | tf_op jit(solution)/shard_map/dot_general | solution.py:169
  242.6 2.7 fusion.28
  245.3 0.6 gather_fusion
  245.9 0.9 select_bitcast_fusion
  246.8 3.5 reshape_reshape.4
  250.2 5.3 %copy.38 = bf16[1,16,16,12,8,8]{5,2,4,1,3,0:T(8,128)(2,1)} copy(bf16[1,16,16,12,8,8]{2,1,5,4,3,0:T(8,128)(2,1)S(1)} %reshape_reshape.4) | data formatting | bytes 786432 | tf_op jit(solution)/shard_map/reshape;reshape | solution.py:182
  255.6 8.3 %reshape.167 = bf16[6,2,128,128]{3,2,1,0:T(8,128)(2,1)S(1)} reshape(bf16[1,12,16,8,16,8]{5,4,3,2,1,0:T(8,128)(2,1)} %bitcast.63) | data formatting | bytes 786432 | tf_op jit(solution)/shard_map/reshape.2
  263.9 6.6 %fusion = bf16[1,128,6,32,2,128]{1,5,3,4,2,0:T(8,128)(2,1)} fusion(pred[128,32,128]{0,2,1:T(8,128)(4,1)S(1)} %copy-done.4, s32[128,32]{0,1:T(8,128)S(1)} %iota_add_fusion, bf16[6,2,128,128]{3,2,1,0:T(8,128)(2,1)S(1)} %reshape.167), kind=kOutput, calls=%fused_computation.2 | convolution fusion | flops 1623719936 | bytes 13516800 | tf_op jit(solution)/shard_map/siu,tkpuv->tskipv/dot_general | solution.py:86
  270.4 31.6 %copy.40 = bf16[1,128,6,32,2,128]{5,4,3,2,1,0:T(2,128)(2,1)} copy(bf16[1,128,6,32,2,128]{1,5,3,4,2,0:T(8,128)(2,1)} %fusion) | data formatting | bytes 25165824 | tf_op jit(solution)/shard_map/convert_element_type | solution.py:91
  302.0 20.5 %squeeze_reshape.3.wm_ref = bf16[128,6,32,256]{3,2,1,0:T(8,128)(2,1)} reshape(bf16[1,128,6,32,2,128]{5,4,3,2,1,0:T(2,128)(2,1)} %copy.40) | data formatting | bytes 25165824 | tf_op jit(solution)/shard_map/squeeze;reshape | solution.py:112
  322.6 22.2 %shard_map.82 = f32[64,128]{1,0:T(8,128)} custom-call(f32[128]{0:T(128)} %w_ref.1, bf16[128,6,32,256]{3,2,1,0:T(8,128)(2,1)} %squeeze_reshape.3.wm_ref, bf16[256,256]{1,0:T(8,128)(2,1)} %pad_maximum_fusion.t1_ref, bf16[128,128]{1,0:T(8,128)(2,1)} %maximum_maximum_fusion.1.t2_ref), custom_call_target="tpu_custom_call" | custom-call | tf_op jit(solution)/shard_map/pallas_call | solution.py:112
  344.8 0.8 slice_multiply_fusion
  345.6 0.7 mul.163
  (34 shorter events, 0.2 us)
Async XLA Ops:
  6.5 1.0 copy-start
  6.5 192.5 %copy-start.2 = (bf16[256,2048]{1,0:T(8,128)(2,1)S(1)}, bf16[256,2048]{1,0:T(8,128)(2,1)}, u32[]{:S(2)}) copy-start(bf16[256,2048]{1,0:T(8,128)(2,1)} %param.8) | copy-start | bytes 3145732
  6.5 192.5 %copy-start.5 = (f32[2048]{0:T(1024)S(1)}, f32[2048]{0:T(1024)}, u32[]{:S(2)}) copy-start(f32[2048]{0:T(1024)} %param.9) | copy-start | bytes 24580
  6.5 187.1 %all-gather.2.cloned.1.call-start = ((), (), s32[]{:S(2)}) async-start(), calls=%async_computation | async-start | bytes 14868480 | tf_op jit(solution)/shard_map/all_gather | solution.py:146
  193.6 22.1 %collective-permute-start.3 = (bf16[2560,2816]{1,0:T(8,128)(2,1)}, bf16[2560,2816]{1,0:T(8,128)(2,1)}, u32[]{:S(2)}, u32[]{:S(2)}) collective-permute-start(bf16[2560,2816]{1,0:T(8,128)(2,1)} %all-gather.2.cloned.1.call-done), channel_id=1, source_target_pairs={{0,1},{1,0},{2,3},{3,2},{4,5},{5,4},{6,7},{7,6},{8,9},{9,8},{10,11... | collective-permute-start | bytes 43253768 | tf_op jit(solution)/shard_map/ppermute | solution.py:147
  193.6 49.0 %collective-permute-start = (bf16[2048,192]{0,1:T(8,128)(2,1)}, bf16[2048,192]{0,1:T(8,128)(2,1)}, u32[]{:S(2)}, u32[]{:S(2)}) collective-permute-start(bf16[2048,192]{0,1:T(8,128)(2,1)} %param.12), channel_id=1, source_target_pairs={{0,1},{1,0},{2,3},{3,2},{4,5},{5,4},{6,7},{7,6},{8,9},{9,8},{10,11... | collective-permute-start | bytes 2359304 | tf_op jit(solution)/shard_map/ppermute | solution.py:149
  194.1 48.5 %collective-permute-start.1 = (bf16[2048,192]{0,1:T(8,128)(2,1)}, bf16[2048,192]{0,1:T(8,128)(2,1)}, u32[]{:S(2)}, u32[]{:S(2)}) collective-permute-start(bf16[2048,192]{0,1:T(8,128)(2,1)} %param.12), channel_id=1, source_target_pairs={{0,2},{1,3},{2,0},{3,1},{4,6},{5,7},{6,4},{7,5},{8,10},{9,11},{10,... | collective-permute-start | bytes 2359304 | tf_op jit(solution)/shard_map/ppermute | solution.py:149
  197.5 45.1 %collective-permute-start.2 = (bf16[2048,192]{0,1:T(8,128)(2,1)}, bf16[2048,192]{0,1:T(8,128)(2,1)}, u32[]{:S(2)}, u32[]{:S(2)}) collective-permute-start(bf16[2048,192]{0,1:T(8,128)(2,1)} %param.12), channel_id=1, source_target_pairs={{0,3},{1,2},{2,1},{3,0},{4,7},{5,6},{6,5},{7,4},{8,11},{9,10},{10,... | collective-permute-start | bytes 2359304 | tf_op jit(solution)/shard_map/ppermute | solution.py:149
  199.9 0.7 copy-start.8
  200.0 2.4 copy-start.6
  234.6 8.0 %copy-start.3 = (bf16[256,2048]{1,0:T(8,128)(2,1)S(1)}, bf16[256,2048]{1,0:T(8,128)(2,1)}, u32[]{:S(2)}) copy-start(bf16[256,2048]{1,0:T(8,128)(2,1)} %param.8) | copy-start | bytes 3145732
  234.6 8.0 %copy-start.7 = (bf16[2048,192]{0,1:T(8,128)(2,1)S(1)}, bf16[2048,192]{0,1:T(8,128)(2,1)}, u32[]{:S(2)}) copy-start(bf16[2048,192]{0,1:T(8,128)(2,1)} %param.12) | copy-start | bytes 2359300
  255.6 8.3 %copy-start.4 = (pred[128,32,128]{0,2,1:T(8,128)(4,1)S(1)}, pred[128,32,128]{0,2,1:T(8,128)(4,1)}, u32[]{:S(2)}) copy-start(pred[128,32,128]{0,2,1:T(8,128)(4,1)} %fusion.22) | copy-start | bytes 1572868
  322.6 23.7 %copy-start.1 = (bf16[88,2048]{1,0:T(8,128)(2,1)S(1)}, bf16[88,2048]{1,0:T(8,128)(2,1)}, u32[]{:S(2)}) copy-start(bf16[88,2048]{1,0:T(8,128)(2,1)} %param.11) | copy-start | bytes 1081348
Sparse Core Ops, SparseCore 0:
  9.5 184.0 all-gather.1

commit v4 on v3

--- a/solution.py
+++ b/solution.py
@@ -40,27 +40,29 @@
     return t1, t2
 
 
-def power_kernel(w_ref, wm_ref, t1_ref, t2_ref, out_ref, rcat, *, sb):
+def power_kernel(w_ref, *refs, sb):
+    wm_refs, (t1_ref, t2_ref, out_ref, rcat) = refs[:6], refs[6:]
     step = pl.program_id(0)
-    blocks = sb * 6
-    x = wm_ref[...].reshape(blocks * W, 2 * ORD)
-    y = jnp.dot(x, t1_ref[...], preferred_element_type=f32)
-    h = y[:, : 2 * PIX] + y[:, 2 * PIX:]
-    hh = h.astype(bf16)
-    hl = (h - hh.astype(f32)).astype(bf16)
-    rcat[3 * W:, :] = jnp.zeros((W, blocks * 2 * PIX), bf16)
-    for n in range(blocks):
-        cols = slice(n * 2 * PIX, (n + 1) * 2 * PIX)
-        rows = slice(n * W, (n + 1) * W)
-        rcat[0:W, cols] = hh[rows, :]
-        rcat[W:2 * W, cols] = hl[rows, :]
-        rcat[2 * W:3 * W, cols] = hh[rows, :]
+    rcat[3 * W:, :] = jnp.zeros((W, sb * 6 * 2 * PIX), bf16)
+    for k in range(6):
+        x = wm_refs[k][...].reshape(sb * W, 2 * ORD)
+        y = jnp.dot(x, t1_ref[...], preferred_element_type=f32)
+        h = y[:, : 2 * PIX] + y[:, 2 * PIX:]
+        hh = h.astype(bf16)
+        hl = (h - hh.astype(f32)).astype(bf16)
+        for j in range(sb):
+            n = k * sb + j
+            cols = slice(n * 2 * PIX, (n + 1) * 2 * PIX)
+            rows = slice(j * W, (j + 1) * W)
+            rcat[0:W, cols] = hh[rows, :]
+            rcat[W:2 * W, cols] = hl[rows, :]
+            rcat[2 * W:3 * W, cols] = hh[rows, :]
     q = jnp.dot(t2_ref[...], rcat[...], preferred_element_type=f32)
     acc = jnp.zeros((PIX, 2 * PIX), f32)
     for j in range(sb):
         part = jnp.zeros((PIX, 2 * PIX), f32)
         for k in range(6):
-            n = j * 6 + k
+            n = k * sb + j
             blk = q[:, n * 2 * PIX:(n + 1) * 2 * PIX]
             rolled = pltpu.roll(blk, PIX, 1)
             er = blk[:PIX] - rolled[PIX:]
@@ -82,26 +84,25 @@
     y0 = jnp.clip(source_index[:, 1], 0, ORD - W)
     rows = x0[:, None] + jnp.arange(W, dtype=jnp.int32)[None, :]
     pick = (rows[:, :, None] == jnp.arange(ORD, dtype=jnp.int32)[None, None, :]).astype(bf16)
-    spec_rows = spec.reshape(T, 6, 2, ORD, ORD)
-    strips = jnp.einsum("siu,tkpuv->tskipv", pick, spec_rows, preferred_element_type=f32)
+    spec_rows = spec.reshape(T, 6, 2, ORD, ORD).transpose(0, 1, 3, 2, 4).reshape(T, 6, ORD, 2 * ORD)
     i = jnp.arange(W, dtype=jnp.int32)
     j = jnp.arange(ORD, dtype=jnp.int32)[None, :] - y0[:, None]
     dist = (i[None, :, None] - W // 2) ** 2 + (j[:, None, :] - W // 2) ** 2
     keep = (dist <= (source_cutoff * source_cutoff)[:, None, None]) & (j[:, None, :] >= 0) & (j[:, None, :] < W)
-    masked = jnp.where(keep[None, :, None, :, None, :], strips, 0.0).astype(bf16)
-    masked = masked.reshape(T, S, 6, W, 2 * ORD)
+    keep = jnp.concatenate([keep, keep], 2)
     t1, t2 = phase_tables()
     t1h, t1l = split_bf16(t1)
     t1s = jnp.concatenate([t1h, t1l], 1)
     t2h, t2l = split_bf16(t2)
     t2c = jnp.concatenate([t2h, t2h, t2l, jnp.zeros((2 * PIX, W), bf16)], 1)
+    block = pl.BlockSpec((sb, W, 2 * ORD), lambda s: (s, 0, 0))
     call = pl.pallas_call(
         functools.partial(power_kernel, sb=sb),
         out_shape=jax.ShapeDtypeStruct((PIX, 2 * PIX), f32),
         grid=(S // sb,),
-        in_specs=[
-            pl.BlockSpec(memory_space=pltpu.SMEM),
-            pl.BlockSpec((sb, 6, W, 2 * ORD), lambda s: (s, 0, 0, 0)),
+        in_specs=[pl.BlockSpec(memory_space=pltpu.SMEM)]
+        + [block] * 6
+        + [
             pl.BlockSpec((2 * ORD, 4 * PIX), lambda s: (0, 0)),
             pl.BlockSpec((2 * PIX, 4 * W), lambda s: (0, 0)),
         ],
@@ -109,7 +110,13 @@
         scratch_shapes=[pltpu.VMEM((4 * W, sb * 6 * 2 * PIX), bf16)],
         compiler_params=pltpu.CompilerParams(dimension_semantics=("arbitrary",)),
     )
-    outs = [call(source_weight.astype(f32), masked[t], t1s, t2c)[:, :PIX] for t in range(T)]
+    outs = []
+    for t in range(T):
+        parts = []
+        for k in range(6):
+            strips = jnp.einsum("siu,un->sin", pick, spec_rows[t, k], preferred_element_type=f32)
+            parts.append(jnp.where(keep, strips, 0.0).astype(bf16))
+        outs.append(call(source_weight.astype(f32), *parts, t1s, t2c)[:, :PIX])
     power = jnp.stack(outs, 0)
     return power.reshape(T, PIX * PIX) * (1.0 / (6.0 * W * W * S))
 

time: 356 us -> 314 us (0.88)
  local copies, waits for them, and re-layouts: 75.1 us -> 23.1 us
  matrix products: 42.3 us -> 51.7 us
    convert_element_type x1 -> x0, local copies, waits for them, and re-layouts: 31.6 us -> none  [imaging(): jnp.where(keep[None, :, None, :, None, :], strips, 0.0).astype(bf16)]
    another operation x2 -> x1, local copies, waits for them, and re-layouts: 28.8 us -> 8.29 us  [imaging(): spec.reshape(T, 6, 2, ORD, ORD).transpose(0, 1, 3, 2, 4)]
    dot_general x1 -> x6, matrix products: 6.59 us -> 16 us  [imaging(): jnp.einsum('siu,un->sin', pick, spec_rows[t, k], preferred_element_type=f32)]
  transfers between devices with their start and end apart: 5 -> 5, of which waited for: 2 -> 2; matrix products, arithmetic and copies ran while one was open for 12% -> 14% of each run, Pallas kernels for 0% -> 0%
where the time goes in v4:
time: 314 us; the launch traced here: 313 us
  waiting for transfers between devices  185 us (59%)
  matrix products  51.7 us (16%)
  Pallas kernels  24.4 us (8%)
  local copies, waits for them, and re-layouts  23.1 us (7%)
  between operations  13.8 us (4%)
  other arithmetic  10.4 us (3%)
  starting transfers between devices  3.89 us (1%)
    all_gather x1, waiting for transfers between devices, local(): gathered = lax.all_gather(packed, 'tile', axis=0, tiled=True)  184 us
    pallas_call x1, Pallas kernels, imaging(): outs.append(call(source_weight.astype(f32), *parts, t1s, t2c)[:, :PIX])  24.4 us
    dot_general x6, matrix products, imaging(): jnp.einsum('siu,un->sin', pick, spec_rows[t, k], preferred_element_type=f32)  16 us
    dot_general x1, matrix products, local(): jnp.dot(normed_other, sibling, preferred_element_type=jnp.float32)  9.91 us
    another operation x2, local copies, waits for them, and re-layouts, local(): coeffs.reshape(tile_count, GRID, GRID, 12, SUB, SUB)  8.8 us
    another operation x1, local copies, waits for them, and re-layouts, imaging(): spec.reshape(T, 6, 2, ORD, ORD).transpose(0, 1, 3, 2, 4)  8.29 us
    dot_general x1, matrix products, local(): jnp.dot(hidden_other, sibling, preferred_element_type=jnp.float32)  7.93 us
    dot_general x1, matrix products, local(): jnp.dot(hidden_mine, gathered, preferred_element_type=jnp.float32)  7.64 us
  transfers between devices with their start and end apart: 5, of which 2 were waited for; matrix products, arithmetic and copies ran while one was open for 14% of the time, Pallas kernels for 0%

profile of v4, /device:TPU:0, one launch (start us, length us, event | category | flops | bytes accessed | tf_op | source)
XLA Modules:
  0.0 312.7 jit_solution(8263556047247393240)
XLA Ops:
  6.6 1.0 copy-done
  7.6 0.9 constant_dynamic-slice_fusion.1
  8.5 0.8 fusion.31
  9.4 184.2 %all-gather.2.cloned.1.call-done = bf16[2560,2816]{1,0:T(8,128)(2,1)} async-done(((bf16[80,2816]{1,0:T(8,128)(2,1)}), bf16[2560,2816]{1,0:T(8,128)(2,1)}) %all-gather.2.cloned.1.call-update) | async-done | bytes 14417936 | tf_op jit(solution)/shard_map/all_gather | solution.py:153
  193.6 0.5 collective-permute-start
  194.1 3.4 %collective-permute-start.1 = (bf16[2048,192]{0,1:T(8,128)(2,1)}, bf16[2048,192]{0,1:T(8,128)(2,1)}, u32[]{:S(2)}, u32[]{:S(2)}) collective-permute-start(bf16[2048,192]{0,1:T(8,128)(2,1)} %param.12), channel_id=1, source_target_pairs={{0,2},{1,3},{2,0},{3,1},{4,6},{5,7},{6,4},{7,5},{8,10},{9,11},{10,... | collective-permute-start | bytes 2359304 | tf_op jit(solution)/shard_map/ppermute | solution.py:156
  197.5 1.5 fusion.16
  199.0 0.3 fusion.18
  199.3 0.5 copy.46
  200.0 0.1 pad.18
  200.1 0.1 pad.20
  200.2 0.4 copy-done.9
  200.5 0.1 fusion.50
  200.7 0.1 copy.60
  200.8 0.1 copy.61
  201.0 0.3 fusion.43
  201.3 0.3 fusion.41
  201.6 0.1 reduce-precision_convert_fusion
  201.7 0.7 pad_maximum_fusion.refs_6_
  202.4 0.1 fusion.39
  202.5 0.7 maximum_maximum_fusion.1.refs_7_
  203.3 1.4 iota_compare_fusion
  204.7 2.4 fusion.21
  207.1 7.5 %fusion.62 = f32[256,2816]{1,0:T(8,128)S(1)} fusion(bf16[256,2560]{0,1:T(8,128)(2,1)S(1)} %bitcast.84, bf16[2560,2816]{1,0:T(8,128)(2,1)} %all-gather.2.cloned.1.call-done), kind=kOutput, calls=%fused_computation.113 | convolution fusion | flops 3690987520 | bytes 18612224 | tf_op jit(solution)/shard_map/dot_general | solution.py:171
  214.6 1.1 collective-permute-done.3
  215.7 9.9 %fusion.15 = bf16[256,2816]{1,0:T(8,128)(2,1)S(1)} fusion(f32[256,2816]{1,0:T(8,128)S(1)} %fusion.62, bf16[256,2560]{0,1:T(8,128)(2,1)S(1)} %bitcast.88, bf16[2560,2816]{1,0:T(8,128)(2,1)} %collective-permute-done.3), kind=kOutput, calls=%fused_computation.28 | convolution fusion | flops 3698196480 | bytes 20054016 | tf_op jit(solution)/shard_map/dot_general | solution.py:171
  225.6 0.7 copy.47
  226.3 0.3 reshape.156
  226.6 0.1 dynamic-slice_bitcast_fusion.1
  226.8 0.1 pad.21.clone
  226.9 0.1 pad.22.clone
  227.0 7.6 %fusion.63 = f32[256,2816]{1,0:T(8,128)S(1)} fusion(bf16[256,2560]{0,1:T(8,128)(2,1)S(1)} %bitcast.85, bf16[2560,2816]{1,0:T(8,128)(2,1)} %all-gather.2.cloned.1.call-done), kind=kOutput, calls=%fused_computation.114 | convolution fusion | flops 3690987520 | bytes 18612224 | tf_op jit(solution)/shard_map/dot_general | solution.py:176
  234.6 7.9 %fusion.64 = f32[256,2816]{1,0:T(8,128)S(1)} fusion(bf16[256,2560]{0,1:T(8,128)(2,1)S(1)} %bitcast.86, bf16[2560,2816]{1,0:T(8,128)(2,1)} %collective-permute-done.3), kind=kOutput, calls=%fused_computation.115 | convolution fusion | flops 3690987520 | bytes 18612224 | tf_op jit(solution)/shard_map/dot_general | solution.py:176
  242.6 2.7 fusion.25
  245.3 0.6 gather_fusion
  245.9 0.9 select_bitcast_fusion
  246.7 3.5 %reshape_reshape.6 = bf16[1,16,16,12,8,8]{2,1,5,4,3,0:T(8,128)(2,1)S(1)} reshape(bf16[256,4,192]{0,2,1:T(8,128)(2,1)} %select_bitcast_fusion) | data formatting | bytes 786432 | tf_op jit(solution)/shard_map/reshape;reshape | solution.py:189
  250.2 5.3 %copy.52 = bf16[1,16,16,12,8,8]{5,2,4,1,3,0:T(8,128)(2,1)} copy(bf16[1,16,16,12,8,8]{2,1,5,4,3,0:T(8,128)(2,1)S(1)} %reshape_reshape.6) | data formatting | bytes 786432 | tf_op jit(solution)/shard_map/reshape;reshape | solution.py:189
  255.5 8.3 %reshape_reshape.7 = bf16[1,6,2,128,128]{4,3,2,1,0:T(8,128)(2,1)S(1)} reshape(bf16[1,12,16,8,16,8]{5,4,3,2,1,0:T(8,128)(2,1)} %bitcast.83) | data formatting | bytes 786432 | tf_op jit(solution)/shard_map/reshape;reshape | solution.py:87
  263.9 2.7 select_convert_fusion.refs_5_
  266.6 2.7 select_convert_fusion.1.refs_4_
  269.3 2.7 select_convert_fusion.2.refs_3_
  272.0 2.7 select_convert_fusion.3.refs_2_
  274.7 2.6 select_convert_fusion.4.refs_1_
  277.3 2.6 select_convert_fusion.5.refs_0_
  280.0 24.4 %shard_map.82 = f32[64,128]{1,0:T(8,128)} custom-call(f32[128]{0:T(128)} %w_ref.1, bf16[128,32,256]{2,1,0:T(8,128)(2,1)} %select_convert_fusion.5.refs_0_, bf16[128,32,256]{2,1,0:T(8,128)(2,1)} %select_convert_fusion.4.refs_1_, bf16[128,32,256]{2,1,0:T(8,128)(2,1)} %select_convert_fusion.3.refs_2_, bf16[128,32,256]{2,1,0:T(8,128)(2,1)} %select_convert_fusion.2.refs_3_, ...), custom_call_target="tpu_custom_call" | custom-call | tf_op jit(solution)/shard_map/pallas_call | solution.py:119
  304.4 0.8 slice_multiply_fusion
  305.2 0.7 mul.163
  (41 shorter events, 0.6 us)
Async XLA Ops:
  6.5 1.0 copy-start
  6.5 192.5 %copy-start.2 = (bf16[256,2048]{1,0:T(8,128)(2,1)S(1)}, bf16[256,2048]{1,0:T(8,128)(2,1)}, u32[]{:S(2)}) copy-start(bf16[256,2048]{1,0:T(8,128)(2,1)} %param.8) | copy-start | bytes 3145732
  6.5 192.5 %copy-start.6 = (f32[2048]{0:T(1024)S(1)}, f32[2048]{0:T(1024)}, u32[]{:S(2)}) copy-start(f32[2048]{0:T(1024)} %param.9) | copy-start | bytes 24580
  6.5 187.0 %all-gather.2.cloned.1.call-start = ((), (), s32[]{:S(2)}) async-start(), calls=%async_computation | async-start | bytes 14868480 | tf_op jit(solution)/shard_map/all_gather | solution.py:153
  193.6 22.1 %collective-permute-start.3 = (bf16[2560,2816]{1,0:T(8,128)(2,1)}, bf16[2560,2816]{1,0:T(8,128)(2,1)}, u32[]{:S(2)}, u32[]{:S(2)}) collective-permute-start(bf16[2560,2816]{1,0:T(8,128)(2,1)} %all-gather.2.cloned.1.call-done), channel_id=1, source_target_pairs={{0,1},{1,0},{2,3},{3,2},{4,5},{5,4},{6,7},{7,6},{8,9},{9,8},{10,11... | collective-permute-start | bytes 43253768 | tf_op jit(solution)/shard_map/ppermute | solution.py:154
  193.6 49.0 %collective-permute-start = (bf16[2048,192]{0,1:T(8,128)(2,1)}, bf16[2048,192]{0,1:T(8,128)(2,1)}, u32[]{:S(2)}, u32[]{:S(2)}) collective-permute-start(bf16[2048,192]{0,1:T(8,128)(2,1)} %param.12), channel_id=1, source_target_pairs={{0,1},{1,0},{2,3},{3,2},{4,5},{5,4},{6,7},{7,6},{8,9},{9,8},{10,11... | collective-permute-start | bytes 2359304 | tf_op jit(solution)/shard_map/ppermute | solution.py:156
  194.1 48.5 %collective-permute-start.1 = (bf16[2048,192]{0,1:T(8,128)(2,1)}, bf16[2048,192]{0,1:T(8,128)(2,1)}, u32[]{:S(2)}, u32[]{:S(2)}) collective-permute-start(bf16[2048,192]{0,1:T(8,128)(2,1)} %param.12), channel_id=1, source_target_pairs={{0,2},{1,3},{2,0},{3,1},{4,6},{5,7},{6,4},{7,5},{8,10},{9,11},{10,... | collective-permute-start | bytes 2359304 | tf_op jit(solution)/shard_map/ppermute | solution.py:156
  197.5 45.1 %collective-permute-start.2 = (bf16[2048,192]{0,1:T(8,128)(2,1)}, bf16[2048,192]{0,1:T(8,128)(2,1)}, u32[]{:S(2)}, u32[]{:S(2)}) collective-permute-start(bf16[2048,192]{0,1:T(8,128)(2,1)} %param.12), channel_id=1, source_target_pairs={{0,3},{1,2},{2,1},{3,0},{4,7},{5,6},{6,5},{7,4},{8,11},{9,10},{10,... | collective-permute-start | bytes 2359304 | tf_op jit(solution)/shard_map/ppermute | solution.py:156
  199.9 0.7 copy-start.9
  200.0 2.4 copy-start.7
  234.6 8.0 %copy-start.3 = (bf16[256,2048]{1,0:T(8,128)(2,1)S(1)}, bf16[256,2048]{1,0:T(8,128)(2,1)}, u32[]{:S(2)}) copy-start(bf16[256,2048]{1,0:T(8,128)(2,1)} %param.8) | copy-start | bytes 3145732
  234.6 8.0 %copy-start.8 = (bf16[2048,192]{0,1:T(8,128)(2,1)S(1)}, bf16[2048,192]{0,1:T(8,128)(2,1)}, u32[]{:S(2)}) copy-start(bf16[2048,192]{0,1:T(8,128)(2,1)} %param.12) | copy-start | bytes 2359300
  255.5 8.4 %copy-start.4 = (pred[128,32,128]{2,1,0:T(32,128)(4,1)S(1)}, pred[128,32,128]{2,1,0:T(32,128)(4,1)}, u32[]{:S(2)}) copy-start(pred[128,32,128]{2,1,0:T(32,128)(4,1)} %fusion.21) | copy-start | bytes 1572868
  255.5 8.4 %copy-start.5 = (pred[128,32,128]{2,0,1:T(32,128)(4,1)S(1)}, pred[128,32,128]{2,0,1:T(32,128)(4,1)}, u32[]{:S(2)}) copy-start(pred[128,32,128]{2,0,1:T(32,128)(4,1)} %iota_compare_fusion) | copy-start | bytes 1572868
  279.9 25.9 %copy-start.1 = (bf16[88,2048]{1,0:T(8,128)(2,1)S(1)}, bf16[88,2048]{1,0:T(8,128)(2,1)}, u32[]{:S(2)}) copy-start(bf16[88,2048]{1,0:T(8,128)(2,1)} %param.11) | copy-start | bytes 1081348
Sparse Core Ops, SparseCore 0:
  9.5 184.0 all-gather.1

commit v5 on v4

--- a/solution.py
+++ b/solution.py
@@ -77,31 +77,30 @@
     out_ref[...] += acc
 
 
-def imaging(spec, source_index, source_cutoff, source_weight, sb=8):
-    T = spec.shape[0]
+def imaging(spec_rows, source_index, source_cutoff, source_weight, sb=8):
+    T = spec_rows.shape[0]
     S = source_index.shape[0]
     x0 = jnp.clip(source_index[:, 0], 0, ORD - W)
     y0 = jnp.clip(source_index[:, 1], 0, ORD - W)
     rows = x0[:, None] + jnp.arange(W, dtype=jnp.int32)[None, :]
     pick = (rows[:, :, None] == jnp.arange(ORD, dtype=jnp.int32)[None, None, :]).astype(bf16)
-    spec_rows = spec.reshape(T, 6, 2, ORD, ORD).transpose(0, 1, 3, 2, 4).reshape(T, 6, ORD, 2 * ORD)
     i = jnp.arange(W, dtype=jnp.int32)
     j = jnp.arange(ORD, dtype=jnp.int32)[None, :] - y0[:, None]
     dist = (i[None, :, None] - W // 2) ** 2 + (j[:, None, :] - W // 2) ** 2
     keep = (dist <= (source_cutoff * source_cutoff)[:, None, None]) & (j[:, None, :] >= 0) & (j[:, None, :] < W)
-    keep = jnp.concatenate([keep, keep], 2)
+    keep = jnp.tile(keep, (1, 1, 12))
     t1, t2 = phase_tables()
     t1h, t1l = split_bf16(t1)
     t1s = jnp.concatenate([t1h, t1l], 1)
     t2h, t2l = split_bf16(t2)
     t2c = jnp.concatenate([t2h, t2h, t2l, jnp.zeros((2 * PIX, W), bf16)], 1)
-    block = pl.BlockSpec((sb, W, 2 * ORD), lambda s: (s, 0, 0))
+    blocks = [pl.BlockSpec((sb, W, 2 * ORD), functools.partial(lambda k, s: (s, 0, k), k)) for k in range(6)]
     call = pl.pallas_call(
         functools.partial(power_kernel, sb=sb),
         out_shape=jax.ShapeDtypeStruct((PIX, 2 * PIX), f32),
         grid=(S // sb,),
         in_specs=[pl.BlockSpec(memory_space=pltpu.SMEM)]
-        + [block] * 6
+        + blocks
         + [
             pl.BlockSpec((2 * ORD, 4 * PIX), lambda s: (0, 0)),
             pl.BlockSpec((2 * PIX, 4 * W), lambda s: (0, 0)),
@@ -112,11 +111,9 @@
     )
     outs = []
     for t in range(T):
-        parts = []
-        for k in range(6):
-            strips = jnp.einsum("siu,un->sin", pick, spec_rows[t, k], preferred_element_type=f32)
-            parts.append(jnp.where(keep, strips, 0.0).astype(bf16))
-        outs.append(call(source_weight.astype(f32), *parts, t1s, t2c)[:, :PIX])
+        strips = jnp.einsum("siu,un->sin", pick, spec_rows[t], preferred_element_type=f32)
+        windows = jnp.where(keep, strips, 0.0).astype(bf16)
+        outs.append(call(source_weight.astype(f32), *([windows] * 6), t1s, t2c)[:, :PIX])
     power = jnp.stack(outs, 0)
     return power.reshape(T, PIX * PIX) * (1.0 / (6.0 * W * W * S))
 
@@ -185,12 +182,12 @@
     order = me ^ jnp.arange(n_src, dtype=jnp.int32)
     coeffs = jnp.take(coeff_parts, order, axis=0).transpose(1, 0, 2).reshape(token_count, -1)
     tile_count = token_count // PATCH
-    spectra = (
-        coeffs.reshape(tile_count, GRID, GRID, 12, SUB, SUB)
-        .transpose(0, 3, 1, 4, 2, 5)
-        .reshape(tile_count, 12, ORD, ORD)
-    )
-    return imaging(spectra, source_index, source_cutoff, source_weight)
+    spec_rows = (
+        coeffs.reshape(tile_count, GRID, GRID, 6, 2, SUB, SUB)
+        .transpose(0, 1, 5, 3, 4, 2, 6)
+        .reshape(tile_count, ORD, 12 * ORD)
+    )
+    return imaging(spec_rows, source_index, source_cutoff, source_weight)
 
 
 def solution(mesh):

time: 314 us -> 329 us (1.048)
  local copies, waits for them, and re-layouts: 23.1 us -> 51.9 us
  matrix products: 51.7 us -> 40.3 us
    another operation x3 -> x5, local copies, waits for them, and re-layouts: 17.1 us -> 44.6 us  [the longest x2 26.5 us: imaging(): keep = jnp.tile(keep, (1, 1, 12))]
    dot_general x6 -> x1, matrix products: 16 us -> 8.22 us  [imaging(): jnp.einsum('siu,un->sin', pick, spec_rows[t], preferred_element_type=f32)]
    dot_general x1, matrix products: 7.64 us -> 3.99 us  [local(): jnp.dot(hidden_mine, gathered, preferred_element_type=jnp.float32)]
  transfers between devices with their start and end apart: 5 -> 5, of which waited for: 2 -> 1; matrix products, arithmetic and copies ran while one was open for 14% -> 20% of each run, Pallas kernels for 0% -> 0%
where the time goes in v5:
time: 329 us; the launch traced here: 327 us
  waiting for transfers between devices  184 us (56%)
  local copies, waits for them, and re-layouts  51.9 us (16%)
  matrix products  40.3 us (12%)
  Pallas kernels  24.5 us (7%)
  between operations  13.8 us (4%)
  other arithmetic  8.48 us (3%)
  starting transfers between devices  3.89 us (1%)
    all_gather x1, waiting for transfers between devices, local(): gathered = lax.all_gather(packed, 'tile', axis=0, tiled=True)  184 us
    another operation x2, local copies, waits for them, and re-layouts, imaging(): keep = jnp.tile(keep, (1, 1, 12))  26.5 us
    pallas_call x1, Pallas kernels, imaging(): call(source_weight.astype(f32), *[windows] * 6, t1s, t2c)[:, :PIX]  24.5 us
    dot_general x1, matrix products, local(): jnp.dot(normed_other, sibling, preferred_element_type=jnp.float32)  9.91 us
    another operation x1, local copies, waits for them, and re-layouts, imaging(): spec_rows[t]  9.38 us
    another operation x2, local copies, waits for them, and re-layouts, local(): coeffs.reshape(tile_count, GRID, GRID, 6, 2, SUB, SUB)  8.81 us
    dot_general x1, matrix products, imaging(): jnp.einsum('siu,un->sin', pick, spec_rows[t], preferred_element_type=f32)  8.22 us
    dot_general x1, matrix products, local(): jnp.dot(hidden_other, sibling, preferred_element_type=jnp.float32)  7.79 us
  transfers between devices with their start and end apart: 5, of which 1 were waited for; matrix products, arithmetic and copies ran while one was open for 20% of the time, Pallas kernels for 0%

profile of v5, /device:TPU:0, one launch (start us, length us, event | category | flops | bytes accessed | tf_op | source)
XLA Modules:
  0.0 327.1 jit_solution(12696923261155429164)
XLA Ops:
  6.6 1.0 copy-done
  7.6 0.9 constant_dynamic-slice_fusion.1
  8.5 0.8 fusion.32
  9.4 184.2 %all-gather.2.cloned.1.call-done = bf16[2560,2816]{1,0:T(8,128)(2,1)} async-done(((bf16[80,2816]{1,0:T(8,128)(2,1)}), bf16[2560,2816]{1,0:T(8,128)(2,1)}) %all-gather.2.cloned.1.call-update) | async-done | bytes 14417936 | tf_op jit(solution)/shard_map/all_gather | solution.py:150
  193.6 0.5 collective-permute-start
  194.1 3.4 %collective-permute-start.1 = (bf16[2048,192]{0,1:T(8,128)(2,1)}, bf16[2048,192]{0,1:T(8,128)(2,1)}, u32[]{:S(2)}, u32[]{:S(2)}) collective-permute-start(bf16[2048,192]{0,1:T(8,128)(2,1)} %param.12), channel_id=1, source_target_pairs={{0,2},{1,3},{2,0},{3,1},{4,6},{5,7},{6,4},{7,5},{8,10},{9,11},{10,... | collective-permute-start | bytes 2359304 | tf_op jit(solution)/shard_map/ppermute | solution.py:153
  197.5 1.5 fusion.16
  199.0 0.3 fusion.18
  199.3 0.5 copy.32
  199.9 0.1 dynamic-slice_bitcast_fusion.2
  200.0 0.1 pad.18
  200.1 0.1 pad.20
  200.2 0.4 copy-done.8
  200.6 0.5 fusion.21
  201.2 3.2 tile.4
  204.4 23.3 %copy.39 = pred[128,32,1536]{2,1,0:T(32,128)(4,1)} copy(pred[128,32,1536]{0,2,1:T(32,128)(4,1)S(1)} %bitcast.51) | data formatting | bytes 12582912 | tf_op jit(solution)/shard_map/tile | solution.py:91
  227.6 0.1 fusion.51
  227.7 0.1 fusion.55
  227.8 0.1 copy.41
  227.9 0.1 copy.42
  228.0 0.1 pad.26.clone
  228.1 0.3 fusion.44
  228.4 0.3 fusion.42
  228.7 0.1 reduce-precision_convert_fusion
  228.8 0.7 pad_maximum_fusion.refs_6_
  229.5 0.7 maximum_maximum_fusion.1.refs_7_
  230.2 1.4 iota_compare_fusion
  231.6 7.7 %fusion.57 = f32[256,2816]{1,0:T(8,128)S(1)} fusion(bf16[256,2560]{0,1:T(8,128)(2,1)S(1)} %bitcast.53, bf16[2560,2816]{1,0:T(8,128)(2,1)} %all-gather.2.cloned.1.call-done), kind=kOutput, calls=%fused_computation.95 | convolution fusion | flops 3690987520 | bytes 18612224 | tf_op jit(solution)/shard_map/dot_general | solution.py:168
  239.3 9.9 %fusion.15 = bf16[256,2816]{1,0:T(8,128)(2,1)S(1)} fusion(f32[256,2816]{1,0:T(8,128)S(1)} %fusion.57, bf16[256,2560]{0,1:T(8,128)(2,1)S(1)} %bitcast.57, bf16[2560,2816]{1,0:T(8,128)(2,1)} %collective-permute-done.3), kind=kOutput, calls=%fused_computation.22 | convolution fusion | flops 3698196480 | bytes 20054016 | tf_op jit(solution)/shard_map/dot_general | solution.py:168
  249.2 0.7 copy.33
  249.9 0.3 reshape.160
  250.3 0.1 dynamic-slice_bitcast_fusion.1
  250.4 0.1 pad.22.clone
  250.5 0.1 pad.21.clone
  250.6 7.8 %fusion.59 = f32[256,2816]{1,0:T(8,128)S(1)} fusion(bf16[256,2560]{0,1:T(8,128)(2,1)S(1)} %bitcast.54, bf16[2560,2816]{1,0:T(8,128)(2,1)} %collective-permute-done.3), kind=kOutput, calls=%fused_computation.97 | convolution fusion | flops 3690987520 | bytes 18612224 | tf_op jit(solution)/shard_map/dot_general | solution.py:173
  258.4 0.8 slice-done.2
  259.2 0.5 slice-done.3
  259.7 4.0 %fusion.58 = f32[256,2816]{1,0:T(8,128)S(1)} fusion(bf16[256,2560]{0,1:T(8,128)(2,1)S(1)} %bitcast.55, bf16[2560,2816]{1,0:T(8,128)(2,1)S(1)} %bitcast.50), kind=kOutput, calls=%fused_computation.96 | convolution fusion | flops 3690987520 | bytes 18612224 | tf_op jit(solution)/shard_map/dot_general | solution.py:173
  263.8 2.7 fusion.26
  266.4 0.6 gather_fusion
  267.0 0.9 select_bitcast_fusion
  267.9 3.5 %reshape_reshape.3 = bf16[1,16,16,6,2,8,8]{2,1,6,5,4,3,0:T(8,128)(2,1)S(1)} reshape(bf16[256,4,192]{0,2,1:T(8,128)(2,1)} %select_bitcast_fusion) | data formatting | bytes 786432 | tf_op jit(solution)/shard_map/reshape;reshape | solution.py:186
  271.4 5.3 %copy.38 = bf16[1,16,16,6,2,8,8]{6,2,4,3,5,1,0:T(8,128)(2,1)} copy(bf16[1,16,16,6,2,8,8]{2,1,6,5,4,3,0:T(8,128)(2,1)S(1)} %reshape_reshape.3) | data formatting | bytes 786432 | tf_op jit(solution)/shard_map/reshape;reshape | solution.py:186
  276.7 9.4 %reshape.172 = bf16[128,1536,1]{1,0,2:T(8,128)(2,1)S(1)} reshape(bf16[1,16,8,6,2,16,8]{6,5,4,3,2,1,0:T(8,128)(2,1)} %bitcast.52) | data formatting | bytes 786432 | tf_op jit(solution)/shard_map/squeeze;reshape | solution.py:114
  286.1 8.2 %select_convert_fusion.refs_0_.refs_1_.refs_2_.refs_3_.refs_4_.refs_5_ = bf16[128,32,1536]{2,1,0:T(8,128)(2,1)} fusion(pred[128,32,1536]{2,1,0:T(32,128)(4,1)} %copy.39, bf16[128,1536,1]{1,0,2:T(8,128)(2,1)S(1)} %reshape.172, pred[128,32,128]{2,0,1:T(32,128)(4,1)S(1)} %copy-done.4), kind=kOutput, calls=%fused_computation.1 | convolution fusion | flops 1623195648 | bytes 19791872 | tf_op jit(solution)/shard_map/siu,un->sin/dot_general | solution.py:114
  294.3 24.5 %shard_map.82 = f32[64,128]{1,0:T(8,128)} custom-call(f32[128]{0:T(128)} %w_ref.1, bf16[128,32,1536]{2,1,0:T(8,128)(2,1)} %select_convert_fusion.refs_0_.refs_1_.refs_2_.refs_3_.refs_4_.refs_5_, bf16[128,32,1536]{2,1,0:T(8,128)(2,1)} %select_convert_fusion.refs_0_.refs_1_.refs_2_.refs_3_.refs_4_.refs_5_, ...), custom_call_target="tpu_custom_call" | custom-call | tf_op jit(solution)/shard_map/pallas_call | solution.py:116
  318.8 0.8 slice_multiply_fusion
  319.6 0.7 mul.163
  (44 shorter events, 0.3 us)
Async XLA Ops:
  6.5 1.0 copy-start
  6.5 192.5 %copy-start.2 = (bf16[256,2048]{1,0:T(8,128)(2,1)S(1)}, bf16[256,2048]{1,0:T(8,128)(2,1)}, u32[]{:S(2)}) copy-start(bf16[256,2048]{1,0:T(8,128)(2,1)} %param.8) | copy-start | bytes 3145732
  6.5 192.5 %copy-start.5 = (f32[2048]{0:T(1024)S(1)}, f32[2048]{0:T(1024)}, u32[]{:S(2)}) copy-start(f32[2048]{0:T(1024)} %param.9) | copy-start | bytes 24580
  6.5 187.0 %all-gather.2.cloned.1.call-start = ((), (), s32[]{:S(2)}) async-start(), calls=%async_computation | async-start | bytes 14868480 | tf_op jit(solution)/shard_map/all_gather | solution.py:150
  193.6 45.7 %collective-permute-start.3 = (bf16[2560,2816]{1,0:T(8,128)(2,1)}, bf16[2560,2816]{1,0:T(8,128)(2,1)}, u32[]{:S(2)}, u32[]{:S(2)}) collective-permute-start(bf16[2560,2816]{1,0:T(8,128)(2,1)} %all-gather.2.cloned.1.call-done), channel_id=1, source_target_pairs={{0,1},{1,0},{2,3},{3,2},{4,5},{5,4},{6,7},{7,6},{8,9},{9,8},{10,11... | collective-permute-start | bytes 43253768 | tf_op jit(solution)/shard_map/ppermute | solution.py:151
  193.6 70.1 %collective-permute-start = (bf16[2048,192]{0,1:T(8,128)(2,1)}, bf16[2048,192]{0,1:T(8,128)(2,1)}, u32[]{:S(2)}, u32[]{:S(2)}) collective-permute-start(bf16[2048,192]{0,1:T(8,128)(2,1)} %param.12), channel_id=1, source_target_pairs={{0,1},{1,0},{2,3},{3,2},{4,5},{5,4},{6,7},{7,6},{8,9},{9,8},{10,11... | collective-permute-start | bytes 2359304 | tf_op jit(solution)/shard_map/ppermute | solution.py:153
  194.1 69.6 %collective-permute-start.1 = (bf16[2048,192]{0,1:T(8,128)(2,1)}, bf16[2048,192]{0,1:T(8,128)(2,1)}, u32[]{:S(2)}, u32[]{:S(2)}) collective-permute-start(bf16[2048,192]{0,1:T(8,128)(2,1)} %param.12), channel_id=1, source_target_pairs={{0,2},{1,3},{2,0},{3,1},{4,6},{5,7},{6,4},{7,5},{8,10},{9,11},{10,... | collective-permute-start | bytes 2359304 | tf_op jit(solution)/shard_map/ppermute | solution.py:153
  197.5 66.3 %collective-permute-start.2 = (bf16[2048,192]{0,1:T(8,128)(2,1)}, bf16[2048,192]{0,1:T(8,128)(2,1)}, u32[]{:S(2)}, u32[]{:S(2)}) collective-permute-start(bf16[2048,192]{0,1:T(8,128)(2,1)} %param.12), channel_id=1, source_target_pairs={{0,3},{1,2},{2,1},{3,0},{4,7},{5,6},{6,5},{7,4},{8,11},{9,10},{10,... | collective-permute-start | bytes 2359304 | tf_op jit(solution)/shard_map/ppermute | solution.py:153
  199.9 0.7 copy-start.8
  199.9 0.7 copy-start.6
  250.4 8.0 %slice-start = ((s8[14417920]{0:T(1024)(128)(4,1)}), s8[4194304]{0:T(1024)(128)(4,1)S(1)}, s32[]{:S(2)}) async-start(s8[14417920]{0:T(1024)(128)(4,1)} %bitcast.49), calls=%async_computation.1 | async-start | bytes 8388608
  250.6 7.8 %slice-start.1 = ((s8[14417920]{0:T(1024)(128)(4,1)}), s8[4194304]{0:T(1024)(128)(4,1)S(1)}, s32[]{:S(2)}) async-start(s8[14417920]{0:T(1024)(128)(4,1)} %bitcast.49), calls=%async_computation.2 | async-start | bytes 8388608
  250.6 8.6 %slice-start.2 = ((s8[14417920]{0:T(1024)(128)(4,1)}), s8[4194304]{0:T(1024)(128)(4,1)S(1)}, s32[]{:S(2)}) async-start(s8[14417920]{0:T(1024)(128)(4,1)} %bitcast.49), calls=%async_computation.3 | async-start | bytes 8388608
  250.6 9.1 %slice-start.3 = ((s8[14417920]{0:T(1024)(128)(4,1)}), s8[1835008]{0:T(1024)(128)(4,1)S(1)}, s32[]{:S(2)}) async-start(s8[14417920]{0:T(1024)(128)(4,1)} %bitcast.49), calls=%async_computation.4 | async-start | bytes 3670016
  259.7 4.0 %copy-start.3 = (bf16[256,2048]{1,0:T(8,128)(2,1)S(1)}, bf16[256,2048]{1,0:T(8,128)(2,1)}, u32[]{:S(2)}) copy-start(bf16[256,2048]{1,0:T(8,128)(2,1)} %param.8) | copy-start | bytes 3145732
  259.7 4.0 %copy-start.7 = (bf16[2048,192]{0,1:T(8,128)(2,1)S(1)}, bf16[2048,192]{0,1:T(8,128)(2,1)}, u32[]{:S(2)}) copy-start(bf16[2048,192]{0,1:T(8,128)(2,1)} %param.12) | copy-start | bytes 2359300
  276.7 9.4 %copy-start.4 = (pred[128,32,128]{2,0,1:T(32,128)(4,1)S(1)}, pred[128,32,128]{2,0,1:T(32,128)(4,1)}, u32[]{:S(2)}) copy-start(pred[128,32,128]{2,0,1:T(32,128)(4,1)} %iota_compare_fusion) | copy-start | bytes 1572868
  294.3 26.0 %copy-start.1 = (bf16[88,2048]{1,0:T(8,128)(2,1)S(1)}, bf16[88,2048]{1,0:T(8,128)(2,1)}, u32[]{:S(2)}) copy-start(bf16[88,2048]{1,0:T(8,128)(2,1)} %param.11) | copy-start | bytes 1081348
Sparse Core Ops, SparseCore 0:
  9.5 184.0 all-gather.1

commit v6 on v5

--- a/solution.py
+++ b/solution.py
@@ -85,10 +85,9 @@
     rows = x0[:, None] + jnp.arange(W, dtype=jnp.int32)[None, :]
     pick = (rows[:, :, None] == jnp.arange(ORD, dtype=jnp.int32)[None, None, :]).astype(bf16)
     i = jnp.arange(W, dtype=jnp.int32)
-    j = jnp.arange(ORD, dtype=jnp.int32)[None, :] - y0[:, None]
+    j = jnp.arange(12 * ORD, dtype=jnp.int32)[None, :] % ORD - y0[:, None]
     dist = (i[None, :, None] - W // 2) ** 2 + (j[:, None, :] - W // 2) ** 2
     keep = (dist <= (source_cutoff * source_cutoff)[:, None, None]) & (j[:, None, :] >= 0) & (j[:, None, :] < W)
-    keep = jnp.tile(keep, (1, 1, 12))
     t1, t2 = phase_tables()
     t1h, t1l = split_bf16(t1)
     t1s = jnp.concatenate([t1h, t1l], 1)

time: 329 us -> 310 us (0.942)
  local copies, waits for them, and re-layouts: 51.9 us -> 24.3 us
  matrix products: 40.3 us -> 46.2 us
    another operation x2 -> x0, local copies, waits for them, and re-layouts: 26.5 us -> none  [imaging(): keep = jnp.tile(keep, (1, 1, 12))]
    dot_general x1, matrix products: 3.99 us -> 7.69 us  [local(): jnp.dot(hidden_mine, gathered, preferred_element_type=jnp.float32)]
  transfers between devices with their start and end apart: 5 -> 5, of which waited for: 1 -> 2; matrix products, arithmetic and copies ran while one was open for 20% -> 14% of each run, Pallas kernels for 0% -> 0%
where the time goes in v6:
time: 310 us; the launch traced here: 308 us
  waiting for transfers between devices  186 us (60%)
  matrix products  46.2 us (15%)
  Pallas kernels  24.5 us (8%)
  local copies, waits for them, and re-layouts  24.3 us (8%)
  between operations  13.8 us (4%)
  other arithmetic  9.88 us (3%)
  starting transfers between devices  3.89 us (1%)
    all_gather x1, waiting for transfers between devices, local(): gathered = lax.all_gather(packed, 'tile', axis=0, tiled=True)  184 us
    pallas_call x1, Pallas kernels, imaging(): call(source_weight.astype(f32), *[windows] * 6, t1s, t2c)[:, :PIX]  24.5 us
    dot_general x1, matrix products, imaging(): jnp.einsum('siu,un->sin', pick, spec_rows[t], preferred_element_type=f32)  10.4 us
    dot_general x1, matrix products, local(): jnp.dot(normed_other, sibling, preferred_element_type=jnp.float32)  9.91 us
    another operation x1, local copies, waits for them, and re-layouts, imaging(): spec_rows[t]  9.44 us
    another operation x2, local copies, waits for them, and re-layouts, local(): coeffs.reshape(tile_count, GRID, GRID, 6, 2, SUB, SUB)  8.85 us
    dot_general x1, matrix products, local(): jnp.dot(hidden_other, sibling, preferred_element_type=jnp.float32)  7.93 us
    dot_general x1, matrix products, local(): jnp.dot(hidden_mine, gathered, preferred_element_type=jnp.float32)  7.69 us
  transfers between devices with their start and end apart: 5, of which 2 were waited for; matrix products, arithmetic and copies ran while one was open for 14% of the time, Pallas kernels for 0%

profile of v6, /device:TPU:0, one launch (start us, length us, event | category | flops | bytes accessed | tf_op | source)
XLA Modules:
  0.0 308.3 jit_solution(17806365017332190594)
XLA Ops:
  6.6 1.0 copy-done
  7.5 0.1 constant_dynamic-slice_fusion
  7.6 0.9 constant_dynamic-slice_fusion.1
  8.5 0.8 fusion.33
  9.3 0.0 all-gather.2.cloned.1.call-update
  9.4 184.2 %all-gather.2.cloned.1.call-done = bf16[2560,2816]{1,0:T(8,128)(2,1)} async-done(((bf16[80,2816]{1,0:T(8,128)(2,1)}), bf16[2560,2816]{1,0:T(8,128)(2,1)}) %all-gather.2.cloned.1.call-update) | async-done | bytes 14417936 | tf_op jit(solution)/shard_map/all_gather | solution.py:149
  193.6 0.5 collective-permute-start
  194.1 3.4 %collective-permute-start.1 = (bf16[2048,192]{0,1:T(8,128)(2,1)}, bf16[2048,192]{0,1:T(8,128)(2,1)}, u32[]{:S(2)}, u32[]{:S(2)}) collective-permute-start(bf16[2048,192]{0,1:T(8,128)(2,1)} %param.12), channel_id=1, source_target_pairs={{0,2},{1,3},{2,0},{3,1},{4,6},{5,7},{6,4},{7,5},{8,10},{9,11},{10,... | collective-permute-start | bytes 2359304 | tf_op jit(solution)/shard_map/ppermute | solution.py:152
  197.5 1.5 fusion.18
  199.0 0.3 fusion.20
  199.3 0.5 copy.30
  199.9 0.1 dynamic-slice_bitcast_fusion.2
  200.0 0.1 pad.18
  200.1 0.1 pad.20
  200.2 0.4 copy-done.10
  200.5 0.1 fusion.50
  200.6 0.1 fusion.57
  200.7 0.1 copy.38
  200.8 0.1 copy.39
  200.9 0.1 pad.26.clone
  201.0 0.3 fusion.43
  201.3 0.3 fusion.41
  201.6 0.1 reduce-precision_convert_fusion
  201.7 0.7 pad_maximum_fusion.refs_6_
  202.4 0.7 maximum_maximum_fusion.1.refs_7_
  203.1 1.4 iota_compare_fusion
  204.5 1.0 subtract_compare_fusion.1
  205.5 1.0 fusion.32
  206.5 7.6 %fusion.59 = f32[256,2816]{1,0:T(8,128)S(1)} fusion(bf16[256,2560]{0,1:T(8,128)(2,1)S(1)} %bitcast.49, bf16[2560,2816]{1,0:T(8,128)(2,1)} %all-gather.2.cloned.1.call-done), kind=kOutput, calls=%fused_computation.100 | convolution fusion | flops 3690987520 | bytes 18612224 | tf_op jit(solution)/shard_map/dot_general | solution.py:167
  214.1 1.6 collective-permute-done.3
  215.7 9.9 %fusion.17 = bf16[256,2816]{1,0:T(8,128)(2,1)S(1)} fusion(f32[256,2816]{1,0:T(8,128)S(1)} %fusion.59, bf16[256,2560]{0,1:T(8,128)(2,1)S(1)} %bitcast.53, bf16[2560,2816]{1,0:T(8,128)(2,1)} %collective-permute-done.3), kind=kOutput, calls=%fused_computation.25 | convolution fusion | flops 3698196480 | bytes 20054016 | tf_op jit(solution)/shard_map/dot_general | solution.py:167
  225.6 0.7 copy.31
  226.3 0.3 reshape.188
  226.6 0.1 dynamic-slice_bitcast_fusion.1
  226.8 0.1 pad.21.clone
  226.9 0.1 pad.22.clone
  227.0 7.7 %fusion.60 = f32[256,2816]{1,0:T(8,128)S(1)} fusion(bf16[256,2560]{0,1:T(8,128)(2,1)S(1)} %bitcast.50, bf16[2560,2816]{1,0:T(8,128)(2,1)} %all-gather.2.cloned.1.call-done), kind=kOutput, calls=%fused_computation.101 | convolution fusion | flops 3690987520 | bytes 18612224 | tf_op jit(solution)/shard_map/dot_general | solution.py:172
  234.7 7.9 %fusion.61 = f32[256,2816]{1,0:T(8,128)S(1)} fusion(bf16[256,2560]{0,1:T(8,128)(2,1)S(1)} %bitcast.51, bf16[2560,2816]{1,0:T(8,128)(2,1)} %collective-permute-done.3), kind=kOutput, calls=%fused_computation.102 | convolution fusion | flops 3690987520 | bytes 18612224 | tf_op jit(solution)/shard_map/dot_general | solution.py:172
  242.7 2.7 fusion.26
  245.3 0.6 gather_fusion
  245.9 0.9 select_bitcast_fusion
  246.8 3.5 %reshape_reshape.3 = bf16[1,16,16,6,2,8,8]{2,1,6,5,4,3,0:T(8,128)(2,1)S(1)} reshape(bf16[256,4,192]{0,2,1:T(8,128)(2,1)} %select_bitcast_fusion) | data formatting | bytes 786432 | tf_op jit(solution)/shard_map/reshape;reshape | solution.py:185
  250.3 5.4 %copy.36 = bf16[1,16,16,6,2,8,8]{6,2,4,3,5,1,0:T(8,128)(2,1)} copy(bf16[1,16,16,6,2,8,8]{2,1,6,5,4,3,0:T(8,128)(2,1)S(1)} %reshape_reshape.3) | data formatting | bytes 786432 | tf_op jit(solution)/shard_map/reshape;reshape | solution.py:185
  255.6 9.4 %reshape.200 = bf16[128,1536,1]{1,0,2:T(8,128)(2,1)S(1)} reshape(bf16[1,16,8,6,2,16,8]{6,5,4,3,2,1,0:T(8,128)(2,1)} %bitcast.48) | data formatting | bytes 786432 | tf_op jit(solution)/shard_map/squeeze;reshape | solution.py:113
  265.1 10.4 %select_convert_fusion.refs_0_.refs_1_.refs_2_.refs_3_.refs_4_.refs_5_ = bf16[128,32,1536]{2,1,0:T(8,128)(2,1)} fusion(bf16[128,1536,1]{1,0,2:T(8,128)(2,1)S(1)} %reshape.200, s32[128]{0:T(128)S(1)} %mul.136, s32[128,1536]{1,0:T(8,128)S(1)} %copy-done.4, s32[32]{0:T(128)S(1)} %add_multiply_fusion, pred[128,1536]{1,0:T(8,128)(4,1)S(1)} %copy-done.6, ...), kind=kOutput, calls=%fused_computation.1 | convolution fusion | flops 1648361472 | bytes 14680704 | tf_op jit(solution)/shard_map/siu,un->sin/dot_general | solution.py:113
  275.5 24.5 %shard_map.82 = f32[64,128]{1,0:T(8,128)} custom-call(f32[128]{0:T(128)} %w_ref.1, bf16[128,32,1536]{2,1,0:T(8,128)(2,1)} %select_convert_fusion.refs_0_.refs_1_.refs_2_.refs_3_.refs_4_.refs_5_, bf16[128,32,1536]{2,1,0:T(8,128)(2,1)} %select_convert_fusion.refs_0_.refs_1_.refs_2_.refs_3_.refs_4_.refs_5_, ...), custom_call_target="tpu_custom_call" | custom-call | tf_op jit(solution)/shard_map/pallas_call | solution.py:115
  300.0 0.8 slice_multiply_fusion
  300.8 0.7 mul.163
  (37 shorter events, 0.1 us)
Async XLA Ops:
  6.5 1.0 copy-start
  6.5 192.5 %copy-start.2 = (bf16[256,2048]{1,0:T(8,128)(2,1)S(1)}, bf16[256,2048]{1,0:T(8,128)(2,1)}, u32[]{:S(2)}) copy-start(bf16[256,2048]{1,0:T(8,128)(2,1)} %param.8) | copy-start | bytes 3145732
  6.5 192.5 %copy-start.7 = (f32[2048]{0:T(1024)S(1)}, f32[2048]{0:T(1024)}, u32[]{:S(2)}) copy-start(f32[2048]{0:T(1024)} %param.9) | copy-start | bytes 24580
  6.5 187.0 %all-gather.2.cloned.1.call-start = ((), (), s32[]{:S(2)}) async-start(), calls=%async_computation | async-start | bytes 14868480 | tf_op jit(solution)/shard_map/all_gather | solution.py:149
  193.6 22.1 %collective-permute-start.3 = (bf16[2560,2816]{1,0:T(8,128)(2,1)}, bf16[2560,2816]{1,0:T(8,128)(2,1)}, u32[]{:S(2)}, u32[]{:S(2)}) collective-permute-start(bf16[2560,2816]{1,0:T(8,128)(2,1)} %all-gather.2.cloned.1.call-done), channel_id=1, source_target_pairs={{0,1},{1,0},{2,3},{3,2},{4,5},{5,4},{6,7},{7,6},{8,9},{9,8},{10,11... | collective-permute-start | bytes 43253768 | tf_op jit(solution)/shard_map/ppermute | solution.py:150
  193.6 49.0 %collective-permute-start = (bf16[2048,192]{0,1:T(8,128)(2,1)}, bf16[2048,192]{0,1:T(8,128)(2,1)}, u32[]{:S(2)}, u32[]{:S(2)}) collective-permute-start(bf16[2048,192]{0,1:T(8,128)(2,1)} %param.12), channel_id=1, source_target_pairs={{0,1},{1,0},{2,3},{3,2},{4,5},{5,4},{6,7},{7,6},{8,9},{9,8},{10,11... | collective-permute-start | bytes 2359304 | tf_op jit(solution)/shard_map/ppermute | solution.py:152
  194.1 48.5 %collective-permute-start.1 = (bf16[2048,192]{0,1:T(8,128)(2,1)}, bf16[2048,192]{0,1:T(8,128)(2,1)}, u32[]{:S(2)}, u32[]{:S(2)}) collective-permute-start(bf16[2048,192]{0,1:T(8,128)(2,1)} %param.12), channel_id=1, source_target_pairs={{0,2},{1,3},{2,0},{3,1},{4,6},{5,7},{6,4},{7,5},{8,10},{9,11},{10,... | collective-permute-start | bytes 2359304 | tf_op jit(solution)/shard_map/ppermute | solution.py:152
  197.5 45.2 %collective-permute-start.2 = (bf16[2048,192]{0,1:T(8,128)(2,1)}, bf16[2048,192]{0,1:T(8,128)(2,1)}, u32[]{:S(2)}, u32[]{:S(2)}) collective-permute-start(bf16[2048,192]{0,1:T(8,128)(2,1)} %param.12), channel_id=1, source_target_pairs={{0,3},{1,2},{2,1},{3,0},{4,7},{5,6},{6,5},{7,4},{8,11},{9,10},{10,... | collective-permute-start | bytes 2359304 | tf_op jit(solution)/shard_map/ppermute | solution.py:152
  199.9 0.7 copy-start.10
  200.0 2.4 copy-start.8
  234.7 8.0 %copy-start.3 = (bf16[256,2048]{1,0:T(8,128)(2,1)S(1)}, bf16[256,2048]{1,0:T(8,128)(2,1)}, u32[]{:S(2)}) copy-start(bf16[256,2048]{1,0:T(8,128)(2,1)} %param.8) | copy-start | bytes 3145732
  234.7 8.0 %copy-start.9 = (bf16[2048,192]{0,1:T(8,128)(2,1)S(1)}, bf16[2048,192]{0,1:T(8,128)(2,1)}, u32[]{:S(2)}) copy-start(bf16[2048,192]{0,1:T(8,128)(2,1)} %param.12) | copy-start | bytes 2359300
  255.6 9.5 %copy-start.4 = (s32[128,1536]{1,0:T(8,128)S(1)}, s32[128,1536]{1,0:T(8,128)}, u32[]{:S(2)}) copy-start(s32[128,1536]{1,0:T(8,128)} %fusion.32) | copy-start | bytes 2359300
  255.6 9.5 %copy-start.5 = (pred[128,32,128]{2,0,1:T(32,128)(4,1)S(1)}, pred[128,32,128]{2,0,1:T(32,128)(4,1)}, u32[]{:S(2)}) copy-start(pred[128,32,128]{2,0,1:T(32,128)(4,1)} %iota_compare_fusion) | copy-start | bytes 1572868
  255.6 9.5 %copy-start.6 = (pred[128,1536]{1,0:T(8,128)(4,1)S(1)}, pred[128,1536]{1,0:T(8,128)(4,1)}, u32[]{:S(2)}) copy-start(pred[128,1536]{1,0:T(8,128)(4,1)} %get-tuple-element.16) | copy-start | bytes 589828
  275.5 26.0 %copy-start.1 = (bf16[88,2048]{1,0:T(8,128)(2,1)S(1)}, bf16[88,2048]{1,0:T(8,128)(2,1)}, u32[]{:S(2)}) copy-start(bf16[88,2048]{1,0:T(8,128)(2,1)} %param.11) | copy-start | bytes 1081348
Sparse Core Ops, SparseCore 0:
  9.5 184.0 all-gather.1

commit v7 on v6

--- a/solution.py
+++ b/solution.py
@@ -85,10 +85,12 @@
     rows = x0[:, None] + jnp.arange(W, dtype=jnp.int32)[None, :]
     pick = (rows[:, :, None] == jnp.arange(ORD, dtype=jnp.int32)[None, None, :]).astype(bf16)
     i = jnp.arange(W, dtype=jnp.int32)
-    j = jnp.arange(12 * ORD, dtype=jnp.int32)[None, :] % ORD - y0[:, None]
+    n = jnp.arange(12 * ORD, dtype=jnp.int32)
+    j = ((n % GRID) * SUB + (n % ORD) // GRID)[None, :] - y0[:, None]
     dist = (i[None, :, None] - W // 2) ** 2 + (j[:, None, :] - W // 2) ** 2
     keep = (dist <= (source_cutoff * source_cutoff)[:, None, None]) & (j[:, None, :] >= 0) & (j[:, None, :] < W)
     t1, t2 = phase_tables()
+    t1 = t1.reshape(2, GRID, SUB, 2 * PIX).transpose(0, 2, 1, 3).reshape(2 * ORD, 2 * PIX)
     t1h, t1l = split_bf16(t1)
     t1s = jnp.concatenate([t1h, t1l], 1)
     t2h, t2l = split_bf16(t2)
@@ -183,7 +185,7 @@
     tile_count = token_count // PATCH
     spec_rows = (
         coeffs.reshape(tile_count, GRID, GRID, 6, 2, SUB, SUB)
-        .transpose(0, 1, 5, 3, 4, 2, 6)
+        .transpose(0, 1, 5, 3, 4, 6, 2)
         .reshape(tile_count, ORD, 12 * ORD)
     )
     return imaging(spec_rows, source_index, source_cutoff, source_weight)

time: 310 us -> 304 us (0.981)
  local copies, waits for them, and re-layouts: 24.3 us -> 18.2 us
    another operation x2 -> x1, local copies, waits for them, and re-layouts: 8.85 us -> 3.49 us  [local(): coeffs.reshape(tile_count, GRID, GRID, 6, 2, SUB, SUB)]
    another operation x1, local copies, waits for them, and re-layouts: 9.44 us -> 6.27 us  [imaging(): spec_rows[t]]
where the time goes in v7:
time: 304 us; the launch traced here: 302 us
  waiting for transfers between devices  186 us (61%)
  matrix products  46.2 us (15%)
  Pallas kernels  24.5 us (8%)
  local copies, waits for them, and re-layouts  18.2 us (6%)
  between operations  13.8 us (5%)
  other arithmetic  9.91 us (3%)
  starting transfers between devices  3.89 us (1%)
    all_gather x1, waiting for transfers between devices, local(): gathered = lax.all_gather(packed, 'tile', axis=0, tiled=True)  184 us
    pallas_call x1, Pallas kernels, imaging(): call(source_weight.astype(f32), *[windows] * 6, t1s, t2c)[:, :PIX]  24.5 us
    dot_general x1, matrix products, imaging(): jnp.einsum('siu,un->sin', pick, spec_rows[t], preferred_element_type=f32)  10.4 us
    dot_general x1, matrix products, local(): jnp.dot(normed_other, sibling, preferred_element_type=jnp.float32)  9.91 us
    dot_general x1, matrix products, local(): jnp.dot(hidden_other, sibling, preferred_element_type=jnp.float32)  7.93 us
    dot_general x1, matrix products, local(): jnp.dot(hidden_mine, gathered, preferred_element_type=jnp.float32)  7.69 us
    dot_general x1, matrix products, local(): jnp.dot(normed_mine, gathered, preferred_element_type=jnp.float32)  7.58 us
    another operation x1, local copies, waits for them, and re-layouts, imaging(): spec_rows[t]  6.27 us
  transfers between devices with their start and end apart: 5, of which 2 were waited for; matrix products, arithmetic and copies ran while one was open for 14% of the time, Pallas kernels for 0%

profile of v7, /device:TPU:0, one launch (start us, length us, event | category | flops | bytes accessed | tf_op | source)
XLA Modules:
  0.0 302.2 jit_solution(16924291254204393191)
XLA Ops:
  6.6 1.0 copy-done
  7.5 0.1 constant_dynamic-slice_fusion
  7.6 0.9 constant_dynamic-slice_fusion.1
  8.5 0.8 fusion.33
  9.3 0.0 all-gather.2.cloned.1.call-update
  9.4 184.2 %all-gather.2.cloned.1.call-done = bf16[2560,2816]{1,0:T(8,128)(2,1)} async-done(((bf16[80,2816]{1,0:T(8,128)(2,1)}), bf16[2560,2816]{1,0:T(8,128)(2,1)}) %all-gather.2.cloned.1.call-update) | async-done | bytes 14417936 | tf_op jit(solution)/shard_map/all_gather | solution.py:151
  193.6 0.5 collective-permute-start
  194.1 3.4 %collective-permute-start.1 = (bf16[2048,192]{0,1:T(8,128)(2,1)}, bf16[2048,192]{0,1:T(8,128)(2,1)}, u32[]{:S(2)}, u32[]{:S(2)}) collective-permute-start(bf16[2048,192]{0,1:T(8,128)(2,1)} %param.12), channel_id=1, source_target_pairs={{0,2},{1,3},{2,0},{3,1},{4,6},{5,7},{6,4},{7,5},{8,10},{9,11},{10,... | collective-permute-start | bytes 2359304 | tf_op jit(solution)/shard_map/ppermute | solution.py:154
  197.5 1.5 fusion.18
  199.0 0.3 fusion.20
  199.3 0.5 copy.32
  199.9 0.1 dynamic-slice_bitcast_fusion.2
  200.0 0.1 pad.18
  200.1 0.1 pad.20
  200.2 0.4 copy-done.10
  200.5 0.1 fusion.60
  200.6 0.1 fusion.67
  200.7 0.1 copy.41
  200.8 0.1 copy.42
  200.9 0.3 fusion.43
  201.2 0.3 fusion.41
  201.5 0.1 maximum_maximum_fusion
  201.6 0.1 pad.26.clone
  201.8 0.7 pad_maximum_fusion.refs_6_
  202.5 0.7 maximum_maximum_fusion.1.refs_7_
  203.2 1.4 iota_compare_fusion
  204.6 1.0 subtract_compare_fusion.1
  205.6 1.0 fusion.32
  206.6 7.6 %fusion.69 = f32[256,2816]{1,0:T(8,128)S(1)} fusion(bf16[256,2560]{0,1:T(8,128)(2,1)S(1)} %bitcast.55, bf16[2560,2816]{1,0:T(8,128)(2,1)} %all-gather.2.cloned.1.call-done), kind=kOutput, calls=%fused_computation.116 | convolution fusion | flops 3690987520 | bytes 18612224 | tf_op jit(solution)/shard_map/dot_general | solution.py:169
  214.2 1.5 collective-permute-done.3
  215.7 9.9 %fusion.17 = bf16[256,2816]{1,0:T(8,128)(2,1)S(1)} fusion(f32[256,2816]{1,0:T(8,128)S(1)} %fusion.69, bf16[256,2560]{0,1:T(8,128)(2,1)S(1)} %bitcast.59, bf16[2560,2816]{1,0:T(8,128)(2,1)} %collective-permute-done.3), kind=kOutput, calls=%fused_computation.25 | convolution fusion | flops 3698196480 | bytes 20054016 | tf_op jit(solution)/shard_map/dot_general | solution.py:169
  225.6 0.7 copy.33
  226.3 0.3 reshape.212
  226.6 0.1 dynamic-slice_bitcast_fusion.1
  226.8 0.1 pad.21.clone
  226.9 0.1 pad.22.clone
  227.0 7.7 %fusion.70 = f32[256,2816]{1,0:T(8,128)S(1)} fusion(bf16[256,2560]{0,1:T(8,128)(2,1)S(1)} %bitcast.56, bf16[2560,2816]{1,0:T(8,128)(2,1)} %all-gather.2.cloned.1.call-done), kind=kOutput, calls=%fused_computation.117 | convolution fusion | flops 3690987520 | bytes 18612224 | tf_op jit(solution)/shard_map/dot_general | solution.py:174
  234.7 7.9 %fusion.71 = f32[256,2816]{1,0:T(8,128)S(1)} fusion(bf16[256,2560]{0,1:T(8,128)(2,1)S(1)} %bitcast.57, bf16[2560,2816]{1,0:T(8,128)(2,1)} %collective-permute-done.3), kind=kOutput, calls=%fused_computation.118 | convolution fusion | flops 3690987520 | bytes 18612224 | tf_op jit(solution)/shard_map/dot_general | solution.py:174
  242.7 2.7 fusion.26
  245.3 0.6 gather_fusion
  245.9 0.9 select_bitcast_fusion
  246.8 3.5 %reshape_reshape.3 = bf16[1,16,16,6,2,8,8]{2,1,6,5,4,3,0:T(8,128)(2,1)S(1)} reshape(bf16[256,4,192]{0,2,1:T(8,128)(2,1)} %select_bitcast_fusion) | data formatting | bytes 786432 | tf_op jit(solution)/shard_map/reshape;reshape | solution.py:187
  250.3 2.4 copy.38
  252.7 6.3 %reshape.226 = bf16[128,1536,1]{1,0,2:T(8,128)(2,1)S(1)} reshape(bf16[1,16,8,6,2,8,16]{6,5,4,3,2,1,0:T(8,128)(2,1)} %copy.38) | data formatting | bytes 786432 | tf_op jit(solution)/shard_map/squeeze;reshape | solution.py:115
  259.0 10.4 %select_convert_fusion.refs_0_.refs_1_.refs_2_.refs_3_.refs_4_.refs_5_ = bf16[128,32,1536]{2,1,0:T(8,128)(2,1)} fusion(bf16[128,1536,1]{1,0,2:T(8,128)(2,1)S(1)} %reshape.226, s32[128]{0:T(128)S(1)} %mul.148, s32[128,1536]{1,0:T(8,128)S(1)} %copy-done.4, s32[32]{0:T(128)S(1)} %add_multiply_fusion, pred[128,1536]{1,0:T(8,128)(4,1)S(1)} %copy-done.6, ...), kind=kOutput, calls=%fused_computation.1 | convolution fusion | flops 1648361472 | bytes 14680704 | tf_op jit(solution)/shard_map/siu,un->sin/dot_general | solution.py:115
  269.4 24.5 %shard_map.82 = f32[64,128]{1,0:T(8,128)} custom-call(f32[128]{0:T(128)} %w_ref.1, bf16[128,32,1536]{2,1,0:T(8,128)(2,1)} %select_convert_fusion.refs_0_.refs_1_.refs_2_.refs_3_.refs_4_.refs_5_, bf16[128,32,1536]{2,1,0:T(8,128)(2,1)} %select_convert_fusion.refs_0_.refs_1_.refs_2_.refs_3_.refs_4_.refs_5_, ...), custom_call_target="tpu_custom_call" | custom-call | tf_op jit(solution)/shard_map/pallas_call | solution.py:117
  293.9 0.8 slice_multiply_fusion
  294.7 0.7 mul.175
  (39 shorter events, 0.2 us)
Async XLA Ops:
  6.5 1.0 copy-start
  6.5 192.5 %copy-start.2 = (bf16[256,2048]{1,0:T(8,128)(2,1)S(1)}, bf16[256,2048]{1,0:T(8,128)(2,1)}, u32[]{:S(2)}) copy-start(bf16[256,2048]{1,0:T(8,128)(2,1)} %param.8) | copy-start | bytes 3145732
  6.5 192.5 %copy-start.7 = (f32[2048]{0:T(1024)S(1)}, f32[2048]{0:T(1024)}, u32[]{:S(2)}) copy-start(f32[2048]{0:T(1024)} %param.9) | copy-start | bytes 24580
  6.5 187.0 %all-gather.2.cloned.1.call-start = ((), (), s32[]{:S(2)}) async-start(), calls=%async_computation | async-start | bytes 14868480 | tf_op jit(solution)/shard_map/all_gather | solution.py:151
  193.6 22.1 %collective-permute-start.3 = (bf16[2560,2816]{1,0:T(8,128)(2,1)}, bf16[2560,2816]{1,0:T(8,128)(2,1)}, u32[]{:S(2)}, u32[]{:S(2)}) collective-permute-start(bf16[2560,2816]{1,0:T(8,128)(2,1)} %all-gather.2.cloned.1.call-done), channel_id=1, source_target_pairs={{0,1},{1,0},{2,3},{3,2},{4,5},{5,4},{6,7},{7,6},{8,9},{9,8},{10,11... | collective-permute-start | bytes 43253768 | tf_op jit(solution)/shard_map/ppermute | solution.py:152
  193.6 49.0 %collective-permute-start = (bf16[2048,192]{0,1:T(8,128)(2,1)}, bf16[2048,192]{0,1:T(8,128)(2,1)}, u32[]{:S(2)}, u32[]{:S(2)}) collective-permute-start(bf16[2048,192]{0,1:T(8,128)(2,1)} %param.12), channel_id=1, source_target_pairs={{0,1},{1,0},{2,3},{3,2},{4,5},{5,4},{6,7},{7,6},{8,9},{9,8},{10,11... | collective-permute-start | bytes 2359304 | tf_op jit(solution)/shard_map/ppermute | solution.py:154
  194.1 48.5 %collective-permute-start.1 = (bf16[2048,192]{0,1:T(8,128)(2,1)}, bf16[2048,192]{0,1:T(8,128)(2,1)}, u32[]{:S(2)}, u32[]{:S(2)}) collective-permute-start(bf16[2048,192]{0,1:T(8,128)(2,1)} %param.12), channel_id=1, source_target_pairs={{0,2},{1,3},{2,0},{3,1},{4,6},{5,7},{6,4},{7,5},{8,10},{9,11},{10,... | collective-permute-start | bytes 2359304 | tf_op jit(solution)/shard_map/ppermute | solution.py:154
  197.5 45.2 %collective-permute-start.2 = (bf16[2048,192]{0,1:T(8,128)(2,1)}, bf16[2048,192]{0,1:T(8,128)(2,1)}, u32[]{:S(2)}, u32[]{:S(2)}) collective-permute-start(bf16[2048,192]{0,1:T(8,128)(2,1)} %param.12), channel_id=1, source_target_pairs={{0,3},{1,2},{2,1},{3,0},{4,7},{5,6},{6,5},{7,4},{8,11},{9,10},{10,... | collective-permute-start | bytes 2359304 | tf_op jit(solution)/shard_map/ppermute | solution.py:154
  199.9 0.7 copy-start.10
  200.0 2.5 copy-start.8
  234.7 8.0 %copy-start.3 = (bf16[256,2048]{1,0:T(8,128)(2,1)S(1)}, bf16[256,2048]{1,0:T(8,128)(2,1)}, u32[]{:S(2)}) copy-start(bf16[256,2048]{1,0:T(8,128)(2,1)} %param.8) | copy-start | bytes 3145732
  234.7 8.0 %copy-start.9 = (bf16[2048,192]{0,1:T(8,128)(2,1)S(1)}, bf16[2048,192]{0,1:T(8,128)(2,1)}, u32[]{:S(2)}) copy-start(bf16[2048,192]{0,1:T(8,128)(2,1)} %param.12) | copy-start | bytes 2359300
  252.7 6.3 %copy-start.4 = (s32[128,1536]{1,0:T(8,128)S(1)}, s32[128,1536]{1,0:T(8,128)}, u32[]{:S(2)}) copy-start(s32[128,1536]{1,0:T(8,128)} %fusion.32) | copy-start | bytes 2359300
  252.7 6.3 %copy-start.5 = (pred[128,32,128]{2,0,1:T(32,128)(4,1)S(1)}, pred[128,32,128]{2,0,1:T(32,128)(4,1)}, u32[]{:S(2)}) copy-start(pred[128,32,128]{2,0,1:T(32,128)(4,1)} %iota_compare_fusion) | copy-start | bytes 1572868
  252.7 6.3 %copy-start.6 = (pred[128,1536]{1,0:T(8,128)(4,1)S(1)}, pred[128,1536]{1,0:T(8,128)(4,1)}, u32[]{:S(2)}) copy-start(pred[128,1536]{1,0:T(8,128)(4,1)} %get-tuple-element.16) | copy-start | bytes 589828
  269.4 26.0 %copy-start.1 = (bf16[88,2048]{1,0:T(8,128)(2,1)S(1)}, bf16[88,2048]{1,0:T(8,128)(2,1)}, u32[]{:S(2)}) copy-start(bf16[88,2048]{1,0:T(8,128)(2,1)} %param.11) | copy-start | bytes 1081348
Sparse Core Ops, SparseCore 0:
  9.5 184.0 all-gather.1

commit v8 on v7

--- a/solution.py
+++ b/solution.py
@@ -77,7 +77,7 @@
     out_ref[...] += acc
 
 
-def imaging(spec_rows, source_index, source_cutoff, source_weight, sb=8):
+def imaging(spec_rows, source_index, source_cutoff, source_weight, sb=16):
     T = spec_rows.shape[0]
     S = source_index.shape[0]
     x0 = jnp.clip(source_index[:, 0], 0, ORD - W)

time: 304 us -> 301 us (level)
  no operation moved by 1% of the time
where the time goes in v8:
time: 301 us; the launch traced here: 300 us
  waiting for transfers between devices  186 us (62%)
  matrix products  46.2 us (15%)
  Pallas kernels  22.3 us (7%)
  local copies, waits for them, and re-layouts  18.2 us (6%)
  between operations  13.8 us (5%)
  other arithmetic  9.91 us (3%)
  starting transfers between devices  3.89 us (1%)
    all_gather x1, waiting for transfers between devices, local(): gathered = lax.all_gather(packed, 'tile', axis=0, tiled=True)  184 us
    pallas_call x1, Pallas kernels, imaging(): call(source_weight.astype(f32), *[windows] * 6, t1s, t2c)[:, :PIX]  22.3 us
    dot_general x1, matrix products, imaging(): jnp.einsum('siu,un->sin', pick, spec_rows[t], preferred_element_type=f32)  10.4 us
    dot_general x1, matrix products, local(): jnp.dot(normed_other, sibling, preferred_element_type=jnp.float32)  9.91 us
    dot_general x1, matrix products, local(): jnp.dot(hidden_other, sibling, preferred_element_type=jnp.float32)  7.93 us
    dot_general x1, matrix products, local(): jnp.dot(hidden_mine, gathered, preferred_element_type=jnp.float32)  7.69 us
    dot_general x1, matrix products, local(): jnp.dot(normed_mine, gathered, preferred_element_type=jnp.float32)  7.58 us
    another operation x1, local copies, waits for them, and re-layouts, imaging(): spec_rows[t]  6.27 us
  transfers between devices with their start and end apart: 5, of which 2 were waited for; matrix products, arithmetic and copies ran while one was open for 14% of the time, Pallas kernels for 0%

profile of v8, /device:TPU:0, one launch (start us, length us, event | category | flops | bytes accessed | tf_op | source)
XLA Modules:
  0.0 300.0 jit_solution(12248346249991894602)
XLA Ops:
  6.6 1.0 copy-done
  7.5 0.1 constant_dynamic-slice_fusion
  7.6 0.9 constant_dynamic-slice_fusion.1
  8.5 0.8 fusion.33
  9.3 0.0 all-gather.2.cloned.1.call-update
  9.4 184.2 %all-gather.2.cloned.1.call-done = bf16[2560,2816]{1,0:T(8,128)(2,1)} async-done(((bf16[80,2816]{1,0:T(8,128)(2,1)}), bf16[2560,2816]{1,0:T(8,128)(2,1)}) %all-gather.2.cloned.1.call-update) | async-done | bytes 14417936 | tf_op jit(solution)/shard_map/all_gather | solution.py:151
  193.6 0.5 collective-permute-start
  194.1 3.4 %collective-permute-start.1 = (bf16[2048,192]{0,1:T(8,128)(2,1)}, bf16[2048,192]{0,1:T(8,128)(2,1)}, u32[]{:S(2)}, u32[]{:S(2)}) collective-permute-start(bf16[2048,192]{0,1:T(8,128)(2,1)} %param.12), channel_id=1, source_target_pairs={{0,2},{1,3},{2,0},{3,1},{4,6},{5,7},{6,4},{7,5},{8,10},{9,11},{10,... | collective-permute-start | bytes 2359304 | tf_op jit(solution)/shard_map/ppermute | solution.py:154
  197.5 1.5 fusion.18
  199.0 0.3 fusion.20
  199.3 0.5 copy.32
  199.9 0.1 dynamic-slice_bitcast_fusion.2
  200.0 0.1 pad.18
  200.1 0.1 pad.20
  200.2 0.4 copy-done.10
  200.5 0.1 fusion.60
  200.6 0.1 fusion.67
  200.7 0.1 copy.41
  200.8 0.1 copy.42
  200.9 0.3 fusion.43
  201.2 0.3 fusion.41
  201.5 0.1 maximum_maximum_fusion
  201.6 0.1 pad.26.clone
  201.8 0.7 pad_maximum_fusion.refs_6_
  202.5 0.7 maximum_maximum_fusion.1.refs_7_
  203.2 1.4 iota_compare_fusion
  204.6 1.0 subtract_compare_fusion.1
  205.6 1.0 fusion.32
  206.6 7.6 %fusion.69 = f32[256,2816]{1,0:T(8,128)S(1)} fusion(bf16[256,2560]{0,1:T(8,128)(2,1)S(1)} %bitcast.55, bf16[2560,2816]{1,0:T(8,128)(2,1)} %all-gather.2.cloned.1.call-done), kind=kOutput, calls=%fused_computation.116 | convolution fusion | flops 3690987520 | bytes 18612224 | tf_op jit(solution)/shard_map/dot_general | solution.py:169
  214.2 1.5 collective-permute-done.3
  215.7 9.9 %fusion.17 = bf16[256,2816]{1,0:T(8,128)(2,1)S(1)} fusion(f32[256,2816]{1,0:T(8,128)S(1)} %fusion.69, bf16[256,2560]{0,1:T(8,128)(2,1)S(1)} %bitcast.59, bf16[2560,2816]{1,0:T(8,128)(2,1)} %collective-permute-done.3), kind=kOutput, calls=%fused_computation.25 | convolution fusion | flops 3698196480 | bytes 20054016 | tf_op jit(solution)/shard_map/dot_general | solution.py:169
  225.6 0.7 copy.33
  226.3 0.3 reshape.212
  226.6 0.1 dynamic-slice_bitcast_fusion.1
  226.8 0.1 pad.21.clone
  226.9 0.1 pad.22.clone
  227.0 7.7 %fusion.70 = f32[256,2816]{1,0:T(8,128)S(1)} fusion(bf16[256,2560]{0,1:T(8,128)(2,1)S(1)} %bitcast.56, bf16[2560,2816]{1,0:T(8,128)(2,1)} %all-gather.2.cloned.1.call-done), kind=kOutput, calls=%fused_computation.117 | convolution fusion | flops 3690987520 | bytes 18612224 | tf_op jit(solution)/shard_map/dot_general | solution.py:174
  234.7 7.9 %fusion.71 = f32[256,2816]{1,0:T(8,128)S(1)} fusion(bf16[256,2560]{0,1:T(8,128)(2,1)S(1)} %bitcast.57, bf16[2560,2816]{1,0:T(8,128)(2,1)} %collective-permute-done.3), kind=kOutput, calls=%fused_computation.118 | convolution fusion | flops 3690987520 | bytes 18612224 | tf_op jit(solution)/shard_map/dot_general | solution.py:174
  242.7 2.7 fusion.26
  245.3 0.6 gather_fusion
  245.9 0.9 select_bitcast_fusion
  246.8 3.5 %reshape_reshape.3 = bf16[1,16,16,6,2,8,8]{2,1,6,5,4,3,0:T(8,128)(2,1)S(1)} reshape(bf16[256,4,192]{0,2,1:T(8,128)(2,1)} %select_bitcast_fusion) | data formatting | bytes 786432 | tf_op jit(solution)/shard_map/reshape;reshape | solution.py:187
  250.3 2.4 copy.38
  252.7 6.3 %reshape.226 = bf16[128,1536,1]{1,0,2:T(8,128)(2,1)S(1)} reshape(bf16[1,16,8,6,2,8,16]{6,5,4,3,2,1,0:T(8,128)(2,1)} %copy.38) | data formatting | bytes 786432 | tf_op jit(solution)/shard_map/squeeze;reshape | solution.py:115
  259.0 10.4 %select_convert_fusion.refs_0_.refs_1_.refs_2_.refs_3_.refs_4_.refs_5_ = bf16[128,32,1536]{2,1,0:T(8,128)(2,1)} fusion(bf16[128,1536,1]{1,0,2:T(8,128)(2,1)S(1)} %reshape.226, s32[128]{0:T(128)S(1)} %mul.148, s32[128,1536]{1,0:T(8,128)S(1)} %copy-done.4, s32[32]{0:T(128)S(1)} %add_multiply_fusion, pred[128,1536]{1,0:T(8,128)(4,1)S(1)} %copy-done.6, ...), kind=kOutput, calls=%fused_computation.1 | convolution fusion | flops 1648361472 | bytes 14680704 | tf_op jit(solution)/shard_map/siu,un->sin/dot_general | solution.py:115
  269.4 22.3 %shard_map.82 = f32[64,128]{1,0:T(8,128)} custom-call(f32[128]{0:T(128)} %w_ref.1, bf16[128,32,1536]{2,1,0:T(8,128)(2,1)} %select_convert_fusion.refs_0_.refs_1_.refs_2_.refs_3_.refs_4_.refs_5_, bf16[128,32,1536]{2,1,0:T(8,128)(2,1)} %select_convert_fusion.refs_0_.refs_1_.refs_2_.refs_3_.refs_4_.refs_5_, ...), custom_call_target="tpu_custom_call" | custom-call | tf_op jit(solution)/shard_map/pallas_call | solution.py:117
  291.7 0.8 slice_multiply_fusion
  292.5 0.7 mul.175
  (39 shorter events, 0.2 us)
Async XLA Ops:
  6.5 1.0 copy-start
  6.5 192.5 %copy-start.2 = (bf16[256,2048]{1,0:T(8,128)(2,1)S(1)}, bf16[256,2048]{1,0:T(8,128)(2,1)}, u32[]{:S(2)}) copy-start(bf16[256,2048]{1,0:T(8,128)(2,1)} %param.8) | copy-start | bytes 3145732
  6.5 192.5 %copy-start.7 = (f32[2048]{0:T(1024)S(1)}, f32[2048]{0:T(1024)}, u32[]{:S(2)}) copy-start(f32[2048]{0:T(1024)} %param.9) | copy-start | bytes 24580
  6.5 187.0 %all-gather.2.cloned.1.call-start = ((), (), s32[]{:S(2)}) async-start(), calls=%async_computation | async-start | bytes 14868480 | tf_op jit(solution)/shard_map/all_gather | solution.py:151
  193.6 22.1 %collective-permute-start.3 = (bf16[2560,2816]{1,0:T(8,128)(2,1)}, bf16[2560,2816]{1,0:T(8,128)(2,1)}, u32[]{:S(2)}, u32[]{:S(2)}) collective-permute-start(bf16[2560,2816]{1,0:T(8,128)(2,1)} %all-gather.2.cloned.1.call-done), channel_id=1, source_target_pairs={{0,1},{1,0},{2,3},{3,2},{4,5},{5,4},{6,7},{7,6},{8,9},{9,8},{10,11... | collective-permute-start | bytes 43253768 | tf_op jit(solution)/shard_map/ppermute | solution.py:152
  193.6 49.0 %collective-permute-start = (bf16[2048,192]{0,1:T(8,128)(2,1)}, bf16[2048,192]{0,1:T(8,128)(2,1)}, u32[]{:S(2)}, u32[]{:S(2)}) collective-permute-start(bf16[2048,192]{0,1:T(8,128)(2,1)} %param.12), channel_id=1, source_target_pairs={{0,1},{1,0},{2,3},{3,2},{4,5},{5,4},{6,7},{7,6},{8,9},{9,8},{10,11... | collective-permute-start | bytes 2359304 | tf_op jit(solution)/shard_map/ppermute | solution.py:154
  194.1 48.5 %collective-permute-start.1 = (bf16[2048,192]{0,1:T(8,128)(2,1)}, bf16[2048,192]{0,1:T(8,128)(2,1)}, u32[]{:S(2)}, u32[]{:S(2)}) collective-permute-start(bf16[2048,192]{0,1:T(8,128)(2,1)} %param.12), channel_id=1, source_target_pairs={{0,2},{1,3},{2,0},{3,1},{4,6},{5,7},{6,4},{7,5},{8,10},{9,11},{10,... | collective-permute-start | bytes 2359304 | tf_op jit(solution)/shard_map/ppermute | solution.py:154
  197.5 45.2 %collective-permute-start.2 = (bf16[2048,192]{0,1:T(8,128)(2,1)}, bf16[2048,192]{0,1:T(8,128)(2,1)}, u32[]{:S(2)}, u32[]{:S(2)}) collective-permute-start(bf16[2048,192]{0,1:T(8,128)(2,1)} %param.12), channel_id=1, source_target_pairs={{0,3},{1,2},{2,1},{3,0},{4,7},{5,6},{6,5},{7,4},{8,11},{9,10},{10,... | collective-permute-start | bytes 2359304 | tf_op jit(solution)/shard_map/ppermute | solution.py:154
  199.9 0.7 copy-start.10
  200.0 2.5 copy-start.8
  234.7 8.0 %copy-start.3 = (bf16[256,2048]{1,0:T(8,128)(2,1)S(1)}, bf16[256,2048]{1,0:T(8,128)(2,1)}, u32[]{:S(2)}) copy-start(bf16[256,2048]{1,0:T(8,128)(2,1)} %param.8) | copy-start | bytes 3145732
  234.7 8.0 %copy-start.9 = (bf16[2048,192]{0,1:T(8,128)(2,1)S(1)}, bf16[2048,192]{0,1:T(8,128)(2,1)}, u32[]{:S(2)}) copy-start(bf16[2048,192]{0,1:T(8,128)(2,1)} %param.12) | copy-start | bytes 2359300
  252.7 6.3 %copy-start.4 = (s32[128,1536]{1,0:T(8,128)S(1)}, s32[128,1536]{1,0:T(8,128)}, u32[]{:S(2)}) copy-start(s32[128,1536]{1,0:T(8,128)} %fusion.32) | copy-start | bytes 2359300
  252.7 6.3 %copy-start.5 = (pred[128,32,128]{2,0,1:T(32,128)(4,1)S(1)}, pred[128,32,128]{2,0,1:T(32,128)(4,1)}, u32[]{:S(2)}) copy-start(pred[128,32,128]{2,0,1:T(32,128)(4,1)} %iota_compare_fusion) | copy-start | bytes 1572868
  252.7 6.3 %copy-start.6 = (pred[128,1536]{1,0:T(8,128)(4,1)S(1)}, pred[128,1536]{1,0:T(8,128)(4,1)}, u32[]{:S(2)}) copy-start(pred[128,1536]{1,0:T(8,128)(4,1)} %get-tuple-element.16) | copy-start | bytes 589828
  269.4 23.8 %copy-start.1 = (bf16[88,2048]{1,0:T(8,128)(2,1)S(1)}, bf16[88,2048]{1,0:T(8,128)(2,1)}, u32[]{:S(2)}) copy-start(bf16[88,2048]{1,0:T(8,128)(2,1)} %param.11) | copy-start | bytes 1081348
Sparse Core Ops, SparseCore 0:
  9.5 184.0 all-gather.1

commit v9 on v8

--- a/solution.py
+++ b/solution.py
@@ -40,30 +40,45 @@
     return t1, t2
 
 
-def power_kernel(w_ref, *refs, sb):
-    wm_refs, (t1_ref, t2_ref, out_ref, rcat) = refs[:6], refs[6:]
+def power_kernel(w_ref, x0_ref, y0_ref, r_ref, spec_ref, t1_ref, t2_ref, out_ref, xs, rcat, *, sb):
     step = pl.program_id(0)
     rcat[3 * W:, :] = jnp.zeros((W, sb * 6 * 2 * PIX), bf16)
+    n = lax.broadcasted_iota(jnp.int32, (W, 2 * ORD), 1)
+    col = (n % GRID) * SUB + (n % ORD) // GRID
+    row = lax.broadcasted_iota(jnp.int32, (W, 2 * ORD), 0)
+    keeps = []
+    for j in range(sb):
+        s = step * sb + j
+        jj = col - y0_ref[s]
+        radius = r_ref[s]
+        keep = ((row - W // 2) ** 2 + (jj - W // 2) ** 2 <= radius * radius) & (jj >= 0) & (jj < W)
+        keeps.append(keep)
     for k in range(6):
-        x = wm_refs[k][...].reshape(sb * W, 2 * ORD)
-        y = jnp.dot(x, t1_ref[...], preferred_element_type=f32)
+        for j in range(sb):
+            s = step * sb + j
+            start = x0_ref[s]
+            base = pl.multiple_of((start // 8) * 8, 8)
+            wide = spec_ref[pl.ds(base, W + 8), pl.ds(k * 2 * ORD, 2 * ORD)]
+            rows = pltpu.roll(wide, (W + 8 - (start - base)) % (W + 8), 0)[:W]
+            xs[j * W:(j + 1) * W, :] = jnp.where(keeps[j], rows, 0.0).astype(bf16)
+        y = jnp.dot(xs[...], t1_ref[...], preferred_element_type=f32)
         h = y[:, : 2 * PIX] + y[:, 2 * PIX:]
         hh = h.astype(bf16)
         hl = (h - hh.astype(f32)).astype(bf16)
         for j in range(sb):
-            n = k * sb + j
-            cols = slice(n * 2 * PIX, (n + 1) * 2 * PIX)
-            rows = slice(j * W, (j + 1) * W)
-            rcat[0:W, cols] = hh[rows, :]
-            rcat[W:2 * W, cols] = hl[rows, :]
-            rcat[2 * W:3 * W, cols] = hh[rows, :]
+            m = k * sb + j
+            cols = slice(m * 2 * PIX, (m + 1) * 2 * PIX)
+            rows_ = slice(j * W, (j + 1) * W)
+            rcat[0:W, cols] = hh[rows_, :]
+            rcat[W:2 * W, cols] = hl[rows_, :]
+            rcat[2 * W:3 * W, cols] = hh[rows_, :]
     q = jnp.dot(t2_ref[...], rcat[...], preferred_element_type=f32)
     acc = jnp.zeros((PIX, 2 * PIX), f32)
     for j in range(sb):
         part = jnp.zeros((PIX, 2 * PIX), f32)
         for k in range(6):
-            n = k * sb + j
-            blk = q[:, n * 2 * PIX:(n + 1) * 2 * PIX]
+            m = k * sb + j
+            blk = q[:, m * 2 * PIX:(m + 1) * 2 * PIX]
             rolled = pltpu.roll(blk, PIX, 1)
             er = blk[:PIX] - rolled[PIX:]
             ei = blk[PIX:] + rolled[:PIX]
@@ -82,39 +97,34 @@
     S = source_index.shape[0]
     x0 = jnp.clip(source_index[:, 0], 0, ORD - W)
     y0 = jnp.clip(source_index[:, 1], 0, ORD - W)
-    rows = x0[:, None] + jnp.arange(W, dtype=jnp.int32)[None, :]
-    pick = (rows[:, :, None] == jnp.arange(ORD, dtype=jnp.int32)[None, None, :]).astype(bf16)
-    i = jnp.arange(W, dtype=jnp.int32)
-    n = jnp.arange(12 * ORD, dtype=jnp.int32)
-    j = ((n % GRID) * SUB + (n % ORD) // GRID)[None, :] - y0[:, None]
-    dist = (i[None, :, None] - W // 2) ** 2 + (j[:, None, :] - W // 2) ** 2
-    keep = (dist <= (source_cutoff * source_cutoff)[:, None, None]) & (j[:, None, :] >= 0) & (j[:, None, :] < W)
     t1, t2 = phase_tables()
     t1 = t1.reshape(2, GRID, SUB, 2 * PIX).transpose(0, 2, 1, 3).reshape(2 * ORD, 2 * PIX)
     t1h, t1l = split_bf16(t1)
     t1s = jnp.concatenate([t1h, t1l], 1)
     t2h, t2l = split_bf16(t2)
     t2c = jnp.concatenate([t2h, t2h, t2l, jnp.zeros((2 * PIX, W), bf16)], 1)
-    blocks = [pl.BlockSpec((sb, W, 2 * ORD), functools.partial(lambda k, s: (s, 0, k), k)) for k in range(6)]
+    smem = pl.BlockSpec(memory_space=pltpu.SMEM)
     call = pl.pallas_call(
         functools.partial(power_kernel, sb=sb),
         out_shape=jax.ShapeDtypeStruct((PIX, 2 * PIX), f32),
         grid=(S // sb,),
-        in_specs=[pl.BlockSpec(memory_space=pltpu.SMEM)]
-        + blocks
+        in_specs=[smem] * 4
         + [
+            pl.BlockSpec((ORD + 8, 12 * ORD), lambda s: (0, 0)),
             pl.BlockSpec((2 * ORD, 4 * PIX), lambda s: (0, 0)),
             pl.BlockSpec((2 * PIX, 4 * W), lambda s: (0, 0)),
         ],
         out_specs=pl.BlockSpec((PIX, 2 * PIX), lambda s: (0, 0)),
-        scratch_shapes=[pltpu.VMEM((4 * W, sb * 6 * 2 * PIX), bf16)],
+        scratch_shapes=[pltpu.VMEM((sb * W, 2 * ORD), bf16), pltpu.VMEM((4 * W, sb * 6 * 2 * PIX), bf16)],
         compiler_params=pltpu.CompilerParams(dimension_semantics=("arbitrary",)),
     )
     outs = []
     for t in range(T):
-        strips = jnp.einsum("siu,un->sin", pick, spec_rows[t], preferred_element_type=f32)
-        windows = jnp.where(keep, strips, 0.0).astype(bf16)
-        outs.append(call(source_weight.astype(f32), *([windows] * 6), t1s, t2c)[:, :PIX])
+        outs.append(
+            call(
+                source_weight.astype(f32), x0, y0, source_cutoff, jnp.pad(spec_rows[t].astype(f32), ((0, 8), (0, 0))), t1s, t2c
+            )[:, :PIX]
+        )
     power = jnp.stack(outs, 0)
     return power.reshape(T, PIX * PIX) * (1.0 / (6.0 * W * W * S))
 

time: 301 us -> 297 us (0.987)
  matrix products: 46.2 us -> 35.7 us
  Pallas kernels: 22.3 us -> 27.5 us
    convert_element_type x0 -> x3, local copies, waits for them, and re-layouts: none -> 12.1 us  [imaging(): spec_rows[t].astype(f32)]
    dot_general x1 -> x0, matrix products: 10.4 us -> none  [imaging(): jnp.einsum('siu,un->sin', pick, spec_rows[t], preferred_element_type=f32)]
    another operation x2 -> x0, local copies, waits for them, and re-layouts: 9.75 us -> none  [the longest x1 6.27 us: imaging(): spec_rows[t]]
    pallas_call x1, Pallas kernels: 22.3 us -> 27.5 us  [imaging(): call(source_weight.astype(f32), x0, y0, source_cutoff, jnp.pad(spec_rows[...]
    ppermute x1, waiting for transfers between devices: 1.52 us -> 4.8 us  [local(): sibling = lax.ppermute(gathered, 'src', [(s, s ^ 1) for s in range(n_src)])]
where the time goes in v9:
time: 297 us; the launch traced here: 296 us
  waiting for transfers between devices  189 us (64%)
  matrix products  35.7 us (12%)
  Pallas kernels  27.5 us (9%)
  local copies, waits for them, and re-layouts  17.8 us (6%)
  between operations  13.7 us (5%)
  other arithmetic  8.07 us (3%)
  starting transfers between devices  3.89 us (1%)
    all_gather x1, waiting for transfers between devices, local(): gathered = lax.all_gather(packed, 'tile', axis=0, tiled=True)  184 us
    pallas_call x1, Pallas kernels, imaging(): call(source_weight.astype(f32), x0, y0, source_cutoff, jnp.pad(spec_rows[...  27.5 us
    convert_element_type x3, local copies, waits for them, and re-layouts, imaging(): spec_rows[t].astype(f32)  12.1 us
    dot_general x1, matrix products, local(): jnp.dot(normed_other, sibling, preferred_element_type=jnp.float32)  9.91 us
    dot_general x1, matrix products, local(): jnp.dot(hidden_other, sibling, preferred_element_type=jnp.float32)  7.95 us
    dot_general x1, matrix products, local(): jnp.dot(hidden_mine, gathered, preferred_element_type=jnp.float32)  7.64 us
    dot_general x1, matrix products, local(): jnp.dot(normed_mine, gathered, preferred_element_type=jnp.float32)  7.53 us
  transfers between devices with their start and end apart: 5, of which 2 were waited for; matrix products, arithmetic and copies ran while one was open for 14% of the time, Pallas kernels for 0%

profile of v9, /device:TPU:0, one launch (start us, length us, event | category | flops | bytes accessed | tf_op | source)
XLA Modules:
  0.0 295.7 jit_solution(2315340249379969015)
XLA Ops:
  6.6 1.0 copy-done
  7.5 0.1 constant_dynamic-slice_fusion
  7.6 0.9 constant_dynamic-slice_fusion.1
  8.5 0.8 fusion.29
  9.3 0.0 all-gather.2.cloned.1.call-update
  9.4 184.2 %all-gather.2.cloned.1.call-done = bf16[2560,2816]{1,0:T(8,128)(2,1)} async-done(((bf16[80,2816]{1,0:T(8,128)(2,1)}), bf16[2560,2816]{1,0:T(8,128)(2,1)}) %all-gather.2.cloned.1.call-update) | async-done | bytes 14417936 | tf_op jit(solution)/shard_map/all_gather | solution.py:161
  193.6 0.5 collective-permute-start
  194.1 3.4 %collective-permute-start.1 = (bf16[2048,192]{0,1:T(8,128)(2,1)}, bf16[2048,192]{0,1:T(8,128)(2,1)}, u32[]{:S(2)}, u32[]{:S(2)}) collective-permute-start(bf16[2048,192]{0,1:T(8,128)(2,1)} %param.12), channel_id=1, source_target_pairs={{0,2},{1,3},{2,0},{3,1},{4,6},{5,7},{6,4},{7,5},{8,10},{9,11},{10,... | collective-permute-start | bytes 2359304 | tf_op jit(solution)/shard_map/ppermute | solution.py:164
  197.5 1.5 fusion.16
  199.0 0.3 fusion.18
  199.3 0.5 copy.29
  199.9 0.1 dynamic-slice_bitcast_fusion.2
  200.0 0.0 copy-start.5
  200.0 0.1 pad.24
  200.1 0.1 pad.26
  200.2 0.1 fusion.46
  200.3 0.1 fusion.50
  200.3 0.1 copy.37
  200.4 0.1 copy.38
  200.6 0.3 fusion.39
  200.8 0.3 fusion.37
  201.1 0.1 maximum_maximum_fusion
  201.3 0.1 pad.34.clone
  201.4 0.7 pad_maximum_fusion.t1_ref
  202.1 0.6 clamp_bitcast_fusion
  202.7 0.7 maximum_maximum_fusion.1.t2_ref
  203.4 7.5 %fusion.52 = f32[256,2816]{1,0:T(8,128)S(1)} fusion(bf16[256,2560]{0,1:T(8,128)(2,1)S(1)} %bitcast.56, bf16[2560,2816]{1,0:T(8,128)(2,1)} %all-gather.2.cloned.1.call-done), kind=kOutput, calls=%fused_computation.85 | convolution fusion | flops 3690987520 | bytes 18612224 | tf_op jit(solution)/shard_map/dot_general | solution.py:179
  210.9 4.8 %collective-permute-done.3 = bf16[2560,2816]{1,0:T(8,128)(2,1)} collective-permute-done((bf16[2560,2816]{1,0:T(8,128)(2,1)}, bf16[2560,2816]{1,0:T(8,128)(2,1)}, u32[]{:S(2)}, u32[]{:S(2)}) %collective-permute-start.3) | collective-permute-done | bytes 14417952 | tf_op jit(solution)/shard_map/ppermute | solution.py:162
  215.7 9.9 %fusion.15 = bf16[256,2816]{1,0:T(8,128)(2,1)S(1)} fusion(f32[256,2816]{1,0:T(8,128)S(1)} %fusion.52, bf16[256,2560]{0,1:T(8,128)(2,1)S(1)} %bitcast.60, bf16[2560,2816]{1,0:T(8,128)(2,1)} %collective-permute-done.3), kind=kOutput, calls=%fused_computation.22 | convolution fusion | flops 3698196480 | bytes 20054016 | tf_op jit(solution)/shard_map/dot_general | solution.py:179
  225.6 0.7 copy.30
  226.3 0.3 reshape.81
  226.7 0.1 dynamic-slice_bitcast_fusion.1
  226.8 0.1 pad.27.clone
  226.9 0.1 pad.28.clone
  227.0 7.6 %fusion.53 = f32[256,2816]{1,0:T(8,128)S(1)} fusion(bf16[256,2560]{0,1:T(8,128)(2,1)S(1)} %bitcast.57, bf16[2560,2816]{1,0:T(8,128)(2,1)} %all-gather.2.cloned.1.call-done), kind=kOutput, calls=%fused_computation.86 | convolution fusion | flops 3690987520 | bytes 18612224 | tf_op jit(solution)/shard_map/dot_general | solution.py:184
  234.6 0.0 copy-start.3
  234.6 0.0 copy-start.6
  234.7 8.0 %fusion.54 = f32[256,2816]{1,0:T(8,128)S(1)} fusion(bf16[256,2560]{0,1:T(8,128)(2,1)S(1)} %bitcast.58, bf16[2560,2816]{1,0:T(8,128)(2,1)} %collective-permute-done.3), kind=kOutput, calls=%fused_computation.87 | convolution fusion | flops 3690987520 | bytes 18612224 | tf_op jit(solution)/shard_map/dot_general | solution.py:184
  242.7 2.7 fusion.23
  245.3 0.6 gather_fusion
  245.9 0.8 select_bitcast_fusion
  246.8 3.5 %convert_element_type.74 = bf16[1,16,16,6,2,8,8]{2,1,6,5,4,3,0:T(8,128)(2,1)S(1)} reshape(bf16[256,4,192]{0,2,1:T(8,128)(2,1)} %select_bitcast_fusion) | data formatting | bytes 786432 | tf_op jit(solution)/shard_map/convert_element_type | solution.py:125
  250.3 2.5 copy.45
  252.7 6.2 %convert_element_type.76 = bf16[128,1536]{1,0:T(8,128)(2,1)S(1)} reshape(bf16[1,16,8,6,2,8,16]{6,5,4,3,2,1,0:T(8,128)(2,1)} %bitcast.55) | data formatting | bytes 786432 | tf_op jit(solution)/shard_map/convert_element_type | solution.py:125
  258.9 1.0 pad_convert_fusion.spec_ref
  259.9 27.5 %shard_map.82 = f32[64,128]{1,0:T(8,128)} custom-call(f32[128]{0:T(128)} %w_ref.1, s32[128]{0:T(128)} %get-tuple-element.16.x0_ref, s32[128]{0:T(128)} %get-tuple-element.15.y0_ref, s32[128]{0:T(128)} %r_ref.1, f32[136,1536]{1,0:T(8,128)} %pad_convert_fusion.spec_ref, bf16[256,256]{1,0:T(8,128)(2,1)} %pad_maximum_fusion.t1_ref, ...), custom_call_target="tpu_custom_call" | custom-call | tf_op jit(solution)/shard_map/pallas_call | solution.py:124
  287.4 0.8 slice_multiply_fusion
  288.2 0.7 mul.159
  (24 shorter events, 0.1 us)
Async XLA Ops:
  6.5 1.0 copy-start
  6.5 192.5 %copy-start.2 = (bf16[256,2048]{1,0:T(8,128)(2,1)S(1)}, bf16[256,2048]{1,0:T(8,128)(2,1)}, u32[]{:S(2)}) copy-start(bf16[256,2048]{1,0:T(8,128)(2,1)} %param.8) | copy-start | bytes 3145732
  6.5 192.5 %copy-start.4 = (f32[2048]{0:T(1024)S(1)}, f32[2048]{0:T(1024)}, u32[]{:S(2)}) copy-start(f32[2048]{0:T(1024)} %param.9) | copy-start | bytes 24580
  6.5 187.1 %all-gather.2.cloned.1.call-start = ((), (), s32[]{:S(2)}) async-start(), calls=%async_computation | async-start | bytes 14868480 | tf_op jit(solution)/shard_map/all_gather | solution.py:161
  193.6 22.1 %collective-permute-start.3 = (bf16[2560,2816]{1,0:T(8,128)(2,1)}, bf16[2560,2816]{1,0:T(8,128)(2,1)}, u32[]{:S(2)}, u32[]{:S(2)}) collective-permute-start(bf16[2560,2816]{1,0:T(8,128)(2,1)} %all-gather.2.cloned.1.call-done), channel_id=1, source_target_pairs={{0,1},{1,0},{2,3},{3,2},{4,5},{5,4},{6,7},{7,6},{8,9},{9,8},{10,11... | collective-permute-start | bytes 43253768 | tf_op jit(solution)/shard_map/ppermute | solution.py:162
  193.6 49.0 %collective-permute-start = (bf16[2048,192]{0,1:T(8,128)(2,1)}, bf16[2048,192]{0,1:T(8,128)(2,1)}, u32[]{:S(2)}, u32[]{:S(2)}) collective-permute-start(bf16[2048,192]{0,1:T(8,128)(2,1)} %param.12), channel_id=1, source_target_pairs={{0,1},{1,0},{2,3},{3,2},{4,5},{5,4},{6,7},{7,6},{8,9},{9,8},{10,11... | collective-permute-start | bytes 2359304 | tf_op jit(solution)/shard_map/ppermute | solution.py:164
  194.1 48.5 %collective-permute-start.1 = (bf16[2048,192]{0,1:T(8,128)(2,1)}, bf16[2048,192]{0,1:T(8,128)(2,1)}, u32[]{:S(2)}, u32[]{:S(2)}) collective-permute-start(bf16[2048,192]{0,1:T(8,128)(2,1)} %param.12), channel_id=1, source_target_pairs={{0,2},{1,3},{2,0},{3,1},{4,6},{5,7},{6,4},{7,5},{8,10},{9,11},{10,... | collective-permute-start | bytes 2359304 | tf_op jit(solution)/shard_map/ppermute | solution.py:164
  197.5 45.1 %collective-permute-start.2 = (bf16[2048,192]{0,1:T(8,128)(2,1)}, bf16[2048,192]{0,1:T(8,128)(2,1)}, u32[]{:S(2)}, u32[]{:S(2)}) collective-permute-start(bf16[2048,192]{0,1:T(8,128)(2,1)} %param.12), channel_id=1, source_target_pairs={{0,3},{1,2},{2,1},{3,0},{4,7},{5,6},{6,5},{7,4},{8,11},{9,10},{10,... | collective-permute-start | bytes 2359304 | tf_op jit(solution)/shard_map/ppermute | solution.py:164
  200.0 2.1 copy-start.5
  234.6 8.0 %copy-start.3 = (bf16[256,2048]{1,0:T(8,128)(2,1)S(1)}, bf16[256,2048]{1,0:T(8,128)(2,1)}, u32[]{:S(2)}) copy-start(bf16[256,2048]{1,0:T(8,128)(2,1)} %param.8) | copy-start | bytes 3145732
  234.6 8.0 %copy-start.6 = (bf16[2048,192]{0,1:T(8,128)(2,1)S(1)}, bf16[2048,192]{0,1:T(8,128)(2,1)}, u32[]{:S(2)}) copy-start(bf16[2048,192]{0,1:T(8,128)(2,1)} %param.12) | copy-start | bytes 2359300
  252.7 36.1 %copy-start.1 = (bf16[88,2048]{1,0:T(8,128)(2,1)S(1)}, bf16[88,2048]{1,0:T(8,128)(2,1)}, u32[]{:S(2)}) copy-start(bf16[88,2048]{1,0:T(8,128)(2,1)} %param.11) | copy-start | bytes 1081348
Sparse Core Ops, SparseCore 0:
  9.5 184.0 all-gather.1

commit v10 on v9

--- a/solution.py
+++ b/solution.py
@@ -57,9 +57,9 @@
         for j in range(sb):
             s = step * sb + j
             start = x0_ref[s]
-            base = pl.multiple_of((start // 8) * 8, 8)
-            wide = spec_ref[pl.ds(base, W + 8), pl.ds(k * 2 * ORD, 2 * ORD)]
-            rows = pltpu.roll(wide, (W + 8 - (start - base)) % (W + 8), 0)[:W]
+            base = pl.multiple_of((start // 16) * 16, 16)
+            wide = spec_ref[pl.ds(base, W + 16), pl.ds(k * 2 * ORD, 2 * ORD)].astype(f32)
+            rows = pltpu.roll(wide, (W + 16 - (start - base)) % (W + 16), 0)[:W]
             xs[j * W:(j + 1) * W, :] = jnp.where(keeps[j], rows, 0.0).astype(bf16)
         y = jnp.dot(xs[...], t1_ref[...], preferred_element_type=f32)
         h = y[:, : 2 * PIX] + y[:, 2 * PIX:]
@@ -110,7 +110,7 @@
         grid=(S // sb,),
         in_specs=[smem] * 4
         + [
-            pl.BlockSpec((ORD + 8, 12 * ORD), lambda s: (0, 0)),
+            pl.BlockSpec((ORD + 16, 12 * ORD), lambda s: (0, 0)),
             pl.BlockSpec((2 * ORD, 4 * PIX), lambda s: (0, 0)),
             pl.BlockSpec((2 * PIX, 4 * W), lambda s: (0, 0)),
         ],
@@ -122,7 +122,7 @@
     for t in range(T):
         outs.append(
             call(
-                source_weight.astype(f32), x0, y0, source_cutoff, jnp.pad(spec_rows[t].astype(f32), ((0, 8), (0, 0))), t1s, t2c
+                source_weight.astype(f32), x0, y0, source_cutoff, jnp.pad(spec_rows[t], ((0, 16), (0, 0))), t1s, t2c
             )[:, :PIX]
         )
     power = jnp.stack(outs, 0)

time: 297 us -> 301 us (1.013)
  Pallas kernels: 27.5 us -> 31.6 us
    convert_element_type x3 -> x0, local copies, waits for them, and re-layouts: 12.1 us -> none  [imaging(): spec_rows[t].astype(f32)]
    another operation x0 -> x3, local copies, waits for them, and re-layouts: none -> 12.1 us  [the longest x1 6.15 us: imaging(): spec_rows[t]]
    pallas_call x1, Pallas kernels: 27.5 us -> 31.6 us  [imaging(): call(source_weight.astype(f32), x0, y0, source_cutoff, jnp.pad(spec_rows[...]
  transfers between devices with their start and end apart: 5 -> 5, of which waited for: 2 -> 2; matrix products, arithmetic and copies ran while one was open for 14% -> 13% of each run, Pallas kernels for 0% -> 0%
where the time goes in v10:
time: 301 us; the launch traced here: 300 us
  waiting for transfers between devices  189 us (63%)
  matrix products  35.7 us (12%)
  Pallas kernels  31.6 us (10%)
  local copies, waits for them, and re-layouts  18.5 us (6%)
  between operations  13.7 us (5%)
  other arithmetic  7.08 us (2%)
  starting transfers between devices  3.89 us (1%)
    all_gather x1, waiting for transfers between devices, local(): gathered = lax.all_gather(packed, 'tile', axis=0, tiled=True)  184 us
    pallas_call x1, Pallas kernels, imaging(): call(source_weight.astype(f32), x0, y0, source_cutoff, jnp.pad(spec_rows[...  31.6 us
    dot_general x1, matrix products, local(): jnp.dot(normed_other, sibling, preferred_element_type=jnp.float32)  9.91 us
    dot_general x1, matrix products, local(): jnp.dot(hidden_other, sibling, preferred_element_type=jnp.float32)  7.95 us
    dot_general x1, matrix products, local(): jnp.dot(hidden_mine, gathered, preferred_element_type=jnp.float32)  7.64 us
    dot_general x1, matrix products, local(): jnp.dot(normed_mine, gathered, preferred_element_type=jnp.float32)  7.53 us
    another operation x1, local copies, waits for them, and re-layouts, imaging(): spec_rows[t]  6.15 us
  transfers between devices with their start and end apart: 5, of which 2 were waited for; matrix products, arithmetic and copies ran while one was open for 13% of the time, Pallas kernels for 0%

profile of v10, /device:TPU:0, one launch (start us, length us, event | category | flops | bytes accessed | tf_op | source)
XLA Modules:
  0.0 299.6 jit_solution(4489204799697314846)
XLA Ops:
  6.6 1.0 copy-done
  7.5 0.1 constant_dynamic-slice_fusion
  7.6 0.9 constant_dynamic-slice_fusion.1
  8.5 0.8 fusion.29
  9.3 0.0 all-gather.2.cloned.1.call-update
  9.4 184.2 %all-gather.2.cloned.1.call-done = bf16[2560,2816]{1,0:T(8,128)(2,1)} async-done(((bf16[80,2816]{1,0:T(8,128)(2,1)}), bf16[2560,2816]{1,0:T(8,128)(2,1)}) %all-gather.2.cloned.1.call-update) | async-done | bytes 14417936 | tf_op jit(solution)/shard_map/all_gather | solution.py:161
  193.6 0.5 collective-permute-start
  194.1 3.4 %collective-permute-start.1 = (bf16[2048,192]{0,1:T(8,128)(2,1)}, bf16[2048,192]{0,1:T(8,128)(2,1)}, u32[]{:S(2)}, u32[]{:S(2)}) collective-permute-start(bf16[2048,192]{0,1:T(8,128)(2,1)} %param.12), channel_id=1, source_target_pairs={{0,2},{1,3},{2,0},{3,1},{4,6},{5,7},{6,4},{7,5},{8,10},{9,11},{10,... | collective-permute-start | bytes 2359304 | tf_op jit(solution)/shard_map/ppermute | solution.py:164
  197.5 1.5 fusion.16
  199.0 0.3 fusion.18
  199.3 0.5 copy.29
  199.9 0.1 dynamic-slice_bitcast_fusion.2
  200.0 0.0 copy-start.5
  200.0 0.1 pad.22
  200.1 0.1 pad.24
  200.2 0.1 fusion.46
  200.3 0.1 fusion.50
  200.3 0.1 copy.37
  200.4 0.1 copy.38
  200.6 0.3 fusion.39
  200.8 0.3 fusion.37
  201.1 0.1 maximum_maximum_fusion
  201.3 0.1 pad.31.clone
  201.4 0.7 pad_maximum_fusion.t1_ref
  202.1 0.6 clamp_bitcast_fusion
  202.7 0.7 maximum_maximum_fusion.1.t2_ref
  203.4 7.5 %fusion.52 = f32[256,2816]{1,0:T(8,128)S(1)} fusion(bf16[256,2560]{0,1:T(8,128)(2,1)S(1)} %bitcast.56, bf16[2560,2816]{1,0:T(8,128)(2,1)} %all-gather.2.cloned.1.call-done), kind=kOutput, calls=%fused_computation.84 | convolution fusion | flops 3690987520 | bytes 18612224 | tf_op jit(solution)/shard_map/dot_general | solution.py:179
  210.9 4.8 %collective-permute-done.3 = bf16[2560,2816]{1,0:T(8,128)(2,1)} collective-permute-done((bf16[2560,2816]{1,0:T(8,128)(2,1)}, bf16[2560,2816]{1,0:T(8,128)(2,1)}, u32[]{:S(2)}, u32[]{:S(2)}) %collective-permute-start.3) | collective-permute-done | bytes 14417952 | tf_op jit(solution)/shard_map/ppermute | solution.py:162
  215.7 9.9 %fusion.15 = bf16[256,2816]{1,0:T(8,128)(2,1)S(1)} fusion(f32[256,2816]{1,0:T(8,128)S(1)} %fusion.52, bf16[256,2560]{0,1:T(8,128)(2,1)S(1)} %bitcast.60, bf16[2560,2816]{1,0:T(8,128)(2,1)} %collective-permute-done.3), kind=kOutput, calls=%fused_computation.22 | convolution fusion | flops 3698196480 | bytes 20054016 | tf_op jit(solution)/shard_map/dot_general | solution.py:179
  225.6 0.7 copy.30
  226.3 0.3 reshape.77
  226.7 0.1 dynamic-slice_bitcast_fusion.1
  226.8 0.1 pad.25.clone
  226.9 0.1 pad.26.clone
  227.0 7.6 %fusion.53 = f32[256,2816]{1,0:T(8,128)S(1)} fusion(bf16[256,2560]{0,1:T(8,128)(2,1)S(1)} %bitcast.57, bf16[2560,2816]{1,0:T(8,128)(2,1)} %all-gather.2.cloned.1.call-done), kind=kOutput, calls=%fused_computation.85 | convolution fusion | flops 3690987520 | bytes 18612224 | tf_op jit(solution)/shard_map/dot_general | solution.py:184
  234.6 0.0 copy-start.3
  234.7 8.0 %fusion.54 = f32[256,2816]{1,0:T(8,128)S(1)} fusion(bf16[256,2560]{0,1:T(8,128)(2,1)S(1)} %bitcast.58, bf16[2560,2816]{1,0:T(8,128)(2,1)} %collective-permute-done.3), kind=kOutput, calls=%fused_computation.86 | convolution fusion | flops 3690987520 | bytes 18612224 | tf_op jit(solution)/shard_map/dot_general | solution.py:184
  242.7 2.7 fusion.23
  245.3 0.6 gather_fusion
  245.9 0.8 select_bitcast_fusion
  246.8 3.5 %reshape_reshape.3 = bf16[1,16,16,6,2,8,8]{2,1,6,5,4,3,0:T(8,128)(2,1)S(1)} reshape(bf16[256,4,192]{0,2,1:T(8,128)(2,1)} %select_bitcast_fusion) | data formatting | bytes 786432 | tf_op jit(solution)/shard_map/reshape;reshape | solution.py:197
  250.3 0.0 copy-start.1
  250.3 2.5 copy.45
  252.7 6.2 %squeeze_reshape.3 = bf16[128,1536]{1,0:T(8,128)(2,1)S(1)} reshape(bf16[1,16,8,6,2,8,16]{6,5,4,3,2,1,0:T(8,128)(2,1)} %bitcast.55) | data formatting | bytes 786432 | tf_op jit(solution)/shard_map/squeeze;reshape | solution.py:125
  258.9 0.8 pad.27.spec_ref
  259.7 31.6 %shard_map.82 = f32[64,128]{1,0:T(8,128)} custom-call(f32[128]{0:T(128)} %w_ref.1, s32[128]{0:T(128)} %get-tuple-element.16.x0_ref, s32[128]{0:T(128)} %get-tuple-element.15.y0_ref, s32[128]{0:T(128)} %r_ref.1, bf16[144,1536]{1,0:T(8,128)(2,1)} %pad.27.spec_ref, bf16[256,256]{1,0:T(8,128)(2,1)} %pad_maximum_fusion.t1_ref, ...), custom_call_target="tpu_custom_call" | custom-call | tf_op jit(solution)/shard_map/pallas_call | solution.py:124
  291.3 0.8 slice_multiply_fusion
  292.0 0.7 mul.159
  (24 shorter events, 0.1 us)
Async XLA Ops:
  6.5 1.0 copy-start
  6.5 192.5 %copy-start.2 = (bf16[256,2048]{1,0:T(8,128)(2,1)S(1)}, bf16[256,2048]{1,0:T(8,128)(2,1)}, u32[]{:S(2)}) copy-start(bf16[256,2048]{1,0:T(8,128)(2,1)} %param.8) | copy-start | bytes 3145732
  6.5 192.5 %copy-start.4 = (f32[2048]{0:T(1024)S(1)}, f32[2048]{0:T(1024)}, u32[]{:S(2)}) copy-start(f32[2048]{0:T(1024)} %param.9) | copy-start | bytes 24580
  6.5 187.1 %all-gather.2.cloned.1.call-start = ((), (), s32[]{:S(2)}) async-start(), calls=%async_computation | async-start | bytes 14868480 | tf_op jit(solution)/shard_map/all_gather | solution.py:161
  193.6 22.1 %collective-permute-start.3 = (bf16[2560,2816]{1,0:T(8,128)(2,1)}, bf16[2560,2816]{1,0:T(8,128)(2,1)}, u32[]{:S(2)}, u32[]{:S(2)}) collective-permute-start(bf16[2560,2816]{1,0:T(8,128)(2,1)} %all-gather.2.cloned.1.call-done), channel_id=1, source_target_pairs={{0,1},{1,0},{2,3},{3,2},{4,5},{5,4},{6,7},{7,6},{8,9},{9,8},{10,11... | collective-permute-start | bytes 43253768 | tf_op jit(solution)/shard_map/ppermute | solution.py:162
  193.6 49.0 %collective-permute-start = (bf16[2048,192]{0,1:T(8,128)(2,1)}, bf16[2048,192]{0,1:T(8,128)(2,1)}, u32[]{:S(2)}, u32[]{:S(2)}) collective-permute-start(bf16[2048,192]{0,1:T(8,128)(2,1)} %param.12), channel_id=1, source_target_pairs={{0,1},{1,0},{2,3},{3,2},{4,5},{5,4},{6,7},{7,6},{8,9},{9,8},{10,11... | collective-permute-start | bytes 2359304 | tf_op jit(solution)/shard_map/ppermute | solution.py:164
  194.1 48.5 %collective-permute-start.1 = (bf16[2048,192]{0,1:T(8,128)(2,1)}, bf16[2048,192]{0,1:T(8,128)(2,1)}, u32[]{:S(2)}, u32[]{:S(2)}) collective-permute-start(bf16[2048,192]{0,1:T(8,128)(2,1)} %param.12), channel_id=1, source_target_pairs={{0,2},{1,3},{2,0},{3,1},{4,6},{5,7},{6,4},{7,5},{8,10},{9,11},{10,... | collective-permute-start | bytes 2359304 | tf_op jit(solution)/shard_map/ppermute | solution.py:164
  197.5 45.1 %collective-permute-start.2 = (bf16[2048,192]{0,1:T(8,128)(2,1)}, bf16[2048,192]{0,1:T(8,128)(2,1)}, u32[]{:S(2)}, u32[]{:S(2)}) collective-permute-start(bf16[2048,192]{0,1:T(8,128)(2,1)} %param.12), channel_id=1, source_target_pairs={{0,3},{1,2},{2,1},{3,0},{4,7},{5,6},{6,5},{7,4},{8,11},{9,10},{10,... | collective-permute-start | bytes 2359304 | tf_op jit(solution)/shard_map/ppermute | solution.py:164
  200.0 2.1 copy-start.5
  234.6 8.0 %copy-start.3 = (bf16[256,2048]{1,0:T(8,128)(2,1)S(1)}, bf16[256,2048]{1,0:T(8,128)(2,1)}, u32[]{:S(2)}) copy-start(bf16[256,2048]{1,0:T(8,128)(2,1)} %param.8) | copy-start | bytes 3145732
  234.6 8.0 %copy-start.6 = (bf16[2048,192]{0,1:T(8,128)(2,1)S(1)}, bf16[2048,192]{0,1:T(8,128)(2,1)}, u32[]{:S(2)}) copy-start(bf16[2048,192]{0,1:T(8,128)(2,1)} %param.12) | copy-start | bytes 2359300
  250.3 42.5 %copy-start.1 = (bf16[88,2048]{1,0:T(8,128)(2,1)S(1)}, bf16[88,2048]{1,0:T(8,128)(2,1)}, u32[]{:S(2)}) copy-start(bf16[88,2048]{1,0:T(8,128)(2,1)} %param.11) | copy-start | bytes 1081348
Sparse Core Ops, SparseCore 0:
  9.5 184.0 all-gather.1

commit v11 on v9

--- a/solution.py
+++ b/solution.py
@@ -89,10 +89,10 @@
     def _():
         out_ref[...] = jnp.zeros_like(out_ref)
 
-    out_ref[...] += acc
-
-
-def imaging(spec_rows, source_index, source_cutoff, source_weight, sb=16):
+    out_ref[...] += acc[:, :PIX]
+
+
+def imaging(spec_rows, source_index, source_cutoff, source_weight, sb=32):
     T = spec_rows.shape[0]
     S = source_index.shape[0]
     x0 = jnp.clip(source_index[:, 0], 0, ORD - W)
@@ -106,7 +106,7 @@
     smem = pl.BlockSpec(memory_space=pltpu.SMEM)
     call = pl.pallas_call(
         functools.partial(power_kernel, sb=sb),
-        out_shape=jax.ShapeDtypeStruct((PIX, 2 * PIX), f32),
+        out_shape=jax.ShapeDtypeStruct((PIX, PIX), f32),
         grid=(S // sb,),
         in_specs=[smem] * 4
         + [
@@ -114,19 +114,20 @@
             pl.BlockSpec((2 * ORD, 4 * PIX), lambda s: (0, 0)),
             pl.BlockSpec((2 * PIX, 4 * W), lambda s: (0, 0)),
         ],
-        out_specs=pl.BlockSpec((PIX, 2 * PIX), lambda s: (0, 0)),
+        out_specs=pl.BlockSpec((PIX, PIX), lambda s: (0, 0)),
         scratch_shapes=[pltpu.VMEM((sb * W, 2 * ORD), bf16), pltpu.VMEM((4 * W, sb * 6 * 2 * PIX), bf16)],
         compiler_params=pltpu.CompilerParams(dimension_semantics=("arbitrary",)),
     )
+    scaled = source_weight.astype(f32) * (1.0 / (6.0 * W * W * S))
     outs = []
     for t in range(T):
         outs.append(
             call(
-                source_weight.astype(f32), x0, y0, source_cutoff, jnp.pad(spec_rows[t].astype(f32), ((0, 8), (0, 0))), t1s, t2c
-            )[:, :PIX]
+                scaled, x0, y0, source_cutoff, jnp.pad(spec_rows[t].astype(f32), ((0, 8), (0, 0))), t1s, t2c
+            )
         )
     power = jnp.stack(outs, 0)
-    return power.reshape(T, PIX * PIX) * (1.0 / (6.0 * W * W * S))
+    return power.reshape(T, PIX * PIX)
 
 
 def local(

time: 297 us -> 296 us (level)
  no operation moved by 1% of the time
where the time goes in v11:
time: 296 us; the launch traced here: 295 us
  waiting for transfers between devices  189 us (64%)
  matrix products  35.7 us (12%)
  Pallas kernels  26.6 us (9%)
  local copies, waits for them, and re-layouts  18.5 us (6%)
  between operations  13.7 us (5%)
  other arithmetic  7.82 us (3%)
  starting transfers between devices  3.89 us (1%)
    all_gather x1, waiting for transfers between devices, local(): gathered = lax.all_gather(packed, 'tile', axis=0, tiled=True)  184 us
    pallas_call x1, Pallas kernels, imaging(): call(scaled, x0, y0, source_cutoff, jnp.pad(spec_rows[t].astype(f32), ((0...  26.6 us
    convert_element_type x3, local copies, waits for them, and re-layouts, imaging(): spec_rows[t].astype(f32)  12.2 us
    dot_general x1, matrix products, local(): jnp.dot(normed_other, sibling, preferred_element_type=jnp.float32)  9.91 us
    dot_general x1, matrix products, local(): jnp.dot(hidden_other, sibling, preferred_element_type=jnp.float32)  7.95 us
    dot_general x1, matrix products, local(): jnp.dot(hidden_mine, gathered, preferred_element_type=jnp.float32)  7.64 us
    dot_general x1, matrix products, local(): jnp.dot(normed_mine, gathered, preferred_element_type=jnp.float32)  7.53 us
  transfers between devices with their start and end apart: 5, of which 2 were waited for; matrix products, arithmetic and copies ran while one was open for 14% of the time, Pallas kernels for 0%

profile of v11, /device:TPU:0, one launch (start us, length us, event | category | flops | bytes accessed | tf_op | source)
XLA Modules:
  0.0 294.8 jit_solution(2966497127305068747)
XLA Ops:
  6.6 1.0 copy-done
  7.5 0.1 constant_dynamic-slice_fusion
  7.6 0.9 constant_dynamic-slice_fusion.1
  8.5 0.8 fusion.29
  9.3 0.0 all-gather.2.cloned.1.call-update
  9.4 184.2 %all-gather.2.cloned.1.call-done = bf16[2560,2816]{1,0:T(8,128)(2,1)} async-done(((bf16[80,2816]{1,0:T(8,128)(2,1)}), bf16[2560,2816]{1,0:T(8,128)(2,1)}) %all-gather.2.cloned.1.call-update) | async-done | bytes 14417936 | tf_op jit(solution)/shard_map/all_gather | solution.py:162
  193.6 0.5 collective-permute-start
  194.1 3.4 %collective-permute-start.1 = (bf16[2048,192]{0,1:T(8,128)(2,1)}, bf16[2048,192]{0,1:T(8,128)(2,1)}, u32[]{:S(2)}, u32[]{:S(2)}) collective-permute-start(bf16[2048,192]{0,1:T(8,128)(2,1)} %param.12), channel_id=1, source_target_pairs={{0,2},{1,3},{2,0},{3,1},{4,6},{5,7},{6,4},{7,5},{8,10},{9,11},{10,... | collective-permute-start | bytes 2359304 | tf_op jit(solution)/shard_map/ppermute | solution.py:165
  197.5 1.5 fusion.16
  199.0 0.3 fusion.18
  199.3 0.5 copy.29
  199.9 0.1 dynamic-slice_bitcast_fusion.2
  200.0 0.0 copy-start.7
  200.0 0.0 copy-start.5
  200.0 0.1 pad.24
  200.1 0.1 pad.26
  200.2 0.1 fusion.46
  200.3 0.1 fusion.50
  200.4 0.1 copy.37
  200.5 0.1 copy.38
  200.6 0.3 fusion.39
  200.8 0.3 fusion.37
  201.1 0.1 maximum_maximum_fusion
  201.3 0.1 pad.34.clone
  201.4 0.7 pad_maximum_fusion.t1_ref
  202.1 0.5 broadcast_multiply_fusion.w_ref
  202.6 0.6 clamp_bitcast_fusion
  203.2 0.7 maximum_maximum_fusion.1.t2_ref
  203.9 7.5 %fusion.52 = f32[256,2816]{1,0:T(8,128)S(1)} fusion(bf16[256,2560]{0,1:T(8,128)(2,1)S(1)} %bitcast.56, bf16[2560,2816]{1,0:T(8,128)(2,1)} %all-gather.2.cloned.1.call-done), kind=kOutput, calls=%fused_computation.85 | convolution fusion | flops 3690987520 | bytes 18612224 | tf_op jit(solution)/shard_map/dot_general | solution.py:180
  211.4 4.3 %collective-permute-done.3 = bf16[2560,2816]{1,0:T(8,128)(2,1)} collective-permute-done((bf16[2560,2816]{1,0:T(8,128)(2,1)}, bf16[2560,2816]{1,0:T(8,128)(2,1)}, u32[]{:S(2)}, u32[]{:S(2)}) %collective-permute-start.3) | collective-permute-done | bytes 14417952 | tf_op jit(solution)/shard_map/ppermute | solution.py:163
  215.7 9.9 %fusion.15 = bf16[256,2816]{1,0:T(8,128)(2,1)S(1)} fusion(f32[256,2816]{1,0:T(8,128)S(1)} %fusion.52, bf16[256,2560]{0,1:T(8,128)(2,1)S(1)} %bitcast.60, bf16[2560,2816]{1,0:T(8,128)(2,1)} %collective-permute-done.3), kind=kOutput, calls=%fused_computation.22 | convolution fusion | flops 3698196480 | bytes 20054016 | tf_op jit(solution)/shard_map/dot_general | solution.py:180
  225.6 0.7 copy.30
  226.3 0.3 reshape.67
  226.7 0.1 dynamic-slice_bitcast_fusion.1
  226.8 0.1 pad.27.clone
  226.9 0.1 pad.28.clone
  227.0 7.6 %fusion.53 = f32[256,2816]{1,0:T(8,128)S(1)} fusion(bf16[256,2560]{0,1:T(8,128)(2,1)S(1)} %bitcast.57, bf16[2560,2816]{1,0:T(8,128)(2,1)} %all-gather.2.cloned.1.call-done), kind=kOutput, calls=%fused_computation.86 | convolution fusion | flops 3690987520 | bytes 18612224 | tf_op jit(solution)/shard_map/dot_general | solution.py:185
  234.6 0.0 copy-start.3
  234.6 8.0 %fusion.54 = f32[256,2816]{1,0:T(8,128)S(1)} fusion(bf16[256,2560]{0,1:T(8,128)(2,1)S(1)} %bitcast.58, bf16[2560,2816]{1,0:T(8,128)(2,1)} %collective-permute-done.3), kind=kOutput, calls=%fused_computation.87 | convolution fusion | flops 3690987520 | bytes 18612224 | tf_op jit(solution)/shard_map/dot_general | solution.py:185
  242.7 2.7 fusion.23
  245.3 0.6 gather_fusion
  245.9 0.9 select_bitcast_fusion
  246.8 3.5 %convert_element_type.74 = bf16[1,16,16,6,2,8,8]{2,1,6,5,4,3,0:T(8,128)(2,1)S(1)} reshape(bf16[256,4,192]{0,2,1:T(8,128)(2,1)} %select_bitcast_fusion) | data formatting | bytes 786432 | tf_op jit(solution)/shard_map/convert_element_type | solution.py:126
  250.3 2.5 copy.45
  252.7 6.2 %convert_element_type.76 = bf16[128,1536]{1,0:T(8,128)(2,1)S(1)} reshape(bf16[1,16,8,6,2,8,16]{6,5,4,3,2,1,0:T(8,128)(2,1)} %bitcast.55) | data formatting | bytes 786432 | tf_op jit(solution)/shard_map/convert_element_type | solution.py:126
  258.9 1.0 pad_convert_fusion.spec_ref
  259.9 26.6 %shard_map.82 = f32[64,64]{1,0:T(8,128)} custom-call(f32[128]{0:T(128)} %broadcast_multiply_fusion.w_ref, s32[128]{0:T(128)} %get-tuple-element.16.x0_ref, s32[128]{0:T(128)} %get-tuple-element.15.y0_ref, s32[128]{0:T(128)} %r_ref.1, f32[136,1536]{1,0:T(8,128)} %pad_convert_fusion.spec_ref, bf16[256,256]{1,0:T(8,128)(2,1)} %pad_maximum_fusion.t1_ref, ...), custom_call_target="tpu_custom_call" | custom-call | tf_op jit(solution)/shard_map/pallas_call | solution.py:125
  286.6 1.4 reshape_stack.3
  (26 shorter events, 0.1 us)
Async XLA Ops:
  6.5 1.0 copy-start
  6.5 192.5 %copy-start.2 = (bf16[256,2048]{1,0:T(8,128)(2,1)S(1)}, bf16[256,2048]{1,0:T(8,128)(2,1)}, u32[]{:S(2)}) copy-start(bf16[256,2048]{1,0:T(8,128)(2,1)} %param.8) | copy-start | bytes 3145732
  6.5 192.5 %copy-start.4 = (f32[2048]{0:T(1024)S(1)}, f32[2048]{0:T(1024)}, u32[]{:S(2)}) copy-start(f32[2048]{0:T(1024)} %param.9) | copy-start | bytes 24580
  6.5 187.1 %all-gather.2.cloned.1.call-start = ((), (), s32[]{:S(2)}) async-start(), calls=%async_computation | async-start | bytes 14868480 | tf_op jit(solution)/shard_map/all_gather | solution.py:162
  193.6 22.1 %collective-permute-start.3 = (bf16[2560,2816]{1,0:T(8,128)(2,1)}, bf16[2560,2816]{1,0:T(8,128)(2,1)}, u32[]{:S(2)}, u32[]{:S(2)}) collective-permute-start(bf16[2560,2816]{1,0:T(8,128)(2,1)} %all-gather.2.cloned.1.call-done), channel_id=1, source_target_pairs={{0,1},{1,0},{2,3},{3,2},{4,5},{5,4},{6,7},{7,6},{8,9},{9,8},{10,11... | collective-permute-start | bytes 43253768 | tf_op jit(solution)/shard_map/ppermute | solution.py:163
  193.6 49.0 %collective-permute-start = (bf16[2048,192]{0,1:T(8,128)(2,1)}, bf16[2048,192]{0,1:T(8,128)(2,1)}, u32[]{:S(2)}, u32[]{:S(2)}) collective-permute-start(bf16[2048,192]{0,1:T(8,128)(2,1)} %param.12), channel_id=1, source_target_pairs={{0,1},{1,0},{2,3},{3,2},{4,5},{5,4},{6,7},{7,6},{8,9},{9,8},{10,11... | collective-permute-start | bytes 2359304 | tf_op jit(solution)/shard_map/ppermute | solution.py:165
  194.1 48.5 %collective-permute-start.1 = (bf16[2048,192]{0,1:T(8,128)(2,1)}, bf16[2048,192]{0,1:T(8,128)(2,1)}, u32[]{:S(2)}, u32[]{:S(2)}) collective-permute-start(bf16[2048,192]{0,1:T(8,128)(2,1)} %param.12), channel_id=1, source_target_pairs={{0,2},{1,3},{2,0},{3,1},{4,6},{5,7},{6,4},{7,5},{8,10},{9,11},{10,... | collective-permute-start | bytes 2359304 | tf_op jit(solution)/shard_map/ppermute | solution.py:165
  197.5 45.1 %collective-permute-start.2 = (bf16[2048,192]{0,1:T(8,128)(2,1)}, bf16[2048,192]{0,1:T(8,128)(2,1)}, u32[]{:S(2)}, u32[]{:S(2)}) collective-permute-start(bf16[2048,192]{0,1:T(8,128)(2,1)} %param.12), channel_id=1, source_target_pairs={{0,3},{1,2},{2,1},{3,0},{4,7},{5,6},{6,5},{7,4},{8,11},{9,10},{10,... | collective-permute-start | bytes 2359304 | tf_op jit(solution)/shard_map/ppermute | solution.py:165
  200.0 2.1 copy-start.7
  200.0 2.6 copy-start.5
  234.6 8.0 %copy-start.3 = (bf16[256,2048]{1,0:T(8,128)(2,1)S(1)}, bf16[256,2048]{1,0:T(8,128)(2,1)}, u32[]{:S(2)}) copy-start(bf16[256,2048]{1,0:T(8,128)(2,1)} %param.8) | copy-start | bytes 3145732
  234.6 8.0 %copy-start.6 = (bf16[2048,192]{0,1:T(8,128)(2,1)S(1)}, bf16[2048,192]{0,1:T(8,128)(2,1)}, u32[]{:S(2)}) copy-start(bf16[2048,192]{0,1:T(8,128)(2,1)} %param.12) | copy-start | bytes 2359300
  252.7 35.3 %copy-start.1 = (bf16[88,2048]{1,0:T(8,128)(2,1)S(1)}, bf16[88,2048]{1,0:T(8,128)(2,1)}, u32[]{:S(2)}) copy-start(bf16[88,2048]{1,0:T(8,128)(2,1)} %param.11) | copy-start | bytes 1081348
Sparse Core Ops, SparseCore 0:
  9.5 184.0 all-gather.1

commit v12 on v11

--- a/solution.py
+++ b/solution.py
@@ -188,11 +188,9 @@
     branch_out = branch_out[:, :d_model]
     mixed = (residual + branch_out).astype(jnp.bfloat16)
     parts = jnp.stack(head_parts, 0)
-    coeff_parts = jnp.einsum("tk,pkc->ptc", mixed, parts, preferred_element_type=jnp.float32).astype(
-        jnp.bfloat16
-    )
     order = me ^ jnp.arange(n_src, dtype=jnp.int32)
-    coeffs = jnp.take(coeff_parts, order, axis=0).transpose(1, 0, 2).reshape(token_count, -1)
+    head_full = jnp.take(parts, order, axis=0).transpose(1, 0, 2).reshape(d_model, -1)
+    coeffs = jnp.dot(mixed, head_full, preferred_element_type=jnp.float32).astype(jnp.bfloat16)
     tile_count = token_count // PATCH
     spec_rows = (
         coeffs.reshape(tile_count, GRID, GRID, 6, 2, SUB, SUB)

time: 296 us -> 332 us (1.12)
  waiting for transfers between devices: 189 us -> 210 us
  local copies, waits for them, and re-layouts: 18.5 us -> 31.6 us
  other arithmetic: 7.82 us -> 11.4 us
    ppermute x3, waiting for transfers between devices: 0.01 us -> 25.6 us  [local(): lax.ppermute(head_weight, 'src', [(s, s ^ k) for s in range(n_src)])]
    ppermute x1, waiting for transfers between devices: 4.28 us -> 0.01 us  [local(): sibling = lax.ppermute(gathered, 'src', [(s, s ^ 1) for s in range(n_src)])]
    dot_general x1, matrix products: 7.64 us -> 3.99 us  [local(): jnp.dot(hidden_mine, gathered, preferred_element_type=jnp.float32)]
  transfers between devices with their start and end apart: 5 -> 5, of which waited for: 2 -> 3; matrix products, arithmetic and copies ran while one was open for 14% -> 7% of each run, Pallas kernels for 0% -> 0%
where the time goes in v12:
time: 332 us; the launch traced here: 330 us
  waiting for transfers between devices  210 us (63%)
  matrix products  32.5 us (10%)
  local copies, waits for them, and re-layouts  31.6 us (10%)
  Pallas kernels  26.6 us (8%)
  between operations  13.7 us (4%)
  other arithmetic  11.4 us (3%)
  starting transfers between devices  3.89 us (1%)
    all_gather x1, waiting for transfers between devices, local(): gathered = lax.all_gather(packed, 'tile', axis=0, tiled=True)  184 us
    pallas_call x1, Pallas kernels, imaging(): call(scaled, x0, y0, source_cutoff, jnp.pad(spec_rows[t].astype(f32), ((0...  26.6 us
    ppermute x3, waiting for transfers between devices, local(): lax.ppermute(head_weight, 'src', [(s, s ^ k) for s in range(n_src)])  25.6 us
    convert_element_type x3, local copies, waits for them, and re-layouts, imaging(): spec_rows[t].astype(f32)  12.1 us
    dot_general x1, matrix products, local(): jnp.dot(normed_other, sibling, preferred_element_type=jnp.float32)  10.9 us
    dot_general x1, matrix products, local(): jnp.dot(hidden_other, sibling, preferred_element_type=jnp.float32)  7.97 us
    dot_general x1, matrix products, local(): jnp.dot(normed_mine, gathered, preferred_element_type=jnp.float32)  7.75 us
  transfers between devices with their start and end apart: 5, of which 3 were waited for; matrix products, arithmetic and copies ran while one was open for 7% of the time, Pallas kernels for 0%

profile of v12, /device:TPU:0, one launch (start us, length us, event | category | flops | bytes accessed | tf_op | source)
XLA Modules:
  0.0 329.6 jit_solution(17205445997885898586)
XLA Ops:
  6.6 1.0 copy-done
  7.6 0.9 constant_dynamic-slice_fusion.1
  8.5 0.8 fusion.14
  9.4 184.2 %all-gather.2.cloned.1.call-done = bf16[2560,2816]{1,0:T(8,128)(2,1)} async-done(((bf16[80,2816]{1,0:T(8,128)(2,1)}), bf16[2560,2816]{1,0:T(8,128)(2,1)}) %all-gather.2.cloned.1.call-update) | async-done | bytes 14417936 | tf_op jit(solution)/shard_map/all_gather | solution.py:162
  193.6 0.5 collective-permute-start.1
  194.1 3.4 %collective-permute-start.2 = (bf16[2048,192]{0,1:T(8,128)(2,1)}, bf16[2048,192]{0,1:T(8,128)(2,1)}, u32[]{:S(2)}, u32[]{:S(2)}) collective-permute-start(bf16[2048,192]{0,1:T(8,128)(2,1)} %param.12), channel_id=1, source_target_pairs={{0,2},{1,3},{2,0},{3,1},{4,6},{5,7},{6,4},{7,5},{8,10},{9,11},{10,... | collective-permute-start | bytes 2359304 | tf_op jit(solution)/shard_map/ppermute | solution.py:165
  197.5 1.5 fusion.8
  199.0 0.3 fusion.10
  199.3 0.5 copy.30
  199.9 0.1 dynamic-slice_bitcast_fusion.2
  200.0 1.2 pad.24
  201.1 1.1 pad.26
  202.3 0.1 fusion.31
  202.4 0.1 fusion.34
  202.4 0.1 copy.39
  202.5 0.1 copy.40
  202.6 0.3 fusion.24
  202.9 0.3 fusion.22
  203.2 0.1 maximum_maximum_fusion
  203.3 0.1 pad.34.clone
  203.5 0.7 pad_maximum_fusion.1.t1_ref
  204.1 0.5 broadcast_multiply_fusion.w_ref
  204.7 0.6 clamp_bitcast_fusion
  205.3 0.7 maximum_maximum_fusion.1.t2_ref
  206.0 10.3 %collective-permute-done.2 = bf16[2048,192]{0,1:T(8,128)(2,1)} collective-permute-done((bf16[2048,192]{0,1:T(8,128)(2,1)}, bf16[2048,192]{0,1:T(8,128)(2,1)}, u32[]{:S(2)}, u32[]{:S(2)}) %collective-permute-start.2) | collective-permute-done | bytes 786464 | tf_op jit(solution)/shard_map/ppermute | solution.py:165
  216.3 15.3 %collective-permute-done.3 = bf16[2048,192]{0,1:T(8,128)(2,1)} collective-permute-done((bf16[2048,192]{0,1:T(8,128)(2,1)}, bf16[2048,192]{0,1:T(8,128)(2,1)}, u32[]{:S(2)}, u32[]{:S(2)}) %collective-permute-start.3) | collective-permute-done | bytes 786464 | tf_op jit(solution)/shard_map/ppermute | solution.py:165
  231.6 2.0 pad_maximum_fusion
  233.7 2.4 gather_fusion
  236.1 2.4 broadcast_select_fusion
  238.5 7.7 %fusion.36 = f32[256,2816]{1,0:T(8,128)S(1)} fusion(bf16[256,2560]{0,1:T(8,128)(2,1)S(1)} %bitcast.54, bf16[2560,2816]{1,0:T(8,128)(2,1)} %all-gather.2.cloned.1.call-done), kind=kOutput, calls=%fused_computation.74 | convolution fusion | flops 3690987520 | bytes 18612224 | tf_op jit(solution)/shard_map/dot_general | solution.py:180
  246.2 10.9 %fusion.7 = bf16[256,2816]{1,0:T(8,128)(2,1)} fusion(f32[256,2816]{1,0:T(8,128)S(1)} %fusion.36, bf16[256,2560]{0,1:T(8,128)(2,1)S(1)} %bitcast.58, bf16[2560,2816]{1,0:T(8,128)(2,1)} %collective-permute-done), kind=kOutput, calls=%fused_computation.15 | convolution fusion | flops 3698196480 | bytes 20054016 | tf_op jit(solution)/shard_map/dot_general | solution.py:180
  257.1 2.5 copy.31
  259.7 3.2 reshape.71
  262.9 1.5 dynamic-slice_bitcast_fusion.1
  264.4 0.1 pad.28.clone
  264.5 0.1 pad.27.clone
  264.6 8.0 %fusion.38 = f32[256,2816]{1,0:T(8,128)S(1)} fusion(bf16[256,2560]{0,1:T(8,128)(2,1)S(1)} %bitcast.55, bf16[2560,2816]{1,0:T(8,128)(2,1)} %collective-permute-done), kind=kOutput, calls=%fused_computation.76 | convolution fusion | flops 3690987520 | bytes 18612224 | tf_op jit(solution)/shard_map/dot_general | solution.py:185
  272.6 0.6 slice-done.2
  273.2 0.5 slice-done.3
  273.7 4.0 %fusion.37 = f32[256,2816]{1,0:T(8,128)S(1)} fusion(bf16[256,2560]{0,1:T(8,128)(2,1)S(1)} %bitcast.56, bf16[2560,2816]{1,0:T(8,128)(2,1)S(1)} %bitcast.51), kind=kOutput, calls=%fused_computation.75 | convolution fusion | flops 3690987520 | bytes 18612224 | tf_op jit(solution)/shard_map/dot_general | solution.py:185
  277.7 1.9 convolution_convert_fusion
  279.6 1.9 copy.36
  281.5 3.5 %convert_element_type.66 = bf16[1,16,16,6,2,8,8]{2,1,6,5,4,3,0:T(8,128)(2,1)S(1)} reshape(bf16[256,768]{0,1:T(8,128)(2,1)} %copy.36) | data formatting | bytes 786432 | tf_op jit(solution)/shard_map/convert_element_type | solution.py:126
  285.0 2.4 copy.37
  287.5 6.2 %convert_element_type.68 = bf16[128,1536]{1,0:T(8,128)(2,1)S(1)} reshape(bf16[1,16,8,6,2,8,16]{6,5,4,3,2,1,0:T(8,128)(2,1)} %copy.37) | data formatting | bytes 786432 | tf_op jit(solution)/shard_map/convert_element_type | solution.py:126
  293.6 1.0 pad_convert_fusion.spec_ref
  294.6 26.6 %shard_map.82 = f32[64,64]{1,0:T(8,128)} custom-call(f32[128]{0:T(128)} %broadcast_multiply_fusion.w_ref, s32[128]{0:T(128)} %get-tuple-element.16.x0_ref, s32[128]{0:T(128)} %get-tuple-element.15.y0_ref, s32[128]{0:T(128)} %r_ref.1, f32[136,1536]{1,0:T(8,128)} %pad_convert_fusion.spec_ref, bf16[256,256]{1,0:T(8,128)(2,1)} %pad_maximum_fusion.1.t1_ref, ...), custom_call_target="tpu_custom_call" | custom-call | tf_op jit(solution)/shard_map/pallas_call | solution.py:125
  321.3 1.4 reshape_stack.3
  (41 shorter events, 0.2 us)
Async XLA Ops:
  6.5 1.0 copy-start
  6.5 192.5 %copy-start.2 = (bf16[256,2048]{1,0:T(8,128)(2,1)S(1)}, bf16[256,2048]{1,0:T(8,128)(2,1)}, u32[]{:S(2)}) copy-start(bf16[256,2048]{1,0:T(8,128)(2,1)} %param.8) | copy-start | bytes 3145732
  6.5 192.5 %copy-start.7 = (f32[2048]{0:T(1024)S(1)}, f32[2048]{0:T(1024)}, u32[]{:S(2)}) copy-start(f32[2048]{0:T(1024)} %param.9) | copy-start | bytes 24580
  6.5 187.0 %all-gather.2.cloned.1.call-start = ((), (), s32[]{:S(2)}) async-start(), calls=%async_computation | async-start | bytes 14868480 | tf_op jit(solution)/shard_map/all_gather | solution.py:162
  193.6 52.6 %collective-permute-start = (bf16[2560,2816]{1,0:T(8,128)(2,1)}, bf16[2560,2816]{1,0:T(8,128)(2,1)}, u32[]{:S(2)}, u32[]{:S(2)}) collective-permute-start(bf16[2560,2816]{1,0:T(8,128)(2,1)} %all-gather.2.cloned.1.call-done), channel_id=1, source_target_pairs={{0,1},{1,0},{2,3},{3,2},{4,5},{5,4},{6,7},{7,6},{8,9},{9,8},{10,11... | collective-permute-start | bytes 43253768 | tf_op jit(solution)/shard_map/ppermute | solution.py:163
  193.6 12.4 %collective-permute-start.1 = (bf16[2048,192]{0,1:T(8,128)(2,1)}, bf16[2048,192]{0,1:T(8,128)(2,1)S(1)}, u32[]{:S(2)}, u32[]{:S(2)}) collective-permute-start(bf16[2048,192]{0,1:T(8,128)(2,1)} %param.12), channel_id=1, source_target_pairs={{0,1},{1,0},{2,3},{3,2},{4,5},{5,4},{6,7},{7,6},{8,9},{9,8},{10,11... | collective-permute-start | bytes 2359304 | tf_op jit(solution)/shard_map/ppermute | solution.py:165
  194.1 22.2 %collective-permute-start.2 = (bf16[2048,192]{0,1:T(8,128)(2,1)}, bf16[2048,192]{0,1:T(8,128)(2,1)}, u32[]{:S(2)}, u32[]{:S(2)}) collective-permute-start(bf16[2048,192]{0,1:T(8,128)(2,1)} %param.12), channel_id=1, source_target_pairs={{0,2},{1,3},{2,0},{3,1},{4,6},{5,7},{6,4},{7,5},{8,10},{9,11},{10,... | collective-permute-start | bytes 2359304 | tf_op jit(solution)/shard_map/ppermute | solution.py:165
  197.5 34.1 %collective-permute-start.3 = (bf16[2048,192]{0,1:T(8,128)(2,1)}, bf16[2048,192]{0,1:T(8,128)(2,1)}, u32[]{:S(2)}, u32[]{:S(2)}) collective-permute-start(bf16[2048,192]{0,1:T(8,128)(2,1)} %param.12), channel_id=1, source_target_pairs={{0,3},{1,2},{2,1},{3,0},{4,7},{5,6},{6,5},{7,4},{8,11},{9,10},{10,... | collective-permute-start | bytes 2359304 | tf_op jit(solution)/shard_map/ppermute | solution.py:165
  200.0 4.2 %copy-start.9 = (f32[128]{0:T(128)S(1)}, f32[128]{0:T(128)}, u32[]{:S(2)}) copy-start(f32[128]{0:T(128)} %param.15) | copy-start | bytes 1540
  200.0 4.7 %copy-start.8 = (s32[128,2]{0,1:T(2,128)S(1)}, s32[128,2]{0,1:T(2,128)}, u32[]{:S(2)}) copy-start(s32[128,2]{0,1:T(2,128)} %param.13) | copy-start | bytes 3076
  206.0 25.6 %copy-start.6 = (bf16[2048,192]{0,1:T(8,128)(2,1)}, bf16[2048,192]{0,1:T(8,128)(2,1)S(1)}, u32[]{:S(2)}) copy-start(bf16[2048,192]{0,1:T(8,128)(2,1)S(1)} %collective-permute-done.1) | copy-start | bytes 2359300
  236.1 2.4 copy-start.4
  238.4 7.8 %copy-start.5 = (bf16[256,32,80]{0,2,1:T(8,128)(2,1)S(1)}, bf16[256,32,80]{0,2,1:T(8,128)(2,1)}, u32[]{:S(2)}) copy-start(bf16[256,32,80]{0,2,1:T(8,128)(2,1)} %pad.26) | copy-start | bytes 3932164
  264.4 8.2 %slice-start = ((s8[14417920]{0:T(1024)(128)(4,1)}), s8[4194304]{0:T(1024)(128)(4,1)S(1)}, s32[]{:S(2)}) async-start(s8[14417920]{0:T(1024)(128)(4,1)} %bitcast.50), calls=%async_computation.1 | async-start | bytes 8388608
  264.6 8.0 %slice-start.1 = ((s8[14417920]{0:T(1024)(128)(4,1)}), s8[4194304]{0:T(1024)(128)(4,1)S(1)}, s32[]{:S(2)}) async-start(s8[14417920]{0:T(1024)(128)(4,1)} %bitcast.50), calls=%async_computation.2 | async-start | bytes 8388608
  264.6 8.6 %slice-start.2 = ((s8[14417920]{0:T(1024)(128)(4,1)}), s8[4194304]{0:T(1024)(128)(4,1)S(1)}, s32[]{:S(2)}) async-start(s8[14417920]{0:T(1024)(128)(4,1)} %bitcast.50), calls=%async_computation.3 | async-start | bytes 8388608
  264.6 9.1 %slice-start.3 = ((s8[14417920]{0:T(1024)(128)(4,1)}), s8[1835008]{0:T(1024)(128)(4,1)S(1)}, s32[]{:S(2)}) async-start(s8[14417920]{0:T(1024)(128)(4,1)} %bitcast.50), calls=%async_computation.4 | async-start | bytes 3670016
  273.7 4.0 %copy-start.3 = (bf16[256,2048]{1,0:T(8,128)(2,1)S(1)}, bf16[256,2048]{1,0:T(8,128)(2,1)}, u32[]{:S(2)}) copy-start(bf16[256,2048]{1,0:T(8,128)(2,1)} %param.8) | copy-start | bytes 3145732
  285.0 37.7 %copy-start.1 = (bf16[88,2048]{1,0:T(8,128)(2,1)S(1)}, bf16[88,2048]{1,0:T(8,128)(2,1)}, u32[]{:S(2)}) copy-start(bf16[88,2048]{1,0:T(8,128)(2,1)} %param.11) | copy-start | bytes 1081348
Sparse Core Ops, SparseCore 0:
  9.5 184.0 all-gather.1

commit v13 on v11

--- a/solution.py
+++ b/solution.py
@@ -57,7 +57,7 @@
         for j in range(sb):
             s = step * sb + j
             start = x0_ref[s]
-            base = pl.multiple_of((start // 8) * 8, 8)
+            base = pl.multiple_of(jnp.minimum((start // 8) * 8, ORD - W - 8), 8)
             wide = spec_ref[pl.ds(base, W + 8), pl.ds(k * 2 * ORD, 2 * ORD)]
             rows = pltpu.roll(wide, (W + 8 - (start - base)) % (W + 8), 0)[:W]
             xs[j * W:(j + 1) * W, :] = jnp.where(keeps[j], rows, 0.0).astype(bf16)
@@ -110,7 +110,7 @@
         grid=(S // sb,),
         in_specs=[smem] * 4
         + [
-            pl.BlockSpec((ORD + 8, 12 * ORD), lambda s: (0, 0)),
+            pl.BlockSpec((ORD, 12 * ORD), lambda s: (0, 0)),
             pl.BlockSpec((2 * ORD, 4 * PIX), lambda s: (0, 0)),
             pl.BlockSpec((2 * PIX, 4 * W), lambda s: (0, 0)),
         ],
@@ -123,7 +123,7 @@
     for t in range(T):
         outs.append(
             call(
-                scaled, x0, y0, source_cutoff, jnp.pad(spec_rows[t].astype(f32), ((0, 8), (0, 0))), t1s, t2c
+                scaled, x0, y0, source_cutoff, spec_rows[t].astype(f32), t1s, t2c
             )
         )
     power = jnp.stack(outs, 0)

time: 296 us -> 301 us (1.017)
  local copies, waits for them, and re-layouts: 18.5 us -> 24.7 us
    convert_element_type x3, local copies, waits for them, and re-layouts: 12.2 us -> 18.4 us  [imaging(): spec_rows[t].astype(f32)]
where the time goes in v13:
time: 301 us; the launch traced here: 300 us
  waiting for transfers between devices  189 us (63%)
  matrix products  35.7 us (12%)
  Pallas kernels  27 us (9%)
  local copies, waits for them, and re-layouts  24.7 us (8%)
  between operations  13.7 us (5%)
  other arithmetic  6.11 us (2%)
  starting transfers between devices  3.89 us (1%)
    all_gather x1, waiting for transfers between devices, local(): gathered = lax.all_gather(packed, 'tile', axis=0, tiled=True)  184 us
    pallas_call x1, Pallas kernels, imaging(): call(scaled, x0, y0, source_cutoff, spec_rows[t].astype(f32), t1s, t2c)  27 us
    convert_element_type x3, local copies, waits for them, and re-layouts, imaging(): spec_rows[t].astype(f32)  18.4 us
    dot_general x1, matrix products, local(): jnp.dot(normed_other, sibling, preferred_element_type=jnp.float32)  9.91 us
    dot_general x1, matrix products, local(): jnp.dot(hidden_other, sibling, preferred_element_type=jnp.float32)  7.95 us
    dot_general x1, matrix products, local(): jnp.dot(hidden_mine, gathered, preferred_element_type=jnp.float32)  7.64 us
    dot_general x1, matrix products, local(): jnp.dot(normed_mine, gathered, preferred_element_type=jnp.float32)  7.53 us
  transfers between devices with their start and end apart: 5, of which 2 were waited for; matrix products, arithmetic and copies ran while one was open for 14% of the time, Pallas kernels for 0%

profile of v13, /device:TPU:0, one launch (start us, length us, event | category | flops | bytes accessed | tf_op | source)
XLA Modules:
  0.0 299.7 jit_solution(7394766711604683833)
XLA Ops:
  6.6 1.0 copy-done
  7.5 0.1 constant_dynamic-slice_fusion
  7.6 0.9 constant_dynamic-slice_fusion.1
  8.5 0.8 fusion.29
  9.3 0.0 all-gather.2.cloned.1.call-update
  9.4 184.2 %all-gather.2.cloned.1.call-done = bf16[2560,2816]{1,0:T(8,128)(2,1)} async-done(((bf16[80,2816]{1,0:T(8,128)(2,1)}), bf16[2560,2816]{1,0:T(8,128)(2,1)}) %all-gather.2.cloned.1.call-update) | async-done | bytes 14417936 | tf_op jit(solution)/shard_map/all_gather | solution.py:162
  193.6 0.5 collective-permute-start
  194.1 3.4 %collective-permute-start.1 = (bf16[2048,192]{0,1:T(8,128)(2,1)}, bf16[2048,192]{0,1:T(8,128)(2,1)}, u32[]{:S(2)}, u32[]{:S(2)}) collective-permute-start(bf16[2048,192]{0,1:T(8,128)(2,1)} %param.12), channel_id=1, source_target_pairs={{0,2},{1,3},{2,0},{3,1},{4,6},{5,7},{6,4},{7,5},{8,10},{9,11},{10,... | collective-permute-start | bytes 2359304 | tf_op jit(solution)/shard_map/ppermute | solution.py:165
  197.5 1.5 fusion.16
  199.0 0.3 fusion.18
  199.3 0.5 copy.29
  199.9 0.1 dynamic-slice_bitcast_fusion.2
  200.0 0.0 copy-start.7
  200.0 0.0 copy-start.5
  200.0 0.1 pad.18
  200.1 0.1 pad.20
  200.2 0.1 fusion.46
  200.3 0.1 fusion.50
  200.4 0.1 copy.37
  200.5 0.1 copy.38
  200.6 0.3 fusion.39
  200.8 0.3 fusion.37
  201.1 0.1 maximum_maximum_fusion
  201.3 0.1 pad.26.clone
  201.4 0.7 pad_maximum_fusion.t1_ref
  202.1 0.5 broadcast_multiply_fusion.w_ref
  202.6 0.6 clamp_bitcast_fusion
  203.2 0.7 maximum_maximum_fusion.1.t2_ref
  203.9 7.5 %fusion.52 = f32[256,2816]{1,0:T(8,128)S(1)} fusion(bf16[256,2560]{0,1:T(8,128)(2,1)S(1)} %bitcast.56, bf16[2560,2816]{1,0:T(8,128)(2,1)} %all-gather.2.cloned.1.call-done), kind=kOutput, calls=%fused_computation.84 | convolution fusion | flops 3690987520 | bytes 18612224 | tf_op jit(solution)/shard_map/dot_general | solution.py:180
  211.4 4.3 %collective-permute-done.3 = bf16[2560,2816]{1,0:T(8,128)(2,1)} collective-permute-done((bf16[2560,2816]{1,0:T(8,128)(2,1)}, bf16[2560,2816]{1,0:T(8,128)(2,1)}, u32[]{:S(2)}, u32[]{:S(2)}) %collective-permute-start.3) | collective-permute-done | bytes 14417952 | tf_op jit(solution)/shard_map/ppermute | solution.py:163
  215.7 9.9 %fusion.15 = bf16[256,2816]{1,0:T(8,128)(2,1)S(1)} fusion(f32[256,2816]{1,0:T(8,128)S(1)} %fusion.52, bf16[256,2560]{0,1:T(8,128)(2,1)S(1)} %bitcast.60, bf16[2560,2816]{1,0:T(8,128)(2,1)} %collective-permute-done.3), kind=kOutput, calls=%fused_computation.22 | convolution fusion | flops 3698196480 | bytes 20054016 | tf_op jit(solution)/shard_map/dot_general | solution.py:180
  225.6 0.7 copy.30
  226.3 0.3 reshape.67
  226.7 0.1 dynamic-slice_bitcast_fusion.1
  226.8 0.1 pad.21.clone
  226.9 0.1 pad.22.clone
  227.0 7.6 %fusion.53 = f32[256,2816]{1,0:T(8,128)S(1)} fusion(bf16[256,2560]{0,1:T(8,128)(2,1)S(1)} %bitcast.57, bf16[2560,2816]{1,0:T(8,128)(2,1)} %all-gather.2.cloned.1.call-done), kind=kOutput, calls=%fused_computation.85 | convolution fusion | flops 3690987520 | bytes 18612224 | tf_op jit(solution)/shard_map/dot_general | solution.py:185
  234.6 0.0 copy-start.3
  234.6 0.0 copy-start.6
  234.6 8.0 %fusion.54 = f32[256,2816]{1,0:T(8,128)S(1)} fusion(bf16[256,2560]{0,1:T(8,128)(2,1)S(1)} %bitcast.58, bf16[2560,2816]{1,0:T(8,128)(2,1)} %collective-permute-done.3), kind=kOutput, calls=%fused_computation.86 | convolution fusion | flops 3690987520 | bytes 18612224 | tf_op jit(solution)/shard_map/dot_general | solution.py:185
  242.7 2.7 fusion.23
  245.3 0.6 gather_fusion
  245.9 0.1 convert_bitcast_fusion
  246.0 4.0 %reshape.73 = f32[1,16,16,6,2,8,8]{2,1,6,5,4,3,0:T(8,128)} reshape(f32[256,4,192]{0,2,1:T(8,128)S(1)} %convert_bitcast_fusion) | data formatting | bytes 1572864 | tf_op jit(solution)/shard_map/convert_element_type | solution.py:126
  250.0 7.5 %copy.45 = f32[1,16,16,6,2,8,8]{2,6,4,3,5,1,0:T(8,128)} copy(f32[1,16,16,6,2,8,8]{2,1,6,5,4,3,0:T(8,128)} %reshape.73) | data formatting | bytes 1572864 | tf_op jit(solution)/shard_map/convert_element_type | solution.py:126
  257.5 6.9 %reshape.72.spec_ref = f32[128,1536]{1,0:T(8,128)} reshape(f32[1,16,8,6,2,8,16]{6,5,4,3,2,1,0:T(8,128)} %bitcast.55) | data formatting | bytes 1572864 | tf_op jit(solution)/shard_map/convert_element_type | solution.py:126
  264.4 27.0 %shard_map.82 = f32[64,64]{1,0:T(8,128)} custom-call(f32[128]{0:T(128)} %broadcast_multiply_fusion.w_ref, s32[128]{0:T(128)} %get-tuple-element.16.x0_ref, s32[128]{0:T(128)} %get-tuple-element.15.y0_ref, s32[128]{0:T(128)} %r_ref.1, f32[128,1536]{1,0:T(8,128)} %reshape.72.spec_ref, bf16[256,256]{1,0:T(8,128)(2,1)} %pad_maximum_fusion.t1_ref, ...), custom_call_target="tpu_custom_call" | custom-call | tf_op jit(solution)/shard_map/pallas_call | solution.py:125
  291.4 1.4 reshape_stack.3
  (25 shorter events, 0.1 us)
Async XLA Ops:
  6.5 1.0 copy-start
  6.5 192.5 %copy-start.2 = (bf16[256,2048]{1,0:T(8,128)(2,1)S(1)}, bf16[256,2048]{1,0:T(8,128)(2,1)}, u32[]{:S(2)}) copy-start(bf16[256,2048]{1,0:T(8,128)(2,1)} %param.8) | copy-start | bytes 3145732
  6.5 192.5 %copy-start.4 = (f32[2048]{0:T(1024)S(1)}, f32[2048]{0:T(1024)}, u32[]{:S(2)}) copy-start(f32[2048]{0:T(1024)} %param.9) | copy-start | bytes 24580
  6.5 187.1 %all-gather.2.cloned.1.call-start = ((), (), s32[]{:S(2)}) async-start(), calls=%async_computation | async-start | bytes 14868480 | tf_op jit(solution)/shard_map/all_gather | solution.py:162
  193.6 22.1 %collective-permute-start.3 = (bf16[2560,2816]{1,0:T(8,128)(2,1)}, bf16[2560,2816]{1,0:T(8,128)(2,1)}, u32[]{:S(2)}, u32[]{:S(2)}) collective-permute-start(bf16[2560,2816]{1,0:T(8,128)(2,1)} %all-gather.2.cloned.1.call-done), channel_id=1, source_target_pairs={{0,1},{1,0},{2,3},{3,2},{4,5},{5,4},{6,7},{7,6},{8,9},{9,8},{10,11... | collective-permute-start | bytes 43253768 | tf_op jit(solution)/shard_map/ppermute | solution.py:163
  193.6 49.0 %collective-permute-start = (bf16[2048,192]{0,1:T(8,128)(2,1)}, bf16[2048,192]{0,1:T(8,128)(2,1)}, u32[]{:S(2)}, u32[]{:S(2)}) collective-permute-start(bf16[2048,192]{0,1:T(8,128)(2,1)} %param.12), channel_id=1, source_target_pairs={{0,1},{1,0},{2,3},{3,2},{4,5},{5,4},{6,7},{7,6},{8,9},{9,8},{10,11... | collective-permute-start | bytes 2359304 | tf_op jit(solution)/shard_map/ppermute | solution.py:165
  194.1 48.5 %collective-permute-start.1 = (bf16[2048,192]{0,1:T(8,128)(2,1)}, bf16[2048,192]{0,1:T(8,128)(2,1)}, u32[]{:S(2)}, u32[]{:S(2)}) collective-permute-start(bf16[2048,192]{0,1:T(8,128)(2,1)} %param.12), channel_id=1, source_target_pairs={{0,2},{1,3},{2,0},{3,1},{4,6},{5,7},{6,4},{7,5},{8,10},{9,11},{10,... | collective-permute-start | bytes 2359304 | tf_op jit(solution)/shard_map/ppermute | solution.py:165
  197.5 45.1 %collective-permute-start.2 = (bf16[2048,192]{0,1:T(8,128)(2,1)}, bf16[2048,192]{0,1:T(8,128)(2,1)}, u32[]{:S(2)}, u32[]{:S(2)}) collective-permute-start(bf16[2048,192]{0,1:T(8,128)(2,1)} %param.12), channel_id=1, source_target_pairs={{0,3},{1,2},{2,1},{3,0},{4,7},{5,6},{6,5},{7,4},{8,11},{9,10},{10,... | collective-permute-start | bytes 2359304 | tf_op jit(solution)/shard_map/ppermute | solution.py:165
  200.0 2.1 copy-start.7
  200.0 2.6 copy-start.5
  234.6 8.0 %copy-start.3 = (bf16[256,2048]{1,0:T(8,128)(2,1)S(1)}, bf16[256,2048]{1,0:T(8,128)(2,1)}, u32[]{:S(2)}) copy-start(bf16[256,2048]{1,0:T(8,128)(2,1)} %param.8) | copy-start | bytes 3145732
  234.6 8.0 %copy-start.6 = (bf16[2048,192]{0,1:T(8,128)(2,1)S(1)}, bf16[2048,192]{0,1:T(8,128)(2,1)}, u32[]{:S(2)}) copy-start(bf16[2048,192]{0,1:T(8,128)(2,1)} %param.12) | copy-start | bytes 2359300
  257.5 35.4 %copy-start.1 = (bf16[88,2048]{1,0:T(8,128)(2,1)S(1)}, bf16[88,2048]{1,0:T(8,128)(2,1)}, u32[]{:S(2)}) copy-start(bf16[88,2048]{1,0:T(8,128)(2,1)} %param.11) | copy-start | bytes 1081348
Sparse Core Ops, SparseCore 0:
  9.5 184.0 all-gather.1

commit v14 on v11

--- a/solution.py
+++ b/solution.py
@@ -92,7 +92,7 @@
     out_ref[...] += acc[:, :PIX]
 
 
-def imaging(spec_rows, source_index, source_cutoff, source_weight, sb=32):
+def imaging(spec_rows, source_index, source_cutoff, source_weight, sb=64):
     T = spec_rows.shape[0]
     S = source_index.shape[0]
     x0 = jnp.clip(source_index[:, 0], 0, ORD - W)

time: 296 us -> 296 us (level)
  no operation moved by 1% of the time
where the time goes in v14:
time: 296 us; the launch traced here: 295 us
  waiting for transfers between devices  189 us (64%)
  matrix products  35.7 us (12%)
  Pallas kernels  26.3 us (9%)
  local copies, waits for them, and re-layouts  18.5 us (6%)
  between operations  13.7 us (5%)
  other arithmetic  7.82 us (3%)
  starting transfers between devices  3.89 us (1%)
    all_gather x1, waiting for transfers between devices, local(): gathered = lax.all_gather(packed, 'tile', axis=0, tiled=True)  184 us
    pallas_call x1, Pallas kernels, imaging(): call(scaled, x0, y0, source_cutoff, jnp.pad(spec_rows[t].astype(f32), ((0...  26.3 us
    convert_element_type x3, local copies, waits for them, and re-layouts, imaging(): spec_rows[t].astype(f32)  12.2 us
    dot_general x1, matrix products, local(): jnp.dot(normed_other, sibling, preferred_element_type=jnp.float32)  9.91 us
    dot_general x1, matrix products, local(): jnp.dot(hidden_other, sibling, preferred_element_type=jnp.float32)  7.95 us
    dot_general x1, matrix products, local(): jnp.dot(hidden_mine, gathered, preferred_element_type=jnp.float32)  7.64 us
    dot_general x1, matrix products, local(): jnp.dot(normed_mine, gathered, preferred_element_type=jnp.float32)  7.53 us
  transfers between devices with their start and end apart: 5, of which 2 were waited for; matrix products, arithmetic and copies ran while one was open for 14% of the time, Pallas kernels for 0%

profile of v14, /device:TPU:0, one launch (start us, length us, event | category | flops | bytes accessed | tf_op | source)
XLA Modules:
  0.0 294.5 jit_solution(12964266433777919212)
XLA Ops:
  6.6 1.0 copy-done
  7.5 0.1 constant_dynamic-slice_fusion
  7.6 0.9 constant_dynamic-slice_fusion.1
  8.5 0.8 fusion.29
  9.3 0.0 all-gather.2.cloned.1.call-update
  9.4 184.2 %all-gather.2.cloned.1.call-done = bf16[2560,2816]{1,0:T(8,128)(2,1)} async-done(((bf16[80,2816]{1,0:T(8,128)(2,1)}), bf16[2560,2816]{1,0:T(8,128)(2,1)}) %all-gather.2.cloned.1.call-update) | async-done | bytes 14417936 | tf_op jit(solution)/shard_map/all_gather | solution.py:162
  193.6 0.5 collective-permute-start
  194.1 3.4 %collective-permute-start.1 = (bf16[2048,192]{0,1:T(8,128)(2,1)}, bf16[2048,192]{0,1:T(8,128)(2,1)}, u32[]{:S(2)}, u32[]{:S(2)}) collective-permute-start(bf16[2048,192]{0,1:T(8,128)(2,1)} %param.12), channel_id=1, source_target_pairs={{0,2},{1,3},{2,0},{3,1},{4,6},{5,7},{6,4},{7,5},{8,10},{9,11},{10,... | collective-permute-start | bytes 2359304 | tf_op jit(solution)/shard_map/ppermute | solution.py:165
  197.5 1.5 fusion.16
  199.0 0.3 fusion.18
  199.3 0.5 copy.29
  199.9 0.1 dynamic-slice_bitcast_fusion.2
  200.0 0.0 copy-start.7
  200.0 0.0 copy-start.5
  200.0 0.1 pad.24
  200.1 0.1 pad.26
  200.2 0.1 fusion.46
  200.3 0.1 fusion.50
  200.4 0.1 copy.37
  200.5 0.1 copy.38
  200.6 0.3 fusion.39
  200.8 0.3 fusion.37
  201.1 0.1 maximum_maximum_fusion
  201.3 0.1 pad.34.clone
  201.4 0.7 pad_maximum_fusion.t1_ref
  202.1 0.5 broadcast_multiply_fusion.w_ref
  202.6 0.6 clamp_bitcast_fusion
  203.2 0.7 maximum_maximum_fusion.1.t2_ref
  203.9 7.5 %fusion.52 = f32[256,2816]{1,0:T(8,128)S(1)} fusion(bf16[256,2560]{0,1:T(8,128)(2,1)S(1)} %bitcast.56, bf16[2560,2816]{1,0:T(8,128)(2,1)} %all-gather.2.cloned.1.call-done), kind=kOutput, calls=%fused_computation.85 | convolution fusion | flops 3690987520 | bytes 18612224 | tf_op jit(solution)/shard_map/dot_general | solution.py:180
  211.4 4.3 %collective-permute-done.3 = bf16[2560,2816]{1,0:T(8,128)(2,1)} collective-permute-done((bf16[2560,2816]{1,0:T(8,128)(2,1)}, bf16[2560,2816]{1,0:T(8,128)(2,1)}, u32[]{:S(2)}, u32[]{:S(2)}) %collective-permute-start.3) | collective-permute-done | bytes 14417952 | tf_op jit(solution)/shard_map/ppermute | solution.py:163
  215.7 9.9 %fusion.15 = bf16[256,2816]{1,0:T(8,128)(2,1)S(1)} fusion(f32[256,2816]{1,0:T(8,128)S(1)} %fusion.52, bf16[256,2560]{0,1:T(8,128)(2,1)S(1)} %bitcast.60, bf16[2560,2816]{1,0:T(8,128)(2,1)} %collective-permute-done.3), kind=kOutput, calls=%fused_computation.22 | convolution fusion | flops 3698196480 | bytes 20054016 | tf_op jit(solution)/shard_map/dot_general | solution.py:180
  225.6 0.7 copy.30
  226.3 0.3 reshape.67
  226.7 0.1 dynamic-slice_bitcast_fusion.1
  226.8 0.1 pad.27.clone
  226.9 0.1 pad.28.clone
  227.0 7.6 %fusion.53 = f32[256,2816]{1,0:T(8,128)S(1)} fusion(bf16[256,2560]{0,1:T(8,128)(2,1)S(1)} %bitcast.57, bf16[2560,2816]{1,0:T(8,128)(2,1)} %all-gather.2.cloned.1.call-done), kind=kOutput, calls=%fused_computation.86 | convolution fusion | flops 3690987520 | bytes 18612224 | tf_op jit(solution)/shard_map/dot_general | solution.py:185
  234.6 0.0 copy-start.3
  234.6 8.0 %fusion.54 = f32[256,2816]{1,0:T(8,128)S(1)} fusion(bf16[256,2560]{0,1:T(8,128)(2,1)S(1)} %bitcast.58, bf16[2560,2816]{1,0:T(8,128)(2,1)} %collective-permute-done.3), kind=kOutput, calls=%fused_computation.87 | convolution fusion | flops 3690987520 | bytes 18612224 | tf_op jit(solution)/shard_map/dot_general | solution.py:185
  242.7 2.7 fusion.23
  245.3 0.6 gather_fusion
  245.9 0.9 select_bitcast_fusion
  246.8 3.5 %convert_element_type.74 = bf16[1,16,16,6,2,8,8]{2,1,6,5,4,3,0:T(8,128)(2,1)S(1)} reshape(bf16[256,4,192]{0,2,1:T(8,128)(2,1)} %select_bitcast_fusion) | data formatting | bytes 786432 | tf_op jit(solution)/shard_map/convert_element_type | solution.py:126
  250.3 2.5 copy.45
  252.7 6.2 %convert_element_type.76 = bf16[128,1536]{1,0:T(8,128)(2,1)S(1)} reshape(bf16[1,16,8,6,2,8,16]{6,5,4,3,2,1,0:T(8,128)(2,1)} %bitcast.55) | data formatting | bytes 786432 | tf_op jit(solution)/shard_map/convert_element_type | solution.py:126
  258.9 1.0 pad_convert_fusion.spec_ref
  259.9 26.3 %shard_map.82 = f32[64,64]{1,0:T(8,128)} custom-call(f32[128]{0:T(128)} %broadcast_multiply_fusion.w_ref, s32[128]{0:T(128)} %get-tuple-element.16.x0_ref, s32[128]{0:T(128)} %get-tuple-element.15.y0_ref, s32[128]{0:T(128)} %r_ref.1, f32[136,1536]{1,0:T(8,128)} %pad_convert_fusion.spec_ref, bf16[256,256]{1,0:T(8,128)(2,1)} %pad_maximum_fusion.t1_ref, ...), custom_call_target="tpu_custom_call" | custom-call | tf_op jit(solution)/shard_map/pallas_call | solution.py:125
  286.2 1.4 reshape_stack.3
  (26 shorter events, 0.1 us)
Async XLA Ops:
  6.5 1.0 copy-start
  6.5 192.5 %copy-start.2 = (bf16[256,2048]{1,0:T(8,128)(2,1)S(1)}, bf16[256,2048]{1,0:T(8,128)(2,1)}, u32[]{:S(2)}) copy-start(bf16[256,2048]{1,0:T(8,128)(2,1)} %param.8) | copy-start | bytes 3145732
  6.5 192.5 %copy-start.4 = (f32[2048]{0:T(1024)S(1)}, f32[2048]{0:T(1024)}, u32[]{:S(2)}) copy-start(f32[2048]{0:T(1024)} %param.9) | copy-start | bytes 24580
  6.5 187.1 %all-gather.2.cloned.1.call-start = ((), (), s32[]{:S(2)}) async-start(), calls=%async_computation | async-start | bytes 14868480 | tf_op jit(solution)/shard_map/all_gather | solution.py:162
  193.6 22.1 %collective-permute-start.3 = (bf16[2560,2816]{1,0:T(8,128)(2,1)}, bf16[2560,2816]{1,0:T(8,128)(2,1)}, u32[]{:S(2)}, u32[]{:S(2)}) collective-permute-start(bf16[2560,2816]{1,0:T(8,128)(2,1)} %all-gather.2.cloned.1.call-done), channel_id=1, source_target_pairs={{0,1},{1,0},{2,3},{3,2},{4,5},{5,4},{6,7},{7,6},{8,9},{9,8},{10,11... | collective-permute-start | bytes 43253768 | tf_op jit(solution)/shard_map/ppermute | solution.py:163
  193.6 49.0 %collective-permute-start = (bf16[2048,192]{0,1:T(8,128)(2,1)}, bf16[2048,192]{0,1:T(8,128)(2,1)}, u32[]{:S(2)}, u32[]{:S(2)}) collective-permute-start(bf16[2048,192]{0,1:T(8,128)(2,1)} %param.12), channel_id=1, source_target_pairs={{0,1},{1,0},{2,3},{3,2},{4,5},{5,4},{6,7},{7,6},{8,9},{9,8},{10,11... | collective-permute-start | bytes 2359304 | tf_op jit(solution)/shard_map/ppermute | solution.py:165
  194.1 48.5 %collective-permute-start.1 = (bf16[2048,192]{0,1:T(8,128)(2,1)}, bf16[2048,192]{0,1:T(8,128)(2,1)}, u32[]{:S(2)}, u32[]{:S(2)}) collective-permute-start(bf16[2048,192]{0,1:T(8,128)(2,1)} %param.12), channel_id=1, source_target_pairs={{0,2},{1,3},{2,0},{3,1},{4,6},{5,7},{6,4},{7,5},{8,10},{9,11},{10,... | collective-permute-start | bytes 2359304 | tf_op jit(solution)/shard_map/ppermute | solution.py:165
  197.5 45.1 %collective-permute-start.2 = (bf16[2048,192]{0,1:T(8,128)(2,1)}, bf16[2048,192]{0,1:T(8,128)(2,1)}, u32[]{:S(2)}, u32[]{:S(2)}) collective-permute-start(bf16[2048,192]{0,1:T(8,128)(2,1)} %param.12), channel_id=1, source_target_pairs={{0,3},{1,2},{2,1},{3,0},{4,7},{5,6},{6,5},{7,4},{8,11},{9,10},{10,... | collective-permute-start | bytes 2359304 | tf_op jit(solution)/shard_map/ppermute | solution.py:165
  200.0 2.1 copy-start.7
  200.0 2.6 copy-start.5
  234.6 8.0 %copy-start.3 = (bf16[256,2048]{1,0:T(8,128)(2,1)S(1)}, bf16[256,2048]{1,0:T(8,128)(2,1)}, u32[]{:S(2)}) copy-start(bf16[256,2048]{1,0:T(8,128)(2,1)} %param.8) | copy-start | bytes 3145732
  234.6 8.0 %copy-start.6 = (bf16[2048,192]{0,1:T(8,128)(2,1)S(1)}, bf16[2048,192]{0,1:T(8,128)(2,1)}, u32[]{:S(2)}) copy-start(bf16[2048,192]{0,1:T(8,128)(2,1)} %param.12) | copy-start | bytes 2359300
  252.7 34.9 %copy-start.1 = (bf16[88,2048]{1,0:T(8,128)(2,1)S(1)}, bf16[88,2048]{1,0:T(8,128)(2,1)}, u32[]{:S(2)}) copy-start(bf16[88,2048]{1,0:T(8,128)(2,1)} %param.11) | copy-start | bytes 1081348
Sparse Core Ops, SparseCore 0:
  9.5 184.0 all-gather.1
